TPU v7x, 128 devices: a whole 4x4x4 slice. The times are simulated.
128 devices in a mesh: section: 2 (over x_lo), owner: 8 (over x_hi, z), pos: 8 (over y, core).
Axes of the slice: x: 4 (x_hi: 2, x_lo: 2; x = x_hi * 2 + x_lo), y: 4, z: 4, core: 2. Of those that a mesh axis runs over, the one named last changes fastest.
Arguments:
- hidden_rows: bfloat16 [2, 131072, 1024], P(None, ('owner', 'pos'), 'section'), may hold values from -144 to 144
- w_proj: bfloat16 [1024, 256], P('section'), may hold values from -0.1875 to 0.1875
- panels: bfloat16 [8192, 256], P(('section', 'owner')), may hold values from -1.5 to 1.5
- cand_ids: int32 [8192], P(('section', 'owner')), may hold values from 0 to 65535
- counts: int32 [65536], replicated, may hold values from 1 to 65535
- target_slot: int32 [262144], P(('section', 'owner', 'pos')), may hold values from 0 to 8191
- block_lists: int32 [1024, 12], P(('section', 'owner', 'pos')), may hold values from 0 to 31, all different within a row
- list_lens: int32 [1024], P(('section', 'owner', 'pos')), may hold values from 1 to 12, 7680 in all
Outputs:
- query_grad: bfloat16 [262144, 256], P(('section', 'owner', 'pos'))
- position_loss: float32 [262144], P(('section', 'owner', 'pos'))
- trunk_grad: bfloat16 [2, 131072, 1024], P(None, ('owner', 'pos'), 'section')
Inputs may be any that keep to these rules, and one draw needn't show every extreme that they name: `block_lists`: each row names 12 different candidate blocks. `list_lens`: entries of a row of block_lists past its length are padding and not scored.
All inputs are finite; a program needn't handle non-finite values. No bound on the sum of `list_lens` on one device may be relied on, other than what follows from the above.
Results may differ from a plain program's by a relative error of at most 0.012.
The roundings to bfloat16 on the way count: a program that leaves them out, or rounds other values in their place, can miss the bound.
Values may be sent and summed in bfloat16 or wider, within the bound.
No kernel may reach another device: no remote copies, remote signals or barrier semaphores. Data moves between devices by JAX's collectives and lax.ppermute only.
A program may use at most 64 MiB of HBM per device.

v0:
```python
import jax
import jax.numpy as jnp
from jax import lax
from jax.sharding import PartitionSpec as P

BLOCK = 256


NEG_FILL = -1e30


def shards(hidden_rows, w_proj, panels, cand_ids, counts, target_slot, block_lists, list_lens):
    halves, rows_dev, width_half = hidden_rows.shape
    embed_width = w_proj.shape[1]
    block_size = BLOCK
    list_width = block_lists.shape[1]
    flat_rows = hidden_rows.reshape(halves * rows_dev, width_half)
    queries = lax.psum_scatter(
        jnp.dot(flat_rows, w_proj, preferred_element_type=jnp.float32),
        "section",
        scatter_dimension=0,
        tiled=True,
    ).astype(jnp.bfloat16)
    own_bias = jnp.log(counts[cand_ids].astype(jnp.float32)).astype(jnp.bfloat16)
    cand_table, bias_table = (
        lax.all_gather(panels, ("section", "owner"), axis=0, tiled=True),
        lax.all_gather(own_bias, ("section", "owner"), axis=0, tiled=True),
    )
    pos_blocks = rows_dev // block_size
    block_count = cand_table.shape[0] // block_size
    table_blocks = cand_table.reshape(block_count, block_size, embed_width)
    bias_blocks = bias_table.reshape(block_count, block_size)
    offsets = lax.broadcasted_iota(jnp.int32, (1, block_size), 1)
    entries = lax.broadcasted_iota(jnp.int32, (list_width, 1), 0)

    def score_block(inputs):
        query_rows, targets, listed, length = inputs
        positive = cand_table[targets]
        pos_logit = jnp.sum(
            query_rows.astype(jnp.float32) * positive.astype(jnp.float32), axis=1
        ) - bias_table[targets].astype(jnp.float32)
        cand_flat = table_blocks[listed].reshape(list_width * block_size, embed_width)
        bias_flat = bias_blocks[listed].reshape(list_width * block_size).astype(jnp.float32)
        slot_ids = (listed[:, None] * block_size + offsets).reshape(list_width * block_size)
        entry_ok = jnp.broadcast_to(entries < length, (list_width, block_size)).reshape(
            list_width * block_size
        )
        products = lax.dot_general(
            query_rows, cand_flat, (((1,), (1,)), ((), ())), preferred_element_type=jnp.float32
        )
        logits = products - bias_flat[None, :]
        usable = (slot_ids[None, :] != targets[:, None]) & entry_ok[None, :]
        masked = jnp.where(usable, logits, NEG_FILL)
        row_max = jnp.maximum(pos_logit, jnp.max(masked, axis=1))
        row_sum = jnp.exp(pos_logit - row_max) + jnp.sum(
            jnp.where(usable, jnp.exp(masked - row_max[:, None]), 0.0), axis=1
        )
        log_total = row_max + jnp.log(row_sum)
        weights = jnp.where(usable, jnp.exp(masked - log_total[:, None]), 0.0).astype(jnp.bfloat16)
        weighted = jnp.dot(weights, cand_flat, preferred_element_type=jnp.float32)
        grad_rows = weighted + (jnp.exp(pos_logit - log_total) - 1.0)[:, None] * positive.astype(
            jnp.float32
        )
        return (grad_rows.astype(jnp.bfloat16), log_total - pos_logit)

    query_grad, position_loss = lax.map(
        score_block,
        (
            queries.reshape(pos_blocks, block_size, embed_width),
            target_slot.reshape(pos_blocks, block_size),
            block_lists,
            list_lens,
        ),
    )
    query_grad = query_grad.reshape(rows_dev, embed_width)
    position_loss = position_loss.reshape(rows_dev)
    trunk_grad = lax.dot_general(
        lax.all_gather(query_grad, "section", axis=0, tiled=True),
        w_proj,
        (((1,), (1,)), ((), ())),
        preferred_element_type=jnp.float32,
    ).astype(jnp.bfloat16)
    return (query_grad, position_loss, trunk_grad.reshape(halves, rows_dev, width_half))


def solution(mesh):
    return jax.shard_map(
        shards,
        mesh=mesh,
        in_specs=(
            P(None, ("owner", "pos"), "section"),
            P("section", None),
            P(("section", "owner"), None),
            P(("section", "owner")),
            P(),
            P(("section", "owner", "pos")),
            P(("section", "owner", "pos"), None),
            P(("section", "owner", "pos")),
        ),
        out_specs=(
            P(("section", "owner", "pos"), None),
            P(("section", "owner", "pos")),
            P(None, ("owner", "pos"), "section"),
        ),
        check_vma=False,
    )
```

profile of v0, /device:TPU:1, one launch (start us, length us, event | category | flops | bytes accessed | tf_op | source)
XLA Modules:
  0.0 435.8 jit_solution(3094247205970796049)
XLA Ops:
  9.0 5.5 %fusion.18 = f32[4096,256]{1,0:T(8,128)} fusion(bf16[4096,512]{1,0:T(8,128)(2,1)} %bitcast.83, bf16[512,256]{1,0:T(8,128)(2,1)S(1)} %copy-done), kind=kOutput, calls=%fused_computation.44 | convolution fusion | flops 1073741824 | bytes 8650752 | tf_op jit(solution)/shard_map/dot_general | solution.py:19
  15.4 3.1 gather_fusion.4
  18.5 35.9 %all-gather = bf16[16,1,512]{2,1,0:T(2,128)(2,1)S(1)} all-gather(bf16[1,1,512]{2,1,0:T(2,128)(2,1)S(1)} %reshape.315), channel_id=1, replica_groups=mesh['section'=2,'owner'=8,'pos'=8] {'section','owner'}, dimensions={0}, use_global_device_ids=true | all-gather | bytes 17408 | tf_op jit(solution)/shard_map/all_gather | solution.py:27
  55.8 18.7 %reduce-scatter.2.cloned.1.call-done = f32[2048,256]{1,0:T(8,128)} async-done(((f32[4096,256]{1,0:T(8,128)}), f32[2048,256]{1,0:T(8,128)}) %reduce-scatter.2.cloned.1.call-update) | async-done | bytes 2097168 | tf_op jit(solution)/shard_map/reduce_scatter | solution.py:18
  77.2 54.1 %all-gather.4.cloned.1.call-done = bf16[8192,256]{1,0:T(8,128)(2,1)} async-done(((bf16[512,256]{1,0:T(8,128)(2,1)}), bf16[8192,256]{1,0:T(8,128)(2,1)}) %all-gather.4.cloned.1.call-update) | async-done | bytes 4194320 | tf_op jit(solution)/shard_map/all_gather | solution.py:26
  131.3 245.1 %while.15 = (s32[]{:T(128)}, bf16[8,256,256]{2,1,0:T(8,128)(2,1)}, f32[8,256]{1,0:T(8,128)}, s32[8,12]{1,0:T(8,128)}, s32[8,256]{1,0:T(8,128)}, /*index=5*/s32[8...) while((s32[]{:T(128)}, bf16[8,256,256]{2,1,0:T(8,128)(2,1)}, ...), condition=%wide.region_5.6_spmd.clone, body=%wide.region_1.5_spmd.clone.sunk | while | flops 817635648 | bytes 16905468 | solution.py:66
  132.0 4.0 gather_fusion
  140.7 3.1 fusion.35
  144.4 3.8 gather_fusion.2
  162.6 4.0 gather_fusion
  171.4 3.1 fusion.35
  175.1 3.8 gather_fusion.2
  193.3 4.0 gather_fusion
  202.0 3.1 fusion.35
  205.7 3.8 gather_fusion.2
  223.9 4.0 gather_fusion
  232.7 3.1 fusion.35
  236.4 3.8 gather_fusion.2
  254.5 4.0 gather_fusion
  263.3 3.1 fusion.35
  267.0 3.8 gather_fusion.2
  285.2 4.0 gather_fusion
  294.0 3.1 fusion.35
  297.6 3.8 gather_fusion.2
  315.8 4.0 gather_fusion
  324.6 3.1 fusion.35
  328.3 3.8 gather_fusion.2
  346.5 4.0 gather_fusion
  355.2 3.1 fusion.35
  358.9 3.8 gather_fusion.2
  377.7 45.7 %all-gather.6.cloned.1.call-done = bf16[4096,256]{1,0:T(8,128)(2,1)} async-done(((bf16[2048,256]{1,0:T(8,128)(2,1)}), bf16[4096,256]{1,0:T(8,128)(2,1)}) %all-gather.6.cloned.1.call-update) | async-done | bytes 2097168 | tf_op jit(solution)/shard_map/all_gather | solution.py:78
  423.4 4.9 %convolution_convert_fusion = bf16[4096,512]{1,0:T(8,128)(2,1)} fusion(bf16[4096,256]{1,0:T(8,128)(2,1)} %all-gather.6.cloned.1.call-done, bf16[512,256]{1,0:T(8,128)(2,1)S(1)} %copy-done), kind=kOutput, calls=%fused_computation.38 | convolution fusion | flops 1075838976 | bytes 6553600 | tf_op jit(solution)/shard_map/dot_general | solution.py:77
  (306 shorter events, 164.3 us)
Async XLA Ops:
  8.0 66.5 %reduce-scatter.2.cloned.1.call-start = ((), (), s32[]{:S(2)}) async-start(), calls=%async_computation.1 | async-start | bytes 6291456 | tf_op jit(solution)/shard_map/reduce_scatter | solution.py:18
  14.4 40.8 %copy-start.9 = (s32[2048]{0:T(1024)S(1)}, s32[2048]{0:T(1024)}, u32[]{:S(2)}) copy-start(s32[2048]{0:T(1024)} %param.15) | copy-start | bytes 24580
  14.4 116.8 %all-gather.4.cloned.1.call-start = ((), (), s32[]{:S(2)}) async-start(), calls=%async_computation.2 | async-start | bytes 4456448 | tf_op jit(solution)/shard_map/all_gather | solution.py:26
  15.0 408.4 %all-gather.6.cloned.1.call-start = ((), (), s32[]{:S(2)}) async-start(), calls=%async_computation.3 | async-start | bytes 3145728 | tf_op jit(solution)/shard_map/all_gather | solution.py:78
  136.8 7.6 %copy-start.2 = (s32[3072]{0:T(1024)}, s32[3072]{0:T(1024)S(1)}, u32[]{:S(2)}) copy-start(s32[3072]{0:T(1024)S(1)} %add.196) | copy-start | bytes 36868 | tf_op jit(solution)/shard_map/while
  138.8 5.6 %copy-start.7 = (s32[1,256]{1,0:T(1,128)}, s32[1,256]{1,0:T(1,128)S(1)}, u32[]{:S(2)}) copy-start(s32[1,256]{1,0:T(1,128)S(1)} %get-tuple-element.297) | copy-start | bytes 3076 | tf_op jit(solution)/shard_map/while
  140.7 3.7 copy-start.3
  152.6 3.7 copy-start.8
  167.4 7.6 %copy-start.2 = (s32[3072]{0:T(1024)}, s32[3072]{0:T(1024)S(1)}, u32[]{:S(2)}) copy-start(s32[3072]{0:T(1024)S(1)} %add.196) | copy-start | bytes 36868 | tf_op jit(solution)/shard_map/while
  169.5 5.6 %copy-start.7 = (s32[1,256]{1,0:T(1,128)}, s32[1,256]{1,0:T(1,128)S(1)}, u32[]{:S(2)}) copy-start(s32[1,256]{1,0:T(1,128)S(1)} %get-tuple-element.297) | copy-start | bytes 3076 | tf_op jit(solution)/shard_map/while
  171.4 3.7 copy-start.3
  183.2 3.7 copy-start.8
  198.1 7.6 %copy-start.2 = (s32[3072]{0:T(1024)}, s32[3072]{0:T(1024)S(1)}, u32[]{:S(2)}) copy-start(s32[3072]{0:T(1024)S(1)} %add.196) | copy-start | bytes 36868 | tf_op jit(solution)/shard_map/while
  200.1 5.6 %copy-start.7 = (s32[1,256]{1,0:T(1,128)}, s32[1,256]{1,0:T(1,128)S(1)}, u32[]{:S(2)}) copy-start(s32[1,256]{1,0:T(1,128)S(1)} %get-tuple-element.297) | copy-start | bytes 3076 | tf_op jit(solution)/shard_map/while
  202.0 3.7 copy-start.3
  213.8 3.7 copy-start.8
  228.7 7.7 %copy-start.2 = (s32[3072]{0:T(1024)}, s32[3072]{0:T(1024)S(1)}, u32[]{:S(2)}) copy-start(s32[3072]{0:T(1024)S(1)} %add.196) | copy-start | bytes 36868 | tf_op jit(solution)/shard_map/while
  230.7 5.6 %copy-start.7 = (s32[1,256]{1,0:T(1,128)}, s32[1,256]{1,0:T(1,128)S(1)}, u32[]{:S(2)}) copy-start(s32[1,256]{1,0:T(1,128)S(1)} %get-tuple-element.297) | copy-start | bytes 3076 | tf_op jit(solution)/shard_map/while
  232.7 3.7 copy-start.3
  244.5 3.7 copy-start.8
  259.4 7.6 %copy-start.2 = (s32[3072]{0:T(1024)}, s32[3072]{0:T(1024)S(1)}, u32[]{:S(2)}) copy-start(s32[3072]{0:T(1024)S(1)} %add.196) | copy-start | bytes 36868 | tf_op jit(solution)/shard_map/while
  261.4 5.6 %copy-start.7 = (s32[1,256]{1,0:T(1,128)}, s32[1,256]{1,0:T(1,128)S(1)}, u32[]{:S(2)}) copy-start(s32[1,256]{1,0:T(1,128)S(1)} %get-tuple-element.297) | copy-start | bytes 3076 | tf_op jit(solution)/shard_map/while
  263.3 3.7 copy-start.3
  290.0 7.6 %copy-start.2 = (s32[3072]{0:T(1024)}, s32[3072]{0:T(1024)S(1)}, u32[]{:S(2)}) copy-start(s32[3072]{0:T(1024)S(1)} %add.196) | copy-start | bytes 36868 | tf_op jit(solution)/shard_map/while
  292.0 5.6 %copy-start.7 = (s32[1,256]{1,0:T(1,128)}, s32[1,256]{1,0:T(1,128)S(1)}, u32[]{:S(2)}) copy-start(s32[1,256]{1,0:T(1,128)S(1)} %get-tuple-element.297) | copy-start | bytes 3076 | tf_op jit(solution)/shard_map/while
  293.9 3.7 copy-start.3
  320.6 7.6 %copy-start.2 = (s32[3072]{0:T(1024)}, s32[3072]{0:T(1024)S(1)}, u32[]{:S(2)}) copy-start(s32[3072]{0:T(1024)S(1)} %add.196) | copy-start | bytes 36868 | tf_op jit(solution)/shard_map/while
  322.7 5.6 %copy-start.7 = (s32[1,256]{1,0:T(1,128)}, s32[1,256]{1,0:T(1,128)S(1)}, u32[]{:S(2)}) copy-start(s32[1,256]{1,0:T(1,128)S(1)} %get-tuple-element.297) | copy-start | bytes 3076 | tf_op jit(solution)/shard_map/while
  324.6 3.7 copy-start.3
  351.3 7.6 %copy-start.2 = (s32[3072]{0:T(1024)}, s32[3072]{0:T(1024)S(1)}, u32[]{:S(2)}) copy-start(s32[3072]{0:T(1024)S(1)} %add.196) | copy-start | bytes 36868 | tf_op jit(solution)/shard_map/while
  353.3 5.6 %copy-start.7 = (s32[1,256]{1,0:T(1,128)}, s32[1,256]{1,0:T(1,128)S(1)}, u32[]{:S(2)}) copy-start(s32[1,256]{1,0:T(1,128)S(1)} %get-tuple-element.297) | copy-start | bytes 3076 | tf_op jit(solution)/shard_map/while
  355.2 3.7 copy-start.3
  (31 other events, 55.3 us)
Sparse Core Ops, SparseCore 0:
  14.6 59.9 reduce-scatter.1
  376.6 46.8 all-gather.5
Sparse Core Ops, SparseCore 1:
  16.6 114.7 all-gather.3
where the time goes:
time: 440 us; the launch traced here: 436 us
  local copies, waits for them, and re-layouts  132 us (30%)
  waiting for transfers between devices  119 us (27%)
  other arithmetic  72.9 us (17%)
  matrix products  59.6 us (14%)
  blocking collectives  35.9 us (8%)
  between operations  15.6 us (4%)
    all_gather x1, waiting for transfers between devices, shards(): lax.all_gather(panels, ('section', 'owner'), axis=0, tiled=True)  54.1 us
    all_gather x1, waiting for transfers between devices, shards(): lax.all_gather(query_grad, 'section', axis=0, tiled=True)  45.7 us
    all_gather x1, blocking collectives, shards(): lax.all_gather(own_bias, ('section', 'owner'), axis=0, tiled=True)  35.9 us
    gather x8, local copies, waits for them, and re-layouts, score_block(): table_blocks[listed].reshape(list_width * block_size, embed_width)  32.2 us
    gather x8, local copies, waits for them, and re-layouts, score_block(): positive = cand_table[targets]  30.7 us
    dot_general x8, matrix products, score_block(): lax.dot_general(query_rows, cand_flat, (((1,), (1,)), ((), ())), preferre...  24.7 us
    dot_general x8, matrix products, score_block(): weighted = jnp.dot(weights, cand_flat, preferred_element_type=jnp.float32)  24.5 us
    gather x8, local copies, waits for them, and re-layouts, score_block(): bias_table[targets].astype(jnp.float32)  21.3 us
  transfers between devices with their start and end apart: 3, of which 3 were waited for; matrix products, arithmetic and copies ran while one was open for 2% of the time, Pallas kernels for 0%

commit v1 on v0

v1 whole, which is shorter than its diff:
```python
import functools

import jax
import jax.numpy as jnp
from jax import lax
from jax.experimental import pallas as pl
from jax.experimental.pallas import tpu as pltpu
from jax.sharding import PartitionSpec as P

BLOCK = 256
NEG_FILL = -1e30
BIAS_ROWS = 16


def score_kernel(list_width, lists_ref, lens_ref, tgt_ref,
                 q_ref, tcol_ref, tab_ref,
                 qg_ref, loss_ref,
                 tabf_ref, bias_ref, pos_ref, pb_ref):
    b = pl.program_id(0)
    n_shards, shard_rows, _ = tab_ref.shape
    own_rows = shard_rows - BIAS_ROWS
    per_shard = own_rows // BLOCK

    @pl.when(b == 0)
    def _():
        for s in range(n_shards):
            tabf_ref[pl.ds(s * own_rows, own_rows), :] = tab_ref[s, pl.ds(0, own_rows), :].astype(jnp.float32)
            extra = tab_ref[s, pl.ds(own_rows, BIAS_ROWS), :].astype(jnp.float32)
            bias_ref[pl.ds(s * per_shard, per_shard), :] = extra[0:per_shard]

    def gather_row(r, carry):
        t = tgt_ref[b * BLOCK + r]
        pos_ref[pl.ds(r, 1), :] = tabf_ref[pl.ds(t, 1), :]
        pb_ref[pl.ds(r, 1), :] = bias_ref[pl.ds(t // BLOCK, 1), :]
        return carry

    lax.fori_loop(0, BLOCK, gather_row, 0, unroll=8)

    q = q_ref[...]
    qf = q.astype(jnp.float32)
    tcol = tcol_ref[...]
    lane = lax.broadcasted_iota(jnp.int32, (BLOCK, BLOCK), 1)
    positive = pos_ref[...]
    pos_bias = jnp.sum(jnp.where(lane == (tcol % BLOCK), pb_ref[...], 0.0), axis=1, keepdims=True)
    pos_logit = jnp.sum(qf * positive, axis=1, keepdims=True) - pos_bias
    length = lens_ref[b]

    def logits_of(k):
        j = lists_ref[b * list_width + k]
        cand = tab_ref[j // per_shard, pl.ds(pl.multiple_of((j % per_shard) * BLOCK, BLOCK), BLOCK), :]
        brow = bias_ref[pl.ds(j, 1), :]
        logits = lax.dot_general(q, cand, (((1,), (1,)), ((), ())),
                                 preferred_element_type=jnp.float32) - brow
        usable = (lane + j * BLOCK) != tcol
        return cand, usable, jnp.where(usable, logits, NEG_FILL)

    def pass_one(k, carry):
        m, s = carry
        _, _, masked = logits_of(k)
        m_new = jnp.maximum(m, jnp.max(masked, axis=1, keepdims=True))
        s = s * jnp.exp(m - m_new) + jnp.sum(jnp.exp(masked - m_new), axis=1, keepdims=True)
        return m_new, s

    m, s = lax.fori_loop(0, length, pass_one, (pos_logit, jnp.ones_like(pos_logit)))
    log_total = m + jnp.log(s)

    def pass_two(k, acc):
        cand, usable, masked = logits_of(k)
        w = jnp.where(usable, jnp.exp(masked - log_total), 0.0).astype(jnp.bfloat16)
        return acc + jnp.dot(w, cand, preferred_element_type=jnp.float32)

    acc = lax.fori_loop(0, length, pass_two, jnp.zeros((BLOCK, q.shape[1]), jnp.float32))
    qg = acc + (jnp.exp(pos_logit - log_total) - 1.0) * positive
    qg_ref[...] = qg.astype(qg_ref.dtype)
    loss_ref[...] = log_total - pos_logit


def score(queries, target_slot, block_lists, list_lens, table):
    rows, embed = queries.shape
    n_blocks = rows // BLOCK
    n_shards, shard_rows, _ = table.shape
    own_rows = shard_rows - BIAS_ROWS
    n_cands = n_shards * own_rows
    list_width = block_lists.shape[1]
    grid_spec = pltpu.PrefetchScalarGridSpec(
        num_scalar_prefetch=3,
        grid=(n_blocks,),
        in_specs=[
            pl.BlockSpec((BLOCK, embed), lambda b, *_: (b, 0)),
            pl.BlockSpec((BLOCK, 1), lambda b, *_: (b, 0)),
            pl.BlockSpec(memory_space=pltpu.VMEM),
        ],
        out_specs=[
            pl.BlockSpec((BLOCK, embed), lambda b, *_: (b, 0)),
            pl.BlockSpec((BLOCK, 1), lambda b, *_: (b, 0)),
        ],
        scratch_shapes=[
            pltpu.VMEM((n_cands, embed), jnp.float32),
            pltpu.VMEM((n_cands // BLOCK, BLOCK), jnp.float32),
            pltpu.VMEM((BLOCK, embed), jnp.float32),
            pltpu.VMEM((BLOCK, BLOCK), jnp.float32),
        ],
    )
    flops = 2 * 2 * rows * embed * BLOCK * 8
    qg, loss = pl.pallas_call(
        functools.partial(score_kernel, list_width),
        grid_spec=grid_spec,
        out_shape=[
            jax.ShapeDtypeStruct((rows, embed), jnp.bfloat16),
            jax.ShapeDtypeStruct((rows, 1), jnp.float32),
        ],
        compiler_params=pltpu.CompilerParams(
            dimension_semantics=("arbitrary",),
            vmem_limit_bytes=60 * 1024 * 1024,
        ),
        cost_estimate=pl.CostEstimate(
            flops=flops, transcendentals=2 * rows * BLOCK * 8,
            bytes_accessed=table.size * 2 + rows * embed * 4),
    )(block_lists.reshape(-1), list_lens, target_slot,
      queries, target_slot.reshape(rows, 1), table)
    return qg, loss.reshape(rows)


def shards(hidden_rows, w_proj, panels, cand_ids, counts, target_slot, block_lists, list_lens):
    halves, rows_dev, width_half = hidden_rows.shape
    embed_width = w_proj.shape[1]
    flat_rows = hidden_rows.reshape(halves * rows_dev, width_half)
    queries = lax.psum_scatter(
        jnp.dot(flat_rows, w_proj, preferred_element_type=jnp.float32),
        "section",
        scatter_dimension=0,
        tiled=True,
    ).astype(jnp.bfloat16)
    own_bias = jnp.log(counts[cand_ids].astype(jnp.float32)).astype(jnp.bfloat16)
    own_rows = panels.shape[0]
    bias_rows = jnp.pad(own_bias.reshape(own_rows // BLOCK, BLOCK),
                        ((0, BIAS_ROWS - own_rows // BLOCK), (0, 0)))
    shard = jnp.concatenate([panels, bias_rows], axis=0)
    table = lax.all_gather(shard, ("section", "owner"), axis=0, tiled=False)
    query_grad, position_loss = score(queries, target_slot, block_lists, list_lens, table)
    trunk_grad = lax.dot_general(
        lax.all_gather(query_grad, "section", axis=0, tiled=True),
        w_proj,
        (((1,), (1,)), ((), ())),
        preferred_element_type=jnp.float32,
    ).astype(jnp.bfloat16)
    return (query_grad, position_loss, trunk_grad.reshape(halves, rows_dev, width_half))


def solution(mesh):
    return jax.shard_map(
        shards,
        mesh=mesh,
        in_specs=(
            P(None, ("owner", "pos"), "section"),
            P("section", None),
            P(("section", "owner"), None),
            P(("section", "owner")),
            P(),
            P(("section", "owner", "pos")),
            P(("section", "owner", "pos"), None),
            P(("section", "owner", "pos")),
        ),
        out_specs=(
            P(("section", "owner", "pos"), None),
            P(("section", "owner", "pos")),
            P(None, ("owner", "pos"), "section"),
        ),
        check_vma=False,
    )
```

time: 440 us -> 281 us (0.64)
  local copies, waits for them, and re-layouts: 132 us -> 6.87 us
  Pallas kernels: 0 us -> 80.3 us
  other arithmetic: 72.9 us -> 5.58 us
  matrix products: 59.6 us -> 10.3 us
  waiting for transfers between devices: 119 us -> 160 us
  blocking collectives: 35.9 us -> 0 us
    gather x32 -> x0, local copies, waits for them, and re-layouts: 94.5 us -> none  [the longest x8 32.2 us: score_block(): table_blocks[listed].reshape(list_width * block_size, embed_width)]
    pallas_call x0 -> x1, Pallas kernels: none -> 80.3 us  [score(): pl.pallas_call(functools.partial(score_kernel, list_width), grid_spec=gri...]
    dot_general x16 -> x0, matrix products: 49.3 us -> none  [the longest x8 24.7 us: score_block(): lax.dot_general(query_rows, cand_flat, (((1,), (1,)), ((), ())), preferre...]
    all_gather x1 -> x0, blocking collectives: 35.9 us -> none  [shards(): lax.all_gather(own_bias, ('section', 'owner'), axis=0, tiled=True)]
    reduce_scatter x1, waiting for transfers between devices: 18.7 us -> 53.2 us  [shards(): lax.psum_scatter(jnp.dot(flat_rows, w_proj, preferred_element_type=jnp.fl...]
    reduce_sum x16 -> x0, other arithmetic: 27 us -> none  [the longest x8 14.1 us: score_block(): jnp.sum(jnp.where(usable, jnp.exp(masked - row_max[:, None]), 0.0), axis=1)]
    select_n x16 -> x0, other arithmetic: 11.2 us -> none  [the longest x8 5.68 us: score_block(): positive = cand_table[targets]]
    dynamic_update_slice x8 -> x0, local copies, waits for them, and re-layouts: 10.4 us -> none  [shards(): lax.map(score_block, (queries.reshape(pos_blocks, block_size, embed_width...]
  transfers between devices with their start and end apart: 3 -> 3, of which waited for: 3 -> 3; matrix products, arithmetic and copies ran while one was open for 2% -> 4% of each run, Pallas kernels for 0% -> 0%
where the time goes in v1:
time: 281 us; the launch traced here: 279 us
  waiting for transfers between devices  160 us (57%)
  Pallas kernels  80.3 us (29%)
  between operations  15.5 us (6%)
  matrix products  10.3 us (4%)
  local copies, waits for them, and re-layouts  6.87 us (2%)
  other arithmetic  5.58 us (2%)
    pallas_call x1, Pallas kernels, score(): pl.pallas_call(functools.partial(score_kernel, list_width), grid_spec=gri...  80.3 us
    all_gather x1, waiting for transfers between devices, shards(): table = lax.all_gather(shard, ('section', 'owner'), axis=0, tiled=False)  54.1 us
    reduce_scatter x1, waiting for transfers between devices, shards(): lax.psum_scatter(jnp.dot(flat_rows, w_proj, preferred_element_type=jnp.fl...  53.2 us
    all_gather x1, waiting for transfers between devices, shards(): lax.all_gather(query_grad, 'section', axis=0, tiled=True)  52.9 us
  transfers between devices with their start and end apart: 3, of which 3 were waited for; matrix products, arithmetic and copies ran while one was open for 4% of the time, Pallas kernels for 0%

profile of v1, /device:TPU:1, one launch (start us, length us, event | category | flops | bytes accessed | tf_op | source)
XLA Modules:
  0.0 279.0 jit_solution(17819847347928840596)
XLA Ops:
  8.0 0.0 copy-start
  8.0 0.0 reduce-scatter.2.cloned.1.call-start
  8.1 0.9 copy-done
  9.0 5.5 %fusion.2 = f32[4096,256]{1,0:T(8,128)} fusion(bf16[4096,512]{1,0:T(8,128)(2,1)} %bitcast.9, bf16[512,256]{1,0:T(8,128)(2,1)S(1)} %copy-done), kind=kOutput, calls=%fused_computation.8 | convolution fusion | flops 1073741824 | bytes 8650752 | tf_op jit(solution)/shard_map/dot_general | solution.py:129
  14.4 0.0 copy-start.5
  14.4 0.0 copy-start.1
  14.4 0.0 copy-start.2
  14.4 0.0 copy-start.3
  14.4 0.0 copy-start.4
  14.4 0.0 reduce-scatter.2.cloned.1.call-update
  14.5 0.0 all-gather.6.cloned.1.call-start
  14.5 0.6 copy-done.5
  15.1 0.3 copy-done.1
  15.4 3.1 %gather_fusion = s32[512]{0:T(512)S(1)} fusion(s32[65536]{0:T(1024)S(1)} %copy-done.1, s32[1024]{0:T(1024)S(1)} %pad_clamp_fusion), kind=kCustom, calls=%fused_computation | custom fusion | bytes 6144 | tf_op jit(solution)/shard_map/gather | solution.py:134
  18.5 0.0 copy-done.2
  18.6 0.7 fusion.1
  19.3 0.0 all-gather.6.cloned.1.call-update
  19.3 0.0 all-gather.4.cloned.1.call-start
  19.4 0.0 copy-done.3
  19.4 1.4 copy.11.tcol_ref
  20.7 0.0 copy-done.4
  20.7 0.6 reshape.26.lists_ref
  21.3 53.2 %reduce-scatter.2.cloned.1.call-done = f32[2048,256]{1,0:T(8,128)} async-done(((f32[4096,256]{1,0:T(8,128)}), f32[2048,256]{1,0:T(8,128)}) %reduce-scatter.2.cloned.1.call-update) | async-done | bytes 2097168 | tf_op jit(solution)/shard_map/reduce_scatter | solution.py:128
  74.5 2.7 convert_element_type.20.q_ref
  77.2 54.1 %all-gather.6.cloned.1.call-done = bf16[8448,256]{1,0:T(8,128)(2,1)} async-done(((bf16[528,256]{1,0:T(8,128)(2,1)}), bf16[8448,256]{1,0:T(8,128)(2,1)}) %all-gather.6.cloned.1.call-update) | async-done | bytes 4325392 | tf_op jit(solution)/shard_map/all_gather | solution.py:139
  131.3 80.3 %shard_map.103 = (bf16[2048,256]{1,0:T(8,128)(2,1)}, f32[2048,1]{1,0:T(8,128)}) custom-call(s32[96]{0:T(128)} %reshape.26.lists_ref, s32[8]{0:T(128)} %lens_ref.1, s32[2048]{0:T(1024)} %tgt_ref.1, bf16[2048,256]{1,0:T(8,128)(2,1)} %convert_element_type.20.q_ref, s32[2048,1]{1,0:T(8,128)} %copy.11.tcol_ref, bf16[16,528,256]{2,1,0:T(8,128)(2,1)} %bitcast.11), custom_call_target="tpu_custom_call" | custom-call | flops 4294967296 | bytes 6422528 | tf_op jit(solution)/shard_map/pallas_call | solution.py:105
  211.6 0.0 all-gather.4.cloned.1.call-update
  211.6 2.2 reduce
  213.8 52.9 %all-gather.4.cloned.1.call-done = bf16[4096,256]{1,0:T(8,128)(2,1)} async-done(((bf16[2048,256]{1,0:T(8,128)(2,1)}), bf16[4096,256]{1,0:T(8,128)(2,1)}) %all-gather.4.cloned.1.call-update) | async-done | bytes 2097168 | tf_op jit(solution)/shard_map/all_gather | solution.py:142
  266.7 4.9 %convolution_convert_fusion = bf16[4096,512]{1,0:T(8,128)(2,1)} fusion(bf16[4096,256]{1,0:T(8,128)(2,1)} %all-gather.4.cloned.1.call-done, bf16[512,256]{1,0:T(8,128)(2,1)S(1)} %copy-done), kind=kOutput, calls=%fused_computation.1 | convolution fusion | flops 1075838976 | bytes 6553600 | tf_op jit(solution)/shard_map/dot_general | solution.py:141
  (4 shorter events, 0.0 us)
Async XLA Ops:
  8.0 1.0 copy-start
  8.0 66.5 %reduce-scatter.2.cloned.1.call-start = ((), (), s32[]{:S(2)}) async-start(), calls=%async_computation.1 | async-start | bytes 6291456 | tf_op jit(solution)/shard_map/reduce_scatter | solution.py:128
  14.4 0.7 copy-start.5
  14.4 1.0 copy-start.1
  14.4 4.1 %copy-start.2 = (bf16[512,256]{1,0:T(8,128)(2,1)S(1)}, bf16[512,256]{1,0:T(8,128)(2,1)}, u32[]{:S(2)}) copy-start(bf16[512,256]{1,0:T(8,128)(2,1)} %param.10) | copy-start | bytes 786436
  14.4 4.9 %copy-start.3 = (s32[2048]{0:T(1024)S(1)}, s32[2048]{0:T(1024)}, u32[]{:S(2)}) copy-start(s32[2048]{0:T(1024)} %tgt_ref.1) | copy-start | bytes 24580
  14.4 6.3 %copy-start.4 = (s32[8,12]{1,0:T(8,128)S(1)}, s32[8,12]{1,0:T(8,128)}, u32[]{:S(2)}) copy-start(s32[8,12]{1,0:T(8,128)} %param.14) | copy-start | bytes 1156
  14.5 116.9 %all-gather.6.cloned.1.call-start = ((), (), s32[]{:S(2)}) async-start(), calls=%async_computation.3 | async-start | bytes 4595712 | tf_op jit(solution)/shard_map/all_gather | solution.py:139
  19.3 247.4 %all-gather.4.cloned.1.call-start = ((), (), s32[]{:S(2)}) async-start(), calls=%async_computation.2 | async-start | bytes 3145728 | tf_op jit(solution)/shard_map/all_gather | solution.py:142
Sparse Core Ops, SparseCore 0:
  14.6 59.9 reduce-scatter.1
  211.7 54.9 all-gather.3
Sparse Core Ops, SparseCore 1:
  19.4 111.9 all-gather.5

commit v2 on v1

v2 whole, which is shorter than its diff:
```python
import functools

import jax
import jax.numpy as jnp
from jax import lax
from jax.experimental import pallas as pl
from jax.experimental.pallas import tpu as pltpu
from jax.sharding import PartitionSpec as P

BLOCK = 256
NEG_FILL = -1e30
BIAS_ROWS = 16
GROUP = 4
EXT = BLOCK + 128


def score_kernel(list_width, n_blocks,
                 lists_ref, lens_ref, tgt_ref, par_ref,
                 q_ref, tcol_ref, tab_a_ref, tab_b_ref,
                 qg_ref, loss_ref,
                 tabb_ref, tabf_ref, bias_ref, pos_ref, ls_ref, acc_ref, sem):
    b = pl.program_id(0)
    n_shards = tab_a_ref.shape[0]
    n_cand_blocks = 2 * n_shards

    def issue(block, slot):
        def one(r, carry):
            t = tgt_ref[block * BLOCK + r]
            pltpu.make_async_copy(tabf_ref.at[pl.ds(t, 1), :], pos_ref.at[slot, pl.ds(r, 1), :],
                                  sem.at[slot]).start()
            return carry
        lax.fori_loop(0, BLOCK, one, 0, unroll=8)

    @pl.when(b == 0)
    def _():
        mine = par_ref[0]
        for s in range(n_shards):
            for ref, par in ((tab_a_ref, mine), (tab_b_ref, 1 - mine)):
                j = 2 * s + par
                blk = ref[s, pl.ds(0, BLOCK), :]
                tabb_ref[j] = blk
                tabf_ref[pl.ds(pl.multiple_of(j * BLOCK, BLOCK), BLOCK), pl.ds(0, BLOCK)] = blk.astype(jnp.float32)
                extra = ref[s, pl.ds(BLOCK, BIAS_ROWS), :].astype(jnp.float32)
                bias_ref[pl.ds(j, 1), :] = extra[0:1]
        eye = (lax.broadcasted_iota(jnp.int32, (BLOCK, BLOCK), 0)
               == lax.broadcasted_iota(jnp.int32, (BLOCK, BLOCK), 1)).astype(jnp.float32)
        bias_col = lax.dot_general(eye, bias_ref[...], (((1,), (1,)), ((), ())),
                                   preferred_element_type=jnp.float32,
                                   precision=lax.Precision.HIGHEST)
        for j in range(n_cand_blocks):
            tabf_ref[pl.ds(j * BLOCK, BLOCK), pl.ds(BLOCK, 128)] = jnp.broadcast_to(
                bias_col[:, j:j + 1], (BLOCK, 128))
        issue(0, 0)

    slot = b % 2

    @pl.when(b + 1 < n_blocks)
    def _():
        issue(b + 1, 1 - slot)

    q = q_ref[...]
    qf = q.astype(jnp.float32)
    tcol = tcol_ref[...]
    lane = lax.broadcasted_iota(jnp.int32, (BLOCK, BLOCK), 1)
    length = lens_ref[b]
    n_groups = (length + GROUP - 1) // GROUP

    pltpu.make_async_copy(pos_ref.at[slot], pos_ref.at[slot], sem.at[slot]).wait()
    pos_ext = pos_ref[slot]
    positive = pos_ext[:, 0:BLOCK]
    pos_logit = jnp.sum(qf * positive, axis=1, keepdims=True) - pos_ext[:, BLOCK:BLOCK + 1]

    def pass_a(g, m):
        for i in range(GROUP):
            k = g * GROUP + i
            j = lists_ref[b * list_width + k]
            cand = tabb_ref[j]
            logits = lax.dot_general(q, cand, (((1,), (1,)), ((), ())),
                                     preferred_element_type=jnp.float32) - bias_ref[pl.ds(j, 1), :]
            usable = jnp.logical_and((lane + j * BLOCK) != tcol, k < length)
            masked = jnp.where(usable, logits, NEG_FILL)
            ls_ref[k] = masked
            m = jnp.maximum(m, jnp.max(masked, axis=1, keepdims=True))
        return m

    m = lax.fori_loop(0, n_groups, pass_a, pos_logit)

    def pass_b(g, s):
        for i in range(GROUP):
            s = s + jnp.exp(ls_ref[g * GROUP + i] - m)
        return s

    s_vec = lax.fori_loop(0, n_groups, pass_b, jnp.zeros((BLOCK, BLOCK), jnp.float32))
    row_sum = jnp.exp(pos_logit - m) + jnp.sum(s_vec, axis=1, keepdims=True)
    log_total = m + jnp.log(row_sum)

    acc_ref[...] = jnp.zeros_like(acc_ref)

    def pass_c(g, carry):
        part = None
        for i in range(GROUP):
            k = g * GROUP + i
            j = lists_ref[b * list_width + k]
            w = jnp.exp(ls_ref[k] - log_total).astype(jnp.bfloat16)
            d = jnp.dot(w, tabb_ref[j], preferred_element_type=jnp.float32)
            part = d if part is None else part + d
        acc_ref[...] += part
        return carry

    lax.fori_loop(0, n_groups, pass_c, 0)
    qg = acc_ref[...] + (jnp.exp(pos_logit - log_total) - 1.0) * positive
    qg_ref[...] = qg.astype(qg_ref.dtype)
    loss_ref[...] = log_total - pos_logit


def score(queries, target_slot, block_lists, list_lens, tab_a, tab_b, parity):
    rows, embed = queries.shape
    n_blocks = rows // BLOCK
    n_shards = tab_a.shape[0]
    n_cands = 2 * n_shards * BLOCK
    list_width = block_lists.shape[1]
    grid_spec = pltpu.PrefetchScalarGridSpec(
        num_scalar_prefetch=4,
        grid=(n_blocks,),
        in_specs=[
            pl.BlockSpec((BLOCK, embed), lambda b, *_: (b, 0)),
            pl.BlockSpec((BLOCK, 1), lambda b, *_: (b, 0)),
            pl.BlockSpec(memory_space=pltpu.VMEM),
            pl.BlockSpec(memory_space=pltpu.VMEM),
        ],
        out_specs=[
            pl.BlockSpec((BLOCK, embed), lambda b, *_: (b, 0)),
            pl.BlockSpec((BLOCK, 1), lambda b, *_: (b, 0)),
        ],
        scratch_shapes=[
            pltpu.VMEM((2 * n_shards, BLOCK, embed), jnp.bfloat16),
            pltpu.VMEM((n_cands, EXT), jnp.float32),
            pltpu.VMEM((2 * n_shards, BLOCK), jnp.float32),
            pltpu.VMEM((2, BLOCK, EXT), jnp.float32),
            pltpu.VMEM((list_width, BLOCK, BLOCK), jnp.float32),
            pltpu.VMEM((BLOCK, embed), jnp.float32),
            pltpu.SemaphoreType.DMA((2,)),
        ],
    )
    flops = 2 * 2 * rows * embed * BLOCK * 8
    qg, loss = pl.pallas_call(
        functools.partial(score_kernel, list_width, n_blocks),
        grid_spec=grid_spec,
        out_shape=[
            jax.ShapeDtypeStruct((rows, embed), jnp.bfloat16),
            jax.ShapeDtypeStruct((rows, 1), jnp.float32),
        ],
        compiler_params=pltpu.CompilerParams(
            dimension_semantics=("arbitrary",),
            vmem_limit_bytes=62 * 1024 * 1024,
        ),
        cost_estimate=pl.CostEstimate(
            flops=flops, transcendentals=2 * rows * BLOCK * 8,
            bytes_accessed=2 * tab_a.size * 2 + rows * embed * 4),
    )(block_lists.reshape(-1), list_lens, target_slot, parity,
      queries, target_slot.reshape(rows, 1), tab_a, tab_b)
    return qg, loss.reshape(rows)


def shards(hidden_rows, w_proj, panels, cand_ids, counts, target_slot, block_lists, list_lens):
    halves, rows_dev, width_half = hidden_rows.shape
    flat_rows = hidden_rows.reshape(halves * rows_dev, width_half)
    queries = lax.psum_scatter(
        jnp.dot(flat_rows, w_proj, preferred_element_type=jnp.float32),
        "section",
        scatter_dimension=0,
        tiled=True,
    ).astype(jnp.bfloat16)
    n_pos = lax.axis_size("pos")
    core = lax.axis_index("pos") % 2
    own_bias = jnp.log(counts[cand_ids].astype(jnp.float32)).astype(jnp.bfloat16)
    own_bias = own_bias.reshape(panels.shape[0] // BLOCK, BLOCK)
    my_block = lax.dynamic_slice_in_dim(panels, core * BLOCK, BLOCK, axis=0)
    my_bias = jnp.pad(lax.dynamic_slice_in_dim(own_bias, core, 1, axis=0), ((0, BIAS_ROWS - 1), (0, 0)))
    shard = jnp.concatenate([my_block, my_bias], axis=0)
    tab_a = lax.all_gather(shard, ("section", "owner"), axis=0, tiled=False)
    swap = [(i, i ^ 1) for i in range(n_pos)]
    tab_b = lax.ppermute(tab_a, "pos", swap)
    parity = core.astype(jnp.int32).reshape(1)
    query_grad, position_loss = score(queries, target_slot, block_lists, list_lens, tab_a, tab_b, parity)
    trunk_grad = lax.dot_general(
        lax.all_gather(query_grad, "section", axis=0, tiled=True),
        w_proj,
        (((1,), (1,)), ((), ())),
        preferred_element_type=jnp.float32,
    ).astype(jnp.bfloat16)
    return (query_grad, position_loss, trunk_grad.reshape(halves, rows_dev, width_half))


def solution(mesh):
    return jax.shard_map(
        shards,
        mesh=mesh,
        in_specs=(
            P(None, ("owner", "pos"), "section"),
            P("section", None),
            P(("section", "owner"), None),
            P(("section", "owner")),
            P(),
            P(("section", "owner", "pos")),
            P(("section", "owner", "pos"), None),
            P(("section", "owner", "pos")),
        ),
        out_specs=(
            P(("section", "owner", "pos"), None),
            P(("section", "owner", "pos")),
            P(None, ("owner", "pos"), "section"),
        ),
        check_vma=False,
    )
```

time: 281 us -> 238 us (0.85)
  Pallas kernels: 80.3 us -> 48 us
  waiting for transfers between devices: 160 us -> 143 us
  starting transfers between devices: 0.12 us -> 8.69 us
    reduce_scatter x1, waiting for transfers between devices: 53.2 us -> 0.01 us  [shards(): lax.psum_scatter(jnp.dot(flat_rows, w_proj, preferred_element_type=jnp.fl...]
    all_gather x1, waiting for transfers between devices: 54.1 us -> 102 us  [shards(): tab_a = lax.all_gather(shard, ('section', 'owner'), axis=0, tiled=False)]
    pallas_call x1, Pallas kernels: 80.3 us -> 48 us  [score(): pl.pallas_call(functools.partial(score_kernel, list_width, n_blocks), gri...]
    all_gather x1, waiting for transfers between devices: 52.9 us -> 40.3 us  [shards(): lax.all_gather(query_grad, 'section', axis=0, tiled=True)]
    ppermute x0 -> x1, starting transfers between devices: none -> 8.56 us  [shards(): tab_b = lax.ppermute(tab_a, 'pos', swap)]
  transfers between devices with their start and end apart: 3 -> 4, of which waited for: 3 -> 2; matrix products, arithmetic and copies ran while one was open for 4% -> 5% of each run, Pallas kernels for 0% -> 0%
where the time goes in v2:
time: 238 us
  waiting for transfers between devices  143 us (60%)
  Pallas kernels  48 us (20%)
  between operations  15.5 us (7%)
  matrix products  10.3 us (4%)
  starting transfers between devices  8.69 us (4%)
  local copies, waits for them, and re-layouts  6.53 us (3%)
  other arithmetic  6.23 us (3%)
    all_gather x1, waiting for transfers between devices, shards(): tab_a = lax.all_gather(shard, ('section', 'owner'), axis=0, tiled=False)  102 us
    pallas_call x1, Pallas kernels, score(): pl.pallas_call(functools.partial(score_kernel, list_width, n_blocks), gri...  48 us
    all_gather x1, waiting for transfers between devices, shards(): lax.all_gather(query_grad, 'section', axis=0, tiled=True)  40.3 us
    ppermute x1, starting transfers between devices, shards(): tab_b = lax.ppermute(tab_a, 'pos', swap)  8.56 us
    dot_general x1, matrix products, shards(): jnp.dot(flat_rows, w_proj, preferred_element_type=jnp.float32)  5.46 us
    dot_general x1, matrix products, shards(): lax.dot_general(lax.all_gather(query_grad, 'section', axis=0, tiled=True)...  4.89 us
  transfers between devices with their start and end apart: 4, of which 2 were waited for; matrix products, arithmetic and copies ran while one was open for 5% of the time, Pallas kernels for 0%

profile of v2, /device:TPU:1, one launch (start us, length us, event | category | flops | bytes accessed | tf_op | source)
XLA Modules:
  0.0 238.1 jit_solution(14964012360322681672)
XLA Ops:
  8.0 0.0 copy-start
  8.0 0.0 all-gather.6.cloned.1.call-start
  8.1 0.7 compare_select_fusion
  8.8 3.6 %gather_fusion = s32[512]{0:T(512)S(1)} fusion(s32[65536]{0:T(1024)} %param.12, s32[1024]{0:T(1024)S(1)} %pad_clamp_fusion), kind=kCustom, calls=%fused_computation | custom fusion | bytes 6144 | tf_op jit(solution)/shard_map/gather | solution.py:176
  12.5 0.9 constant_dynamic-slice_fusion.1
  13.4 0.7 fusion.1
  14.1 0.0 all-gather.6.cloned.1.call-update
  14.1 0.0 reduce-scatter.2.cloned.1.call-start
  14.1 0.0 copy-done
  14.2 5.5 %fusion.2 = f32[4096,256]{1,0:T(8,128)} fusion(bf16[4096,512]{1,0:T(8,128)(2,1)} %bitcast.10, bf16[512,256]{1,0:T(8,128)(2,1)S(1)} %copy-done), kind=kOutput, calls=%fused_computation.10 | convolution fusion | flops 1073741824 | bytes 8650752 | tf_op jit(solution)/shard_map/dot_general | solution.py:169
  19.6 0.0 copy-start.2
  19.6 0.0 copy-start.1
  19.6 0.0 reduce-scatter.2.cloned.1.call-update
  19.6 0.0 all-gather.4.cloned.1.call-start
  19.7 102.4 %all-gather.6.cloned.1.call-done = bf16[4352,256]{1,0:T(8,128)(2,1)} async-done(((bf16[272,256]{1,0:T(8,128)(2,1)}), bf16[4352,256]{1,0:T(8,128)(2,1)}) %all-gather.6.cloned.1.call-update) | async-done | bytes 2228240 | tf_op jit(solution)/shard_map/all_gather | solution.py:181
  122.1 8.6 %collective-permute-start = (bf16[16,272,256]{2,1,0:T(8,128)(2,1)}, bf16[16,272,256]{2,1,0:T(8,128)(2,1)}, u32[]{:S(2)}, u32[]{:S(2)}) collective-permute-start(bf16[16,272,256]{2,1,0:T(8,128)(2,1)} %bitcast.12), channel_id=1, source_target_pairs={{0,1},{1,0},{2,3},{3,2},{4,5},{5,4},{6,7},{7,6},{8,9},{9,8},{10,11... | collective-permute-start | bytes 6684680 | tf_op jit(solution)/shard_map/ppermute | solution.py:183
  130.6 0.0 copy-done.2
  130.7 0.6 reshape.29.lists_ref
  131.2 0.0 copy-done.1
  131.2 1.3 copy.11.tcol_ref
  132.6 0.0 reduce-scatter.2.cloned.1.call-done
  132.6 2.7 %convert_element_type.20.q_ref = bf16[2048,256]{1,0:T(8,128)(2,1)} convert(f32[2048,256]{1,0:T(8,128)} %reduce-scatter.2.cloned.1.call-done) | non-fusion elementwise | flops 524288 | bytes 3145728 | tf_op jit(solution)/shard_map/convert_element_type | solution.py:173
  135.3 0.0 collective-permute-done.tab_b_ref
  135.3 48.0 %shard_map.103 = (bf16[2048,256]{1,0:T(8,128)(2,1)}, f32[2048,1]{1,0:T(8,128)}) custom-call(s32[96]{0:T(128)} %reshape.29.lists_ref, s32[8]{0:T(128)} %lens_ref.1, s32[2048]{0:T(1024)} %tgt_ref.1, s32[1]{0:T(128)} %bitcast.par_ref, bf16[2048,256]{1,0:T(8,128)(2,1)} %convert_element_type.20.q_ref, s32[2048,1]{1,0:T(8,128)} %copy.11.tcol_ref, ...), custom_call_target="tpu_custom_call" | custom-call | flops 4294967296 | bytes 6553600 | tf_op jit(solution)/shard_map/pallas_call | solution.py:146
  183.3 0.0 all-gather.4.cloned.1.call-update
  183.3 2.2 reduce
  185.5 40.3 %all-gather.4.cloned.1.call-done = bf16[4096,256]{1,0:T(8,128)(2,1)} async-done(((bf16[2048,256]{1,0:T(8,128)(2,1)}), bf16[4096,256]{1,0:T(8,128)(2,1)}) %all-gather.4.cloned.1.call-update) | async-done | bytes 2097168 | tf_op jit(solution)/shard_map/all_gather | solution.py:187
  225.8 4.9 %convolution_convert_fusion = bf16[4096,512]{1,0:T(8,128)(2,1)} fusion(bf16[4096,256]{1,0:T(8,128)(2,1)} %all-gather.4.cloned.1.call-done, bf16[512,256]{1,0:T(8,128)(2,1)S(1)} %copy-done), kind=kOutput, calls=%fused_computation.1 | convolution fusion | flops 1075838976 | bytes 6553600 | tf_op jit(solution)/shard_map/dot_general | solution.py:186
  (4 shorter events, 0.0 us)
Async XLA Ops:
  8.0 6.2 %copy-start = (bf16[512,256]{1,0:T(8,128)(2,1)S(1)}, bf16[512,256]{1,0:T(8,128)(2,1)}, u32[]{:S(2)}) copy-start(bf16[512,256]{1,0:T(8,128)(2,1)} %param.9) | copy-start | bytes 786436
  8.0 114.1 %all-gather.6.cloned.1.call-start = ((), (), s32[]{:S(2)}) async-start(), calls=%async_computation.3 | async-start | bytes 2367488 | tf_op jit(solution)/shard_map/all_gather | solution.py:181
  14.1 118.5 %reduce-scatter.2.cloned.1.call-start = ((), (), s32[]{:S(2)}) async-start(), calls=%async_computation.1 | async-start | bytes 6291456 | tf_op jit(solution)/shard_map/reduce_scatter | solution.py:168
  19.6 111.0 %copy-start.2 = (s32[8,12]{1,0:T(8,128)S(1)}, s32[8,12]{1,0:T(8,128)}, u32[]{:S(2)}) copy-start(s32[8,12]{1,0:T(8,128)} %param.14) | copy-start | bytes 1156
  19.6 111.6 %copy-start.1 = (s32[2048]{0:T(1024)S(1)}, s32[2048]{0:T(1024)}, u32[]{:S(2)}) copy-start(s32[2048]{0:T(1024)} %tgt_ref.1) | copy-start | bytes 24580
  19.6 206.1 %all-gather.4.cloned.1.call-start = ((), (), s32[]{:S(2)}) async-start(), calls=%async_computation.2 | async-start | bytes 3145728 | tf_op jit(solution)/shard_map/all_gather | solution.py:187
  122.1 13.2 %collective-permute-start = (bf16[16,272,256]{2,1,0:T(8,128)(2,1)}, bf16[16,272,256]{2,1,0:T(8,128)(2,1)}, u32[]{:S(2)}, u32[]{:S(2)}) collective-permute-start(bf16[16,272,256]{2,1,0:T(8,128)(2,1)} %bitcast.12), channel_id=1, source_target_pairs={{0,1},{1,0},{2,3},{3,2},{4,5},{5,4},{6,7},{7,6},{8,9},{9,8},{10,11... | collective-permute-start | bytes 6684680 | tf_op jit(solution)/shard_map/ppermute | solution.py:183
Sparse Core Ops, SparseCore 0:
  14.2 107.8 all-gather.5
Sparse Core Ops, SparseCore 1:
  19.7 59.8 reduce-scatter.1
  183.4 42.4 all-gather.3

commit v3 on v2

--- a/solution.py
+++ b/solution.py
@@ -14,7 +14,7 @@
 EXT = BLOCK + 128
 
 
-def score_kernel(list_width, n_blocks,
+def score_kernel(list_width, n_blocks, dists,
                  lists_ref, lens_ref, tgt_ref, par_ref,
                  q_ref, tcol_ref, tab_a_ref, tab_b_ref,
                  qg_ref, loss_ref,
@@ -34,9 +34,14 @@
     @pl.when(b == 0)
     def _():
         mine = par_ref[0]
+        me = par_ref[1]
         for s in range(n_shards):
+            away = 0
+            for bit, d in enumerate(dists):
+                if (s >> bit) & 1:
+                    away ^= d
             for ref, par in ((tab_a_ref, mine), (tab_b_ref, 1 - mine)):
-                j = 2 * s + par
+                j = 2 * (me ^ away) + par
                 blk = ref[s, pl.ds(0, BLOCK), :]
                 tabb_ref[j] = blk
                 tabf_ref[pl.ds(pl.multiple_of(j * BLOCK, BLOCK), BLOCK), pl.ds(0, BLOCK)] = blk.astype(jnp.float32)
@@ -113,7 +118,7 @@
     loss_ref[...] = log_total - pos_logit
 
 
-def score(queries, target_slot, block_lists, list_lens, tab_a, tab_b, parity):
+def score(queries, target_slot, block_lists, list_lens, tab_a, tab_b, parity, dists):
     rows, embed = queries.shape
     n_blocks = rows // BLOCK
     n_shards = tab_a.shape[0]
@@ -144,7 +149,7 @@
     )
     flops = 2 * 2 * rows * embed * BLOCK * 8
     qg, loss = pl.pallas_call(
-        functools.partial(score_kernel, list_width, n_blocks),
+        functools.partial(score_kernel, list_width, n_blocks, dists),
         grid_spec=grid_spec,
         out_shape=[
             jax.ShapeDtypeStruct((rows, embed), jnp.bfloat16),
@@ -165,26 +170,39 @@
 def shards(hidden_rows, w_proj, panels, cand_ids, counts, target_slot, block_lists, list_lens):
     halves, rows_dev, width_half = hidden_rows.shape
     flat_rows = hidden_rows.reshape(halves * rows_dev, width_half)
-    queries = lax.psum_scatter(
-        jnp.dot(flat_rows, w_proj, preferred_element_type=jnp.float32),
-        "section",
-        scatter_dimension=0,
-        tiled=True,
-    ).astype(jnp.bfloat16)
+    n_sec = lax.axis_size("section")
+    sec = lax.axis_index("section")
+    partner = [(i, i ^ 1) for i in range(n_sec)]
+    partial = jnp.dot(flat_rows, w_proj, preferred_element_type=jnp.float32).reshape(halves, rows_dev, -1)
+    sent = lax.ppermute(lax.dynamic_index_in_dim(partial, 1 - sec, 0, keepdims=False), "section", partner)
+    queries = (lax.dynamic_index_in_dim(partial, sec, 0, keepdims=False) + sent).astype(jnp.bfloat16)
     n_pos = lax.axis_size("pos")
     core = lax.axis_index("pos") % 2
+    n_own = lax.axis_size("owner")
+    me = sec * n_own + lax.axis_index("owner")
     own_bias = jnp.log(counts[cand_ids].astype(jnp.float32)).astype(jnp.bfloat16)
     own_bias = own_bias.reshape(panels.shape[0] // BLOCK, BLOCK)
     my_block = lax.dynamic_slice_in_dim(panels, core * BLOCK, BLOCK, axis=0)
     my_bias = jnp.pad(lax.dynamic_slice_in_dim(own_bias, core, 1, axis=0), ((0, BIAS_ROWS - 1), (0, 0)))
-    shard = jnp.concatenate([my_block, my_bias], axis=0)
-    tab_a = lax.all_gather(shard, ("section", "owner"), axis=0, tiled=False)
-    swap = [(i, i ^ 1) for i in range(n_pos)]
-    tab_b = lax.ppermute(tab_a, "pos", swap)
-    parity = core.astype(jnp.int32).reshape(1)
-    query_grad, position_loss = score(queries, target_slot, block_lists, list_lens, tab_a, tab_b, parity)
+    buf = jnp.concatenate([my_block, my_bias], axis=0)[None]
+    n_group = n_sec * n_own
+    dists = []
+    d = n_group // 2
+    while d >= 1:
+        dists.append(d)
+        d //= 2
+    for d in dists:
+        got = lax.ppermute(buf, ("section", "owner"), [(i, i ^ d) for i in range(n_group)])
+        buf = jnp.concatenate([buf, got], axis=0)
+    tab_b = lax.ppermute(buf, "pos", [(i, i ^ 1) for i in range(n_pos)])
+    parity = jnp.stack([core, me]).astype(jnp.int32)
+    query_grad, position_loss = score(queries, target_slot, block_lists, list_lens, buf, tab_b, parity,
+                                      tuple(dists))
+    other_grad = lax.ppermute(query_grad, "section", partner)
+    both = jnp.where(sec == 0, jnp.concatenate([query_grad, other_grad], axis=0),
+                     jnp.concatenate([other_grad, query_grad], axis=0))
     trunk_grad = lax.dot_general(
-        lax.all_gather(query_grad, "section", axis=0, tiled=True),
+        both,
         w_proj,
         (((1,), (1,)), ((), ())),
         preferred_element_type=jnp.float32,

time: 238 us -> 168 us (0.71)
  the two profiles are of different devices: /device:TPU:1 before, /device:TPU:88 now
where the time goes in v3:
time: 168 us; the launch traced here: 165 us
  waiting for transfers between devices  83.3 us (50%)
  Pallas kernels  46 us (27%)
  local copies, waits for them, and re-layouts  11.1 us (7%)
  starting transfers between devices  8.41 us (5%)
  matrix products  8.32 us (5%)
  other arithmetic  7.23 us (4%)
    pallas_call x1, Pallas kernels, score(): pl.pallas_call(functools.partial(score_kernel, list_width, n_blocks, dist...  46 us
    ppermute x4, waiting for transfers between devices, shards(): lax.ppermute(buf, ('section', 'owner'), [(i, i ^ d) for i in range(n_grou...  36.8 us
    ppermute x1, waiting for transfers between devices, shards(): lax.ppermute(lax.dynamic_index_in_dim(partial, 1 - sec, 0, keepdims=False...  24 us
    ppermute x1, waiting for transfers between devices, shards(): other_grad = lax.ppermute(query_grad, 'section', partner)  22.5 us
    ppermute x4, starting transfers between devices, shards(): lax.ppermute(buf, ('section', 'owner'), [(i, i ^ d) for i in range(n_grou...  6.38 us
    dot_general x1, matrix products, shards(): lax.dot_general(both, w_proj, (((1,), (1,)), ((), ())), preferred_element...  4.88 us
    gather x1, local copies, waits for them, and re-layouts, shards(): counts[cand_ids].astype(jnp.float32)  3.63 us
    dot_general x1, matrix products, shards(): jnp.dot(flat_rows, w_proj, preferred_element_type=jnp.float32)  3.44 us
  transfers between devices with their start and end apart: 7, of which 6 were waited for; matrix products, arithmetic and copies ran while one was open for 10% of the time, Pallas kernels for 0%

profile of v3, /device:TPU:88, one launch (start us, length us, event | category | flops | bytes accessed | tf_op | source)
XLA Modules:
  0.0 165.1 jit_solution(9321716287797791669)
XLA Ops:
  0.6 0.0 copy-start
  0.7 0.7 compare_select_fusion
  1.4 3.6 %gather_fusion = s32[512]{0:T(512)S(1)} fusion(s32[65536]{0:T(1024)} %param.12, s32[1024]{0:T(1024)S(1)} %pad_clamp_fusion), kind=kCustom, calls=%fused_computation | custom fusion | bytes 6144 | tf_op jit(solution)/shard_map/gather | solution.py:183
  5.2 0.6 copy-done.2
  5.8 1.5 collective-permute-start.1
  7.3 3.9 %collective-permute-done.1 = bf16[1,272,256]{2,1,0:T(8,128)(2,1)S(1)} collective-permute-done((bf16[1,272,256]{2,1,0:T(8,128)(2,1)S(1)}, bf16[1,272,256]{2,1,0:T(8,128)(2,1)S(1)}, u32[]{:S(2)}, u32[]{:S(2)}) %collective-permute-start.1) | collective-permute-done | bytes 139296 | tf_op jit(solution)/shard_map/ppermute | solution.py:195
  11.2 3.1 %collective-permute-start.2 = (bf16[2,272,256]{2,1,0:T(8,128)(2,1)S(1)}, bf16[2,272,256]{2,1,0:T(8,128)(2,1)S(1)}, u32[]{:S(2)}, u32[]{:S(2)}) collective-permute-start(bf16[2,272,256]{2,1,0:T(8,128)(2,1)S(1)} %pad_maximum_fusion.2), channel_id=1, source_target_pairs={{0,32},{8,40},{16,48},{24,56},{32,0},{40,8},{48,16},{56,24},{64,96... | collective-permute-start | bytes 835592 | tf_op jit(solution)/shard_map/ppermute | solution.py:195
  14.4 6.0 %collective-permute-done.2 = bf16[2,272,256]{2,1,0:T(8,128)(2,1)S(1)} collective-permute-done((bf16[2,272,256]{2,1,0:T(8,128)(2,1)S(1)}, bf16[2,272,256]{2,1,0:T(8,128)(2,1)S(1)}, u32[]{:S(2)}, u32[]{:S(2)}) %collective-permute-start.2) | collective-permute-done | bytes 278560 | tf_op jit(solution)/shard_map/ppermute | solution.py:195
  20.4 0.1 pad_maximum_fusion.1
  20.4 0.1 collective-permute-start.3
  20.5 14.5 %collective-permute-done.3 = bf16[4,272,256]{2,1,0:T(8,128)(2,1)S(1)} collective-permute-done((bf16[4,272,256]{2,1,0:T(8,128)(2,1)S(1)}, bf16[4,272,256]{2,1,0:T(8,128)(2,1)S(1)}, u32[]{:S(2)}, u32[]{:S(2)}) %collective-permute-start.3) | collective-permute-done | bytes 557088 | tf_op jit(solution)/shard_map/ppermute | solution.py:195
  35.1 0.1 pad_maximum_fusion
  35.2 1.7 %collective-permute-start.4 = (bf16[8,272,256]{2,1,0:T(8,128)(2,1)S(1)}, bf16[8,272,256]{2,1,0:T(8,128)(2,1)S(1)}, u32[]{:S(2)}, u32[]{:S(2)}) collective-permute-start(bf16[8,272,256]{2,1,0:T(8,128)(2,1)S(1)} %pad_maximum_fusion), channel_id=1, source_target_pairs={{0,8},{8,0},{16,24},{24,16},{32,40},{40,32},{48,56},{56,48},{64,72... | collective-permute-start | bytes 3342344 | tf_op jit(solution)/shard_map/ppermute | solution.py:195
  36.9 3.4 %fusion.8 = f32[2,2048,256]{2,1,0:T(8,128)S(1)} fusion(bf16[2,2048,512]{2,1,0:T(8,128)(2,1)} %param.8, bf16[512,256]{1,0:T(8,128)(2,1)S(1)} %copy-done), kind=kOutput, calls=%fused_computation.17 | convolution fusion | flops 1073741824 | bytes 8650752 | tf_op jit(solution)/shard_map/dot_general | solution.py:176
  40.4 1.5 dynamic-slice_bitcast_fusion
  41.9 1.5 collective-permute-start
  43.3 0.7 constant_dynamic-update-slice_fusion.4
  44.0 0.7 constant_dynamic-update-slice_fusion.3
  44.7 0.7 constant_dynamic-update-slice_fusion.2
  45.4 0.8 constant_dynamic-update-slice_fusion.1
  46.2 12.4 %collective-permute-done.4 = bf16[8,272,256]{2,1,0:T(8,128)(2,1)S(1)} collective-permute-done((bf16[8,272,256]{2,1,0:T(8,128)(2,1)S(1)}, bf16[8,272,256]{2,1,0:T(8,128)(2,1)S(1)}, u32[]{:S(2)}, u32[]{:S(2)}) %collective-permute-start.4) | collective-permute-done | bytes 1114144 | tf_op jit(solution)/shard_map/ppermute | solution.py:195
  58.6 1.1 constant_dynamic-update-slice_fusion.tab_a_ref
  59.7 0.6 reshape.27.lists_ref
  60.3 1.3 copy.11.tcol_ref
  61.6 0.6 pad_add_fusion.par_ref
  62.2 24.0 %collective-permute-done = f32[2048,256]{1,0:T(8,128)S(1)} collective-permute-done((f32[2048,256]{1,0:T(8,128)}, f32[2048,256]{1,0:T(8,128)S(1)}, u32[]{:S(2)}, u32[]{:S(2)}) %collective-permute-start) | collective-permute-done | bytes 2097184 | tf_op jit(solution)/shard_map/ppermute | solution.py:177
  86.2 2.8 %fusion.5.q_ref = bf16[2048,256]{1,0:T(8,128)(2,1)} fusion(f32[2048,256]{1,0:T(8,128)S(1)} %collective-permute-done, f32[2,2048,256]{2,1,0:T(8,128)} %copy-done.1, s32[]{:T(128)S(6)} %select_n.32), kind=kLoop, calls=%fused_computation.9 | loop fusion | flops 1048576 | bytes 5242884 | tf_op jit(solution)/shard_map/convert_element_type | solution.py:178
  89.0 46.0 %shard_map.103 = (bf16[2048,256]{1,0:T(8,128)(2,1)}, f32[2048,1]{1,0:T(8,128)}) custom-call(s32[96]{0:T(128)} %reshape.27.lists_ref, s32[8]{0:T(128)} %lens_ref.1, s32[2048]{0:T(1024)} %tgt_ref.1, s32[2]{0:T(128)} %pad_add_fusion.par_ref, bf16[2048,256]{1,0:T(8,128)(2,1)} %fusion.5.q_ref, s32[2048,1]{1,0:T(8,128)} %copy.11.tcol_ref, ...), custom_call_target="tpu_custom_call" | custom-call | flops 4294967296 | bytes 6553600 | tf_op jit(solution)/shard_map/pallas_call | solution.py:151
  135.0 0.5 collective-permute-start.6
  135.6 2.2 %reduce = f32[2048]{0:T(1024)} reduce(f32[2048,1]{1,0:T(8,128)} %get-tuple-element.6, f32[]{:T(128)} %constant.51), dimensions={1}, to_apply=%get-tuple-element.6.reduce_sub_computation | reduce | bytes 16388 | tf_op jit(solution)/shard_map/pallas_call | solution.py:151
  137.7 22.5 %collective-permute-done.6 = bf16[2048,256]{1,0:T(8,128)(2,1)S(1)} collective-permute-done((bf16[2048,256]{1,0:T(8,128)(2,1)}, bf16[2048,256]{1,0:T(8,128)(2,1)S(1)}, u32[]{:S(2)}, u32[]{:S(2)}) %collective-permute-start.6) | collective-permute-done | bytes 1048608 | tf_op jit(solution)/shard_map/ppermute | solution.py:201
  160.2 4.9 %convolution_convert_fusion = bf16[4096,512]{1,0:T(8,128)(2,1)} fusion(bf16[512,256]{1,0:T(8,128)(2,1)S(1)} %copy-done, bf16[2048,256]{1,0:T(8,128)(2,1)S(1)} %collective-permute-done.6, bf16[2048,256]{1,0:T(8,128)(2,1)} %get-tuple-element.2, pred[]{:T(512)S(6)} %eq.5), kind=kOutput, calls=%fused_computation.1 | convolution fusion | flops 1085276160 | bytes 6553601 | tf_op jit(solution)/shard_map/dot_general | solution.py:204
  (21 shorter events, 0.1 us)
Async XLA Ops:
  0.6 36.3 %copy-start = (bf16[512,256]{1,0:T(8,128)(2,1)S(1)}, bf16[512,256]{1,0:T(8,128)(2,1)}, u32[]{:S(2)}) copy-start(bf16[512,256]{1,0:T(8,128)(2,1)} %param.9) | copy-start | bytes 786436
  0.6 4.5 %copy-start.4 = (bf16[512,256]{1,0:T(8,128)(2,1)S(1)}, bf16[512,256]{1,0:T(8,128)(2,1)}, u32[]{:S(2)}) copy-start(bf16[512,256]{1,0:T(8,128)(2,1)} %param.10) | copy-start | bytes 786436
  5.1 0.7 copy-start.2
  5.8 5.4 %collective-permute-start.1 = (bf16[1,272,256]{2,1,0:T(8,128)(2,1)S(1)}, bf16[1,272,256]{2,1,0:T(8,128)(2,1)S(1)}, u32[]{:S(2)}, u32[]{:S(2)}) collective-permute-start(bf16[1,272,256]{2,1,0:T(8,128)(2,1)S(1)} %fusion.11), channel_id=1, source_target_pairs={{0,64},{8,72},{16,80},{24,88},{32,96},{40,104},{48,112},{56,120},{... | collective-permute-start | bytes 417800 | tf_op jit(solution)/shard_map/ppermute | solution.py:195
  11.2 9.1 %collective-permute-start.2 = (bf16[2,272,256]{2,1,0:T(8,128)(2,1)S(1)}, bf16[2,272,256]{2,1,0:T(8,128)(2,1)S(1)}, u32[]{:S(2)}, u32[]{:S(2)}) collective-permute-start(bf16[2,272,256]{2,1,0:T(8,128)(2,1)S(1)} %pad_maximum_fusion.2), channel_id=1, source_target_pairs={{0,32},{8,40},{16,48},{24,56},{32,0},{40,8},{48,16},{56,24},{64,96... | collective-permute-start | bytes 835592 | tf_op jit(solution)/shard_map/ppermute | solution.py:195
  20.4 14.6 %collective-permute-start.3 = (bf16[4,272,256]{2,1,0:T(8,128)(2,1)S(1)}, bf16[4,272,256]{2,1,0:T(8,128)(2,1)S(1)}, u32[]{:S(2)}, u32[]{:S(2)}) collective-permute-start(bf16[4,272,256]{2,1,0:T(8,128)(2,1)S(1)} %pad_maximum_fusion.1), channel_id=1, source_target_pairs={{0,16},{8,24},{16,0},{24,8},{32,48},{40,56},{48,32},{56,40},{64,80... | collective-permute-start | bytes 1671176 | tf_op jit(solution)/shard_map/ppermute | solution.py:195
  35.2 23.4 %collective-permute-start.4 = (bf16[8,272,256]{2,1,0:T(8,128)(2,1)S(1)}, bf16[8,272,256]{2,1,0:T(8,128)(2,1)S(1)}, u32[]{:S(2)}, u32[]{:S(2)}) collective-permute-start(bf16[8,272,256]{2,1,0:T(8,128)(2,1)S(1)} %pad_maximum_fusion), channel_id=1, source_target_pairs={{0,8},{8,0},{16,24},{24,16},{32,40},{40,32},{48,56},{56,48},{64,72... | collective-permute-start | bytes 3342344 | tf_op jit(solution)/shard_map/ppermute | solution.py:195
  40.3 3.7 %copy-start.1 = (f32[2,2048,256]{2,1,0:T(8,128)}, f32[2,2048,256]{2,1,0:T(8,128)S(1)}, u32[]{:S(2)}) copy-start(f32[2,2048,256]{2,1,0:T(8,128)S(1)} %fusion.8) | copy-start | bytes 12582916
  40.3 3.0 %copy-start.3 = (bf16[256,256]{1,0:T(8,128)(2,1)S(1)}, bf16[256,256]{1,0:T(8,128)(2,1)}, u32[]{:S(2)}) copy-start(bf16[256,256]{1,0:T(8,128)(2,1)} %copy-done.2) | copy-start | bytes 393220
  41.9 17.8 %copy-start.6 = (s32[8,12]{1,0:T(8,128)S(1)}, s32[8,12]{1,0:T(8,128)}, u32[]{:S(2)}) copy-start(s32[8,12]{1,0:T(8,128)} %param.14) | copy-start | bytes 1156
  41.9 18.4 %copy-start.5 = (s32[2048]{0:T(1024)S(1)}, s32[2048]{0:T(1024)}, u32[]{:S(2)}) copy-start(s32[2048]{0:T(1024)} %tgt_ref.1) | copy-start | bytes 24580
  41.9 44.3 %collective-permute-start = (f32[2048,256]{1,0:T(8,128)}, f32[2048,256]{1,0:T(8,128)S(1)}, u32[]{:S(2)}, u32[]{:S(2)}) collective-permute-start(f32[2048,256]{1,0:T(8,128)} %dynamic-slice_bitcast_fusion), channel_id=1, source_target_pairs={{0,64},{64,0},{1,65},{65,1},{2,66},{66,2},{3,67},{67,3},{4,68},{68... | collective-permute-start | bytes 6291464 | tf_op jit(solution)/shard_map/ppermute | solution.py:177
  59.7 29.4 %collective-permute-start.5 = (bf16[16,272,256]{2,1,0:T(8,128)(2,1)}, bf16[16,272,256]{2,1,0:T(8,128)(2,1)}, u32[]{:S(2)}, u32[]{:S(2)}) collective-permute-start(bf16[16,272,256]{2,1,0:T(8,128)(2,1)} %constant_dynamic-update-slice_fusion.tab_a_ref), channel_id=1, source_target_pairs={{0,1},{1,0},{2,3},{3,2},{4,5},{5,4},{6,7},{7,6},{8,9},{9,8},{10,11... | collective-permute-start | bytes 6684680 | tf_op jit(solution)/shard_map/ppermute | solution.py:197
  135.0 25.2 %collective-permute-start.6 = (bf16[2048,256]{1,0:T(8,128)(2,1)}, bf16[2048,256]{1,0:T(8,128)(2,1)S(1)}, u32[]{:S(2)}, u32[]{:S(2)}) collective-permute-start(bf16[2048,256]{1,0:T(8,128)(2,1)} %get-tuple-element.2), channel_id=1, source_target_pairs={{0,64},{64,0},{1,65},{65,1},{2,66},{66,2},{3,67},{67,3},{4,68},{68... | collective-permute-start | bytes 3145736 | tf_op jit(solution)/shard_map/ppermute | solution.py:201

commit v4 on v3

--- a/solution.py
+++ b/solution.py
@@ -174,8 +174,6 @@
     sec = lax.axis_index("section")
     partner = [(i, i ^ 1) for i in range(n_sec)]
     partial = jnp.dot(flat_rows, w_proj, preferred_element_type=jnp.float32).reshape(halves, rows_dev, -1)
-    sent = lax.ppermute(lax.dynamic_index_in_dim(partial, 1 - sec, 0, keepdims=False), "section", partner)
-    queries = (lax.dynamic_index_in_dim(partial, sec, 0, keepdims=False) + sent).astype(jnp.bfloat16)
     n_pos = lax.axis_size("pos")
     core = lax.axis_index("pos") % 2
     n_own = lax.axis_size("owner")
@@ -185,15 +183,21 @@
     my_block = lax.dynamic_slice_in_dim(panels, core * BLOCK, BLOCK, axis=0)
     my_bias = jnp.pad(lax.dynamic_slice_in_dim(own_bias, core, 1, axis=0), ((0, BIAS_ROWS - 1), (0, 0)))
     buf = jnp.concatenate([my_block, my_bias], axis=0)[None]
+    partial, buf = lax.optimization_barrier((partial, buf))
     n_group = n_sec * n_own
     dists = []
-    d = n_group // 2
-    while d >= 1:
-        dists.append(d)
-        d //= 2
-    for d in dists:
-        got = lax.ppermute(buf, ("section", "owner"), [(i, i ^ d) for i in range(n_group)])
-        buf = jnp.concatenate([buf, got], axis=0)
+    step = 1
+    while step < n_group:
+        radix = min(4, n_group // step)
+        got = [lax.ppermute(buf, ("section", "owner"), [(i, i ^ (m * step)) for i in range(n_group)])
+               for m in range(1, radix)]
+        buf = jnp.concatenate([buf] + got, axis=0)
+        while radix > 1:
+            dists.append(step)
+            step *= 2
+            radix //= 2
+    sent = lax.ppermute(lax.dynamic_index_in_dim(partial, 1 - sec, 0, keepdims=False), "section", partner)
+    queries = (lax.dynamic_index_in_dim(partial, sec, 0, keepdims=False) + sent).astype(jnp.bfloat16)
     tab_b = lax.ppermute(buf, "pos", [(i, i ^ 1) for i in range(n_pos)])
     parity = jnp.stack([core, me]).astype(jnp.int32)
     query_grad, position_loss = score(queries, target_slot, block_lists, list_lens, buf, tab_b, parity,

time: 168 us -> 180 us (1.071)
  the two profiles are of different devices: /device:TPU:88 before, /device:TPU:1 now
where the time goes in v4:
time: 180 us; the launch traced here: 181 us
  waiting for transfers between devices  84.1 us (47%)
  Pallas kernels  51.1 us (28%)
  local copies, waits for them, and re-layouts  15.2 us (8%)
  starting transfers between devices  13.5 us (8%)
  matrix products  10.4 us (6%)
  other arithmetic  6.35 us (4%)
    pallas_call x1, Pallas kernels, score(): pl.pallas_call(functools.partial(score_kernel, list_width, n_blocks, dist...  51.1 us
    ppermute x1, waiting for transfers between devices, shards(): lax.ppermute(lax.dynamic_index_in_dim(partial, 1 - sec, 0, keepdims=False...  37 us
    ppermute x6, waiting for transfers between devices, shards(): lax.ppermute(buf, ('section', 'owner'), [(i, i ^ m * step) for i in range...  24.4 us
    ppermute x1, waiting for transfers between devices, shards(): other_grad = lax.ppermute(query_grad, 'section', partner)  22.7 us
    ppermute x6, starting transfers between devices, shards(): lax.ppermute(buf, ('section', 'owner'), [(i, i ^ m * step) for i in range...  9.45 us
    dot_general x1, matrix products, shards(): jnp.dot(flat_rows, w_proj, preferred_element_type=jnp.float32)  5.49 us
    unnamed x13, local copies, waits for them, and re-layouts  4.91 us
    dot_general x1, matrix products, shards(): lax.dot_general(both, w_proj, (((1,), (1,)), ((), ())), preferred_element...  4.88 us
  transfers between devices with their start and end apart: 9, of which 7 were waited for; matrix products, arithmetic and copies ran while one was open for 9% of the time, Pallas kernels for 0%

profile of v4, /device:TPU:1, one launch (start us, length us, event | category | flops | bytes accessed | tf_op | source)
XLA Modules:
  0.0 181.4 jit_solution(49353040587885113)
XLA Ops:
  0.7 0.7 compare_select_fusion
  1.4 3.6 %gather_fusion = s32[512]{0:T(512)S(1)} fusion(s32[65536]{0:T(1024)} %param.12, s32[1024]{0:T(1024)S(1)} %pad_clamp_fusion), kind=kCustom, calls=%fused_computation | custom fusion | bytes 6144 | tf_op jit(solution)/shard_map/gather | solution.py:181
  5.1 5.5 %fusion.8 = f32[2,2048,256]{2,1,0:T(8,128)} fusion(bf16[2,2048,512]{2,1,0:T(8,128)(2,1)} %param.8, bf16[512,256]{1,0:T(8,128)(2,1)S(1)} %copy-done), kind=kOutput, calls=%fused_computation.14 | convolution fusion | flops 1073741824 | bytes 8650752 | tf_op jit(solution)/shard_map/dot_general | solution.py:176
  10.6 2.5 %collective-permute-start.1 = (bf16[1,272,256]{2,1,0:T(8,128)(2,1)S(1)}, bf16[1,272,256]{2,1,0:T(8,128)(2,1)S(1)}, u32[]{:S(2)}, u32[]{:S(2)}) collective-permute-start(bf16[1,272,256]{2,1,0:T(8,128)(2,1)S(1)} %fusion.11), channel_id=1, source_target_pairs={{0,8},{8,0},{16,24},{24,16},{32,40},{40,32},{48,56},{56,48},{64,72... | collective-permute-start | bytes 417800 | tf_op jit(solution)/shard_map/ppermute | solution.py:192
  13.2 3.3 %collective-permute-start.2 = (bf16[1,272,256]{2,1,0:T(8,128)(2,1)S(1)}, bf16[1,272,256]{2,1,0:T(8,128)(2,1)S(1)}, u32[]{:S(2)}, u32[]{:S(2)}) collective-permute-start(bf16[1,272,256]{2,1,0:T(8,128)(2,1)S(1)} %fusion.11), channel_id=1, source_target_pairs={{0,16},{8,24},{16,0},{24,8},{32,48},{40,56},{48,32},{56,40},{64,80... | collective-permute-start | bytes 417800 | tf_op jit(solution)/shard_map/ppermute | solution.py:192
  16.5 0.7 constant_dynamic-update-slice_fusion.3
  17.2 0.7 constant_dynamic-update-slice_fusion.2
  17.9 4.6 %collective-permute-done.2 = bf16[1,272,256]{2,1,0:T(8,128)(2,1)S(1)} collective-permute-done((bf16[1,272,256]{2,1,0:T(8,128)(2,1)S(1)}, bf16[1,272,256]{2,1,0:T(8,128)(2,1)S(1)}, u32[]{:S(2)}, u32[]{:S(2)}) %collective-permute-start.2) | collective-permute-done | bytes 139296 | tf_op jit(solution)/shard_map/ppermute | solution.py:192
  22.5 0.7 constant_dynamic-update-slice_fusion.1
  23.3 1.9 %collective-permute-done.3 = bf16[1,272,256]{2,1,0:T(8,128)(2,1)S(1)} collective-permute-done((bf16[1,272,256]{2,1,0:T(8,128)(2,1)S(1)}, bf16[1,272,256]{2,1,0:T(8,128)(2,1)S(1)}, u32[]{:S(2)}, u32[]{:S(2)}) %collective-permute-start.3) | collective-permute-done | bytes 139296 | tf_op jit(solution)/shard_map/ppermute | solution.py:192
  25.1 0.7 constant_dynamic-update-slice_fusion
  25.8 2.7 %collective-permute-start.4 = (bf16[4,272,256]{2,1,0:T(8,128)(2,1)}, bf16[4,272,256]{2,1,0:T(8,128)(2,1)}, u32[]{:S(2)}, u32[]{:S(2)}) collective-permute-start(bf16[4,272,256]{2,1,0:T(8,128)(2,1)} %get-tuple-element.11), channel_id=1, source_target_pairs={{0,32},{8,40},{16,48},{24,56},{32,0},{40,8},{48,16},{56,24},{64,96... | collective-permute-start | bytes 1671176 | tf_op jit(solution)/shard_map/ppermute | solution.py:192
  28.6 0.3 collective-permute-start.5
  28.9 0.5 collective-permute-start.6
  29.5 3.1 %dynamic-slice_bitcast_fusion = f32[2048,256]{1,0:T(8,128)} fusion(f32[2,2048,256]{2,1,0:T(8,128)} %fusion.8, s32[]{:T(128)S(6)} %select_n.36), kind=kLoop, calls=%fused_computation.10 | loop fusion | bytes 4194308 | tf_op jit(solution)/shard_map/jit(dynamic_index_in_dim)/squeeze | solution.py:199
  32.6 0.9 collective-permute-start
  33.4 7.3 %collective-permute-done.4 = bf16[4,272,256]{2,1,0:T(8,128)(2,1)} collective-permute-done((bf16[4,272,256]{2,1,0:T(8,128)(2,1)}, bf16[4,272,256]{2,1,0:T(8,128)(2,1)}, u32[]{:S(2)}, u32[]{:S(2)}) %collective-permute-start.4) | collective-permute-done | bytes 557088 | tf_op jit(solution)/shard_map/ppermute | solution.py:192
  40.7 1.9 %constant_dynamic-update-slice_fusion.6 = bf16[16,272,256]{2,1,0:T(8,128)(2,1)} fusion(bf16[16,272,256]{2,1,0:T(8,128)(2,1)} %get-tuple-element.12, bf16[4,272,256]{2,1,0:T(8,128)(2,1)} %collective-permute-done.4), kind=kLoop, calls=%fused_computation.24 | loop fusion | bytes 1114112
  42.6 10.0 %collective-permute-done.5 = bf16[4,272,256]{2,1,0:T(8,128)(2,1)S(1)} collective-permute-done((bf16[4,272,256]{2,1,0:T(8,128)(2,1)}, bf16[4,272,256]{2,1,0:T(8,128)(2,1)S(1)}, u32[]{:S(2)}, u32[]{:S(2)}) %collective-permute-start.5) | collective-permute-done | bytes 557088 | tf_op jit(solution)/shard_map/ppermute | solution.py:192
  52.6 0.8 constant_dynamic-update-slice_fusion.5
  53.5 0.6 collective-permute-done.6
  54.0 0.8 constant_dynamic-update-slice_fusion.4.tab_a_ref
  54.9 3.1 %collective-permute-start.7 = (bf16[16,272,256]{2,1,0:T(8,128)(2,1)}, bf16[16,272,256]{2,1,0:T(8,128)(2,1)}, u32[]{:S(2)}, u32[]{:S(2)}) collective-permute-start(bf16[16,272,256]{2,1,0:T(8,128)(2,1)} %constant_dynamic-update-slice_fusion.4.tab_a_ref), channel_id=1, source_target_pairs={{0,1},{1,0},{2,3},{3,2},{4,5},{5,4},{6,7},{7,6},{8,9},{9,8},{10,11... | collective-permute-start | bytes 6684680 | tf_op jit(solution)/shard_map/ppermute | solution.py:201
  58.0 0.6 reshape.27.lists_ref
  58.6 1.3 copy.11.tcol_ref
  60.0 0.6 pad_add_fusion.par_ref
  60.6 37.0 %collective-permute-done = f32[2048,256]{1,0:T(8,128)S(1)} collective-permute-done((f32[2048,256]{1,0:T(8,128)}, f32[2048,256]{1,0:T(8,128)S(1)}, u32[]{:S(2)}, u32[]{:S(2)}) %collective-permute-start) | collective-permute-done | bytes 2097184 | tf_op jit(solution)/shard_map/ppermute | solution.py:199
  97.5 2.8 %fusion.5.q_ref = bf16[2048,256]{1,0:T(8,128)(2,1)} fusion(f32[2048,256]{1,0:T(8,128)S(1)} %collective-permute-done, f32[2,2048,256]{2,1,0:T(8,128)} %fusion.8, s32[]{:T(128)S(6)} %select_n.35), kind=kLoop, calls=%fused_computation.9 | loop fusion | flops 1048576 | bytes 5242884 | tf_op jit(solution)/shard_map/convert_element_type | solution.py:200
  100.4 51.1 %shard_map.103 = (bf16[2048,256]{1,0:T(8,128)(2,1)}, f32[2048,1]{1,0:T(8,128)}) custom-call(s32[96]{0:T(128)} %reshape.27.lists_ref, s32[8]{0:T(128)} %lens_ref.1, s32[2048]{0:T(1024)} %tgt_ref.1, s32[2]{0:T(128)} %pad_add_fusion.par_ref, bf16[2048,256]{1,0:T(8,128)(2,1)} %fusion.5.q_ref, s32[2048,1]{1,0:T(8,128)} %copy.11.tcol_ref, ...), custom_call_target="tpu_custom_call" | custom-call | flops 4294967296 | bytes 6553600 | tf_op jit(solution)/shard_map/pallas_call | solution.py:151
  151.6 2.2 %reduce = f32[2048]{0:T(1024)} reduce(f32[2048,1]{1,0:T(8,128)} %get-tuple-element.10, f32[]{:T(128)} %constant.51), dimensions={1}, to_apply=%get-tuple-element.10.reduce_sub_computation | reduce | bytes 16388 | tf_op jit(solution)/shard_map/pallas_call | solution.py:151
  153.8 22.7 %collective-permute-done.8 = bf16[2048,256]{1,0:T(8,128)(2,1)S(1)} collective-permute-done((bf16[2048,256]{1,0:T(8,128)(2,1)}, bf16[2048,256]{1,0:T(8,128)(2,1)S(1)}, u32[]{:S(2)}, u32[]{:S(2)}) %collective-permute-start.8) | collective-permute-done | bytes 1048608 | tf_op jit(solution)/shard_map/ppermute | solution.py:205
  176.5 4.9 %convolution_convert_fusion = bf16[4096,512]{1,0:T(8,128)(2,1)} fusion(bf16[512,256]{1,0:T(8,128)(2,1)S(1)} %copy-done, bf16[2048,256]{1,0:T(8,128)(2,1)S(1)} %collective-permute-done.8, bf16[2048,256]{1,0:T(8,128)(2,1)} %get-tuple-element.4, pred[]{:T(512)S(6)} %eq.5), kind=kOutput, calls=%fused_computation.1 | convolution fusion | flops 1085276160 | bytes 6553601 | tf_op jit(solution)/shard_map/dot_general | solution.py:208
  (18 shorter events, 0.2 us)
Async XLA Ops:
  0.6 4.4 %copy-start = (bf16[512,256]{1,0:T(8,128)(2,1)S(1)}, bf16[512,256]{1,0:T(8,128)(2,1)}, u32[]{:S(2)}) copy-start(bf16[512,256]{1,0:T(8,128)(2,1)} %param.9) | copy-start | bytes 786436
  5.1 5.5 %copy-start.1 = (bf16[512,256]{1,0:T(8,128)(2,1)S(1)}, bf16[512,256]{1,0:T(8,128)(2,1)}, u32[]{:S(2)}) copy-start(bf16[512,256]{1,0:T(8,128)(2,1)} %param.10) | copy-start | bytes 786436
  10.6 6.6 %collective-permute-start.1 = (bf16[1,272,256]{2,1,0:T(8,128)(2,1)S(1)}, bf16[1,272,256]{2,1,0:T(8,128)(2,1)S(1)}, u32[]{:S(2)}, u32[]{:S(2)}) collective-permute-start(bf16[1,272,256]{2,1,0:T(8,128)(2,1)S(1)} %fusion.11), channel_id=1, source_target_pairs={{0,8},{8,0},{16,24},{24,16},{32,40},{40,32},{48,56},{56,48},{64,72... | collective-permute-start | bytes 417800 | tf_op jit(solution)/shard_map/ppermute | solution.py:192
  13.2 9.4 %collective-permute-start.2 = (bf16[1,272,256]{2,1,0:T(8,128)(2,1)S(1)}, bf16[1,272,256]{2,1,0:T(8,128)(2,1)S(1)}, u32[]{:S(2)}, u32[]{:S(2)}) collective-permute-start(bf16[1,272,256]{2,1,0:T(8,128)(2,1)S(1)} %fusion.11), channel_id=1, source_target_pairs={{0,16},{8,24},{16,0},{24,8},{32,48},{40,56},{48,32},{56,40},{64,80... | collective-permute-start | bytes 417800 | tf_op jit(solution)/shard_map/ppermute | solution.py:192
  16.5 8.7 %collective-permute-start.3 = (bf16[1,272,256]{2,1,0:T(8,128)(2,1)S(1)}, bf16[1,272,256]{2,1,0:T(8,128)(2,1)S(1)}, u32[]{:S(2)}, u32[]{:S(2)}) collective-permute-start(bf16[1,272,256]{2,1,0:T(8,128)(2,1)S(1)} %fusion.11), channel_id=1, source_target_pairs={{0,24},{8,16},{16,8},{24,0},{32,56},{40,48},{48,40},{56,32},{64,88... | collective-permute-start | bytes 417800 | tf_op jit(solution)/shard_map/ppermute | solution.py:192
  25.8 14.8 %collective-permute-start.4 = (bf16[4,272,256]{2,1,0:T(8,128)(2,1)}, bf16[4,272,256]{2,1,0:T(8,128)(2,1)}, u32[]{:S(2)}, u32[]{:S(2)}) collective-permute-start(bf16[4,272,256]{2,1,0:T(8,128)(2,1)} %get-tuple-element.11), channel_id=1, source_target_pairs={{0,32},{8,40},{16,48},{24,56},{32,0},{40,8},{48,16},{56,24},{64,96... | collective-permute-start | bytes 1671176 | tf_op jit(solution)/shard_map/ppermute | solution.py:192
  28.6 24.0 %collective-permute-start.5 = (bf16[4,272,256]{2,1,0:T(8,128)(2,1)}, bf16[4,272,256]{2,1,0:T(8,128)(2,1)S(1)}, u32[]{:S(2)}, u32[]{:S(2)}) collective-permute-start(bf16[4,272,256]{2,1,0:T(8,128)(2,1)} %get-tuple-element.11), channel_id=1, source_target_pairs={{0,64},{8,72},{16,80},{24,88},{32,96},{40,104},{48,112},{56,120},{... | collective-permute-start | bytes 1671176 | tf_op jit(solution)/shard_map/ppermute | solution.py:192
  28.9 25.1 %collective-permute-start.6 = (bf16[4,272,256]{2,1,0:T(8,128)(2,1)}, bf16[4,272,256]{2,1,0:T(8,128)(2,1)S(1)}, u32[]{:S(2)}, u32[]{:S(2)}) collective-permute-start(bf16[4,272,256]{2,1,0:T(8,128)(2,1)} %get-tuple-element.11), channel_id=1, source_target_pairs={{0,96},{8,104},{16,112},{24,120},{32,64},{40,72},{48,80},{56,88},{... | collective-permute-start | bytes 1671176 | tf_op jit(solution)/shard_map/ppermute | solution.py:192
  32.6 25.5 %copy-start.3 = (s32[8,12]{1,0:T(8,128)S(1)}, s32[8,12]{1,0:T(8,128)}, u32[]{:S(2)}) copy-start(s32[8,12]{1,0:T(8,128)} %param.14) | copy-start | bytes 1156
  32.6 26.1 %copy-start.2 = (s32[2048]{0:T(1024)S(1)}, s32[2048]{0:T(1024)}, u32[]{:S(2)}) copy-start(s32[2048]{0:T(1024)} %tgt_ref.1) | copy-start | bytes 24580
  32.6 65.0 %collective-permute-start = (f32[2048,256]{1,0:T(8,128)}, f32[2048,256]{1,0:T(8,128)S(1)}, u32[]{:S(2)}, u32[]{:S(2)}) collective-permute-start(f32[2048,256]{1,0:T(8,128)} %dynamic-slice_bitcast_fusion), channel_id=1, source_target_pairs={{0,64},{64,0},{1,65},{65,1},{2,66},{66,2},{3,67},{67,3},{4,68},{68... | collective-permute-start | bytes 6291464 | tf_op jit(solution)/shard_map/ppermute | solution.py:199
  54.9 45.5 %collective-permute-start.7 = (bf16[16,272,256]{2,1,0:T(8,128)(2,1)}, bf16[16,272,256]{2,1,0:T(8,128)(2,1)}, u32[]{:S(2)}, u32[]{:S(2)}) collective-permute-start(bf16[16,272,256]{2,1,0:T(8,128)(2,1)} %constant_dynamic-update-slice_fusion.4.tab_a_ref), channel_id=1, source_target_pairs={{0,1},{1,0},{2,3},{3,2},{4,5},{5,4},{6,7},{7,6},{8,9},{9,8},{10,11... | collective-permute-start | bytes 6684680 | tf_op jit(solution)/shard_map/ppermute | solution.py:201
  151.5 25.0 %collective-permute-start.8 = (bf16[2048,256]{1,0:T(8,128)(2,1)}, bf16[2048,256]{1,0:T(8,128)(2,1)S(1)}, u32[]{:S(2)}, u32[]{:S(2)}) collective-permute-start(bf16[2048,256]{1,0:T(8,128)(2,1)} %get-tuple-element.4), channel_id=1, source_target_pairs={{0,64},{64,0},{1,65},{65,1},{2,66},{66,2},{3,67},{67,3},{4,68},{68... | collective-permute-start | bytes 3145736 | tf_op jit(solution)/shard_map/ppermute | solution.py:205

commit v5 on v3

--- a/solution.py
+++ b/solution.py
@@ -7,6 +7,7 @@
 from jax.experimental.pallas import tpu as pltpu
 from jax.sharding import PartitionSpec as P
 
+
 BLOCK = 256
 NEG_FILL = -1e30
 BIAS_ROWS = 16
@@ -16,7 +17,7 @@
 
 def score_kernel(list_width, n_blocks, dists,
                  lists_ref, lens_ref, tgt_ref, par_ref,
-                 q_ref, tcol_ref, tab_a_ref, tab_b_ref,
+                 qa_ref, qb_ref, tcol_ref, tab_a_ref, tab_b_ref,
                  qg_ref, loss_ref,
                  tabb_ref, tabf_ref, bias_ref, pos_ref, ls_ref, acc_ref, sem):
     b = pl.program_id(0)
@@ -29,6 +30,7 @@
             pltpu.make_async_copy(tabf_ref.at[pl.ds(t, 1), :], pos_ref.at[slot, pl.ds(r, 1), :],
                                   sem.at[slot]).start()
             return carry
+
         lax.fori_loop(0, BLOCK, one, 0, unroll=8)
 
     @pl.when(b == 0)
@@ -63,7 +65,7 @@
     def _():
         issue(b + 1, 1 - slot)
 
-    q = q_ref[...]
+    q = (qa_ref[...] + qb_ref[...]).astype(jnp.bfloat16)
     qf = q.astype(jnp.float32)
     tcol = tcol_ref[...]
     lane = lax.broadcasted_iota(jnp.int32, (BLOCK, BLOCK), 1)
@@ -118,8 +120,8 @@
     loss_ref[...] = log_total - pos_logit
 
 
-def score(queries, target_slot, block_lists, list_lens, tab_a, tab_b, parity, dists):
-    rows, embed = queries.shape
+def score(q_mine, q_sent, target_slot, block_lists, list_lens, tab_a, tab_b, parity, dists):
+    rows, embed = q_mine.shape
     n_blocks = rows // BLOCK
     n_shards = tab_a.shape[0]
     n_cands = 2 * n_shards * BLOCK
@@ -129,6 +131,7 @@
         grid=(n_blocks,),
         in_specs=[
             pl.BlockSpec((BLOCK, embed), lambda b, *_: (b, 0)),
+            pl.BlockSpec((BLOCK, embed), lambda b, *_: (b, 0)),
             pl.BlockSpec((BLOCK, 1), lambda b, *_: (b, 0)),
             pl.BlockSpec(memory_space=pltpu.VMEM),
             pl.BlockSpec(memory_space=pltpu.VMEM),
@@ -163,7 +166,7 @@
             flops=flops, transcendentals=2 * rows * BLOCK * 8,
             bytes_accessed=2 * tab_a.size * 2 + rows * embed * 4),
     )(block_lists.reshape(-1), list_lens, target_slot, parity,
-      queries, target_slot.reshape(rows, 1), tab_a, tab_b)
+      q_mine, q_sent, target_slot.reshape(rows, 1), tab_a, tab_b)
     return qg, loss.reshape(rows)
 
 
@@ -174,8 +177,6 @@
     sec = lax.axis_index("section")
     partner = [(i, i ^ 1) for i in range(n_sec)]
     partial = jnp.dot(flat_rows, w_proj, preferred_element_type=jnp.float32).reshape(halves, rows_dev, -1)
-    sent = lax.ppermute(lax.dynamic_index_in_dim(partial, 1 - sec, 0, keepdims=False), "section", partner)
-    queries = (lax.dynamic_index_in_dim(partial, sec, 0, keepdims=False) + sent).astype(jnp.bfloat16)
     n_pos = lax.axis_size("pos")
     core = lax.axis_index("pos") % 2
     n_own = lax.axis_size("owner")
@@ -185,20 +186,43 @@
     my_block = lax.dynamic_slice_in_dim(panels, core * BLOCK, BLOCK, axis=0)
     my_bias = jnp.pad(lax.dynamic_slice_in_dim(own_bias, core, 1, axis=0), ((0, BIAS_ROWS - 1), (0, 0)))
     buf = jnp.concatenate([my_block, my_bias], axis=0)[None]
+    partial, buf = lax.optimization_barrier((partial, buf))
     n_group = n_sec * n_own
+    steps = [4, 1] if n_group == 16 else []
     dists = []
-    d = n_group // 2
-    while d >= 1:
-        dists.append(d)
-        d //= 2
-    for d in dists:
-        got = lax.ppermute(buf, ("section", "owner"), [(i, i ^ d) for i in range(n_group)])
-        buf = jnp.concatenate([buf, got], axis=0)
+    if steps:
+        for step in steps:
+            got = [lax.ppermute(buf, ("section", "owner"), [(i, i ^ (m * step)) for i in range(n_group)])
+                   for m in range(1, 4)]
+            buf = jnp.concatenate([buf] + got, axis=0)
+            dists += [step, 2 * step]
+    else:
+        d = n_group // 2
+        while d >= 1:
+            got = lax.ppermute(buf, ("section", "owner"), [(i, i ^ d) for i in range(n_group)])
+            buf = jnp.concatenate([buf, got], axis=0)
+            dists.append(d)
+            d //= 2
     tab_b = lax.ppermute(buf, "pos", [(i, i ^ 1) for i in range(n_pos)])
     parity = jnp.stack([core, me]).astype(jnp.int32)
-    query_grad, position_loss = score(queries, target_slot, block_lists, list_lens, buf, tab_b, parity,
-                                      tuple(dists))
-    other_grad = lax.ppermute(query_grad, "section", partner)
+    mine = lax.dynamic_index_in_dim(partial, sec, 0, keepdims=False)
+    theirs = lax.dynamic_index_in_dim(partial, 1 - sec, 0, keepdims=False)
+    n_chunks = 2
+    rows_chunk = rows_dev // n_chunks
+    blocks_chunk = rows_chunk // BLOCK
+    grads, losses, others = [], [], []
+    for c in range(n_chunks):
+        rows = slice(c * rows_chunk, (c + 1) * rows_chunk)
+        blocks = slice(c * blocks_chunk, (c + 1) * blocks_chunk)
+        sent = lax.ppermute(theirs[rows], "section", partner)
+        grad, loss = score(mine[rows], sent, target_slot[rows], block_lists[blocks], list_lens[blocks], buf, tab_b,
+                           parity, tuple(dists))
+        grads.append(grad)
+        losses.append(loss)
+        others.append(lax.ppermute(grad, "section", partner))
+    query_grad = jnp.concatenate(grads, axis=0)
+    other_grad = jnp.concatenate(others, axis=0)
+    position_loss = jnp.concatenate(losses, axis=0)
     both = jnp.where(sec == 0, jnp.concatenate([query_grad, other_grad], axis=0),
                      jnp.concatenate([other_grad, query_grad], axis=0))
     trunk_grad = lax.dot_general(

time: 168 us -> 164 us (0.976)
  the two profiles are of different devices: /device:TPU:88 before, /device:TPU:31 now
where the time goes in v5:
time: 164 us
  waiting for transfers between devices  57.8 us (35%)
  Pallas kernels  55.8 us (34%)
  local copies, waits for them, and re-layouts  16.9 us (10%)
  starting transfers between devices  13.7 us (8%)
  matrix products  13.1 us (8%)
  other arithmetic  5.54 us (3%)
    pallas_call x2, Pallas kernels, score(): pl.pallas_call(functools.partial(score_kernel, list_width, n_blocks, dist...  55.8 us
    ppermute x6, waiting for transfers between devices, shards(): lax.ppermute(buf, ('section', 'owner'), [(i, i ^ m * step) for i in range...  29.2 us
    ppermute x2, waiting for transfers between devices, shards(): sent = lax.ppermute(theirs[rows], 'section', partner)  18.7 us
    ppermute x2, waiting for transfers between devices, shards(): others.append(lax.ppermute(grad, 'section', partner))  9.9 us
    ppermute x6, starting transfers between devices, shards(): lax.ppermute(buf, ('section', 'owner'), [(i, i ^ m * step) for i in range...  8.29 us
    dot_general x1, matrix products, shards(): lax.dot_general(both, w_proj, (((1,), (1,)), ((), ())), preferred_element...  7.65 us
    dot_general x1, matrix products, shards(): jnp.dot(flat_rows, w_proj, preferred_element_type=jnp.float32)  5.49 us
    slice x1, local copies, waits for them, and re-layouts, shards(): sent = lax.ppermute(theirs[rows], 'section', partner)  3.95 us
  transfers between devices with their start and end apart: 11, of which 8 were waited for; matrix products, arithmetic and copies ran while one was open for 10% of the time, Pallas kernels for 34%

profile of v5, /device:TPU:31, one launch (start us, length us, event | category | flops | bytes accessed | tf_op | source)
XLA Modules:
  0.0 163.6 jit_solution(10859402053515326049)
XLA Ops:
  0.7 0.7 compare_select_fusion
  1.4 3.6 %gather_fusion = s32[512]{0:T(512)S(1)} fusion(s32[65536]{0:T(1024)} %param.12, s32[1024]{0:T(1024)S(1)} %pad_clamp_fusion), kind=kCustom, calls=%fused_computation | custom fusion | bytes 6144 | tf_op jit(solution)/shard_map/gather | solution.py:184
  5.1 5.5 %fusion.15 = f32[2,2048,256]{2,1,0:T(8,128)} fusion(bf16[2,2048,512]{2,1,0:T(8,128)(2,1)} %param.8, bf16[512,256]{1,0:T(8,128)(2,1)S(1)} %copy-done), kind=kOutput, calls=%fused_computation.24 | convolution fusion | flops 1073741824 | bytes 8650752 | tf_op jit(solution)/shard_map/dot_general | solution.py:179
  10.6 1.2 collective-permute-start.1
  11.8 2.1 %collective-permute-start.3 = (bf16[1,272,256]{2,1,0:T(8,128)(2,1)S(1)}, bf16[1,272,256]{2,1,0:T(8,128)(2,1)S(1)}, u32[]{:S(2)}, u32[]{:S(2)}) collective-permute-start(bf16[1,272,256]{2,1,0:T(8,128)(2,1)S(1)} %fusion.18), channel_id=1, source_target_pairs={{0,96},{8,104},{16,112},{24,120},{32,64},{40,72},{48,80},{56,88},{... | collective-permute-start | bytes 417800 | tf_op jit(solution)/shard_map/ppermute | solution.py:195
  14.0 0.7 constant_dynamic-update-slice_fusion.3
  14.6 2.1 %collective-permute-done.1 = bf16[1,272,256]{2,1,0:T(8,128)(2,1)S(1)} collective-permute-done((bf16[1,272,256]{2,1,0:T(8,128)(2,1)S(1)}, bf16[1,272,256]{2,1,0:T(8,128)(2,1)S(1)}, u32[]{:S(2)}, u32[]{:S(2)}) %collective-permute-start.1) | collective-permute-done | bytes 139296 | tf_op jit(solution)/shard_map/ppermute | solution.py:195
  16.8 0.7 constant_dynamic-update-slice_fusion.2
  17.6 0.7 constant_dynamic-update-slice_fusion.1
  18.2 2.4 %collective-permute-done.3 = bf16[1,272,256]{2,1,0:T(8,128)(2,1)S(1)} collective-permute-done((bf16[1,272,256]{2,1,0:T(8,128)(2,1)S(1)}, bf16[1,272,256]{2,1,0:T(8,128)(2,1)S(1)}, u32[]{:S(2)}, u32[]{:S(2)}) %collective-permute-start.3) | collective-permute-done | bytes 139296 | tf_op jit(solution)/shard_map/ppermute | solution.py:195
  20.7 0.7 constant_dynamic-update-slice_fusion
  21.4 1.7 %collective-permute-start.4 = (bf16[4,272,256]{2,1,0:T(8,128)(2,1)S(1)}, bf16[4,272,256]{2,1,0:T(8,128)(2,1)S(1)}, u32[]{:S(2)}, u32[]{:S(2)}) collective-permute-start(bf16[4,272,256]{2,1,0:T(8,128)(2,1)S(1)} %get-tuple-element.19), channel_id=1, source_target_pairs={{0,8},{8,0},{16,24},{24,16},{32,40},{40,32},{48,56},{56,48},{64,72... | collective-permute-start | bytes 1671176 | tf_op jit(solution)/shard_map/ppermute | solution.py:195
  23.0 3.3 %collective-permute-start.5 = (bf16[4,272,256]{2,1,0:T(8,128)(2,1)S(1)}, bf16[4,272,256]{2,1,0:T(8,128)(2,1)S(1)}, u32[]{:S(2)}, u32[]{:S(2)}) collective-permute-start(bf16[4,272,256]{2,1,0:T(8,128)(2,1)S(1)} %get-tuple-element.19), channel_id=1, source_target_pairs={{0,16},{8,24},{16,0},{24,8},{32,48},{40,56},{48,32},{56,40},{64,80... | collective-permute-start | bytes 1671176 | tf_op jit(solution)/shard_map/ppermute | solution.py:195
  26.3 9.0 %collective-permute-done.4 = bf16[4,272,256]{2,1,0:T(8,128)(2,1)S(1)} collective-permute-done((bf16[4,272,256]{2,1,0:T(8,128)(2,1)S(1)}, bf16[4,272,256]{2,1,0:T(8,128)(2,1)S(1)}, u32[]{:S(2)}, u32[]{:S(2)}) %collective-permute-start.4) | collective-permute-done | bytes 557088 | tf_op jit(solution)/shard_map/ppermute | solution.py:195
  35.3 0.8 constant_dynamic-update-slice_fusion.6
  36.2 14.3 %collective-permute-done.5 = bf16[4,272,256]{2,1,0:T(8,128)(2,1)S(1)} collective-permute-done((bf16[4,272,256]{2,1,0:T(8,128)(2,1)S(1)}, bf16[4,272,256]{2,1,0:T(8,128)(2,1)S(1)}, u32[]{:S(2)}, u32[]{:S(2)}) %collective-permute-start.5) | collective-permute-done | bytes 557088 | tf_op jit(solution)/shard_map/ppermute | solution.py:195
  50.4 0.8 constant_dynamic-update-slice_fusion.5
  51.3 1.2 collective-permute-done.6
  52.5 0.9 constant_dynamic-update-slice_fusion.4.tab_a_ref
  53.3 2.0 %collective-permute-start.7 = (bf16[16,272,256]{2,1,0:T(8,128)(2,1)}, bf16[16,272,256]{2,1,0:T(8,128)(2,1)}, u32[]{:S(2)}, u32[]{:S(2)}) collective-permute-start(bf16[16,272,256]{2,1,0:T(8,128)(2,1)} %constant_dynamic-update-slice_fusion.4.tab_a_ref), channel_id=1, source_target_pairs={{0,1},{1,0},{2,3},{3,2},{4,5},{5,4},{6,7},{7,6},{8,9},{9,8},{10,11... | collective-permute-start | bytes 6684680 | tf_op jit(solution)/shard_map/ppermute | solution.py:206
  55.4 4.0 %dynamic-slice_bitcast_fusion.2 = (f32[1024,256]{1,0:T(8,128)S(1)}, f32[1024,256]{1,0:T(8,128)}, f32[1024,256]{1,0:T(8,128)S(1)}, f32[1024,256]{1,0:T(8,128)}) fusion(f32[2,2048,256]{2,1,0:T(8,128)} %fusion.15, s32[]{:T(128)S(6)} %select_n.36, s32[]{:T(128)S(6)} %select_n.35, s32[]{:T(128)S(6)} %add.40), kind=kLoop, calls=%fused_computation.19 | loop fusion | bytes 8388620 | tf_op jit(solution)/shard_map/slice | solution.py:217
  59.9 0.9 collective-permute-start
  61.5 1.0 copy.12.tcol_ref
  63.1 1.1 copy.11.tcol_ref
  65.4 18.7 %collective-permute-done.8.qb_ref = f32[1024,256]{1,0:T(8,128)} collective-permute-done((f32[1024,256]{1,0:T(8,128)S(1)}, f32[1024,256]{1,0:T(8,128)}, u32[]{:S(2)}, u32[]{:S(2)}) %collective-permute-start.8) | collective-permute-done | bytes 1048608 | tf_op jit(solution)/shard_map/ppermute | solution.py:217
  84.1 26.3 %shard_map.104 = (bf16[1024,256]{1,0:T(8,128)(2,1)}, f32[1024,1]{1,0:T(8,128)}) custom-call(s32[48]{0:T(128)} %reshape.42.lists_ref, s32[4]{0:T(128)} %get-tuple-element.32.lens_ref, s32[1024]{0:T(1024)} %copy-done.6, s32[2]{0:T(128)} %pad_add_fusion.par_ref, f32[1024,256]{1,0:T(8,128)} %get-tuple-element.18.qa_ref, ...), custom_call_target="tpu_custom_call" | custom-call | flops 2147483648 | bytes 5505024 | tf_op jit(solution)/shard_map/pallas_call | solution.py:154
  110.4 1.8 %collective-permute-start.10 = (bf16[1024,256]{1,0:T(8,128)(2,1)}, bf16[1024,256]{1,0:T(8,128)(2,1)S(1)}, u32[]{:S(2)}, u32[]{:S(2)}) collective-permute-start(bf16[1024,256]{1,0:T(8,128)(2,1)} %get-tuple-element.12), channel_id=1, source_target_pairs={{0,64},{64,0},{1,65},{65,1},{2,66},{66,2},{3,67},{67,3},{4,68},{68... | collective-permute-start | bytes 1572872 | tf_op jit(solution)/shard_map/ppermute | solution.py:222
  112.3 29.5 %shard_map.103 = (bf16[1024,256]{1,0:T(8,128)(2,1)}, f32[1024,1]{1,0:T(8,128)}) custom-call(s32[48]{0:T(128)} %reshape.40.lists_ref, s32[4]{0:T(128)} %get-tuple-element.31.lens_ref, s32[1024]{0:T(1024)} %copy-done.5, s32[2]{0:T(128)} %pad_add_fusion.par_ref, f32[1024,256]{1,0:T(8,128)} %get-tuple-element.16.qa_ref, ...), custom_call_target="tpu_custom_call" | custom-call | flops 2147483648 | bytes 5505024 | tf_op jit(solution)/shard_map/pallas_call | solution.py:154
  142.1 1.2 reduce
  144.0 2.1 %pad_maximum_fusion = bf16[2048,256]{1,0:T(8,128)(2,1)} fusion(bf16[1024,256]{1,0:T(8,128)(2,1)S(1)} %copy-done.2, bf16[1024,256]{1,0:T(8,128)(2,1)} %get-tuple-element.11), kind=kLoop, calls=%fused_computation.21 | loop fusion | flops 2097152 | bytes 2097152 | tf_op jit(solution)/shard_map/concatenate | solution.py:223
  146.1 9.9 %collective-permute-done.9 = bf16[1024,256]{1,0:T(8,128)(2,1)S(1)} collective-permute-done((bf16[1024,256]{1,0:T(8,128)(2,1)}, bf16[1024,256]{1,0:T(8,128)(2,1)S(1)}, u32[]{:S(2)}, u32[]{:S(2)}) %collective-permute-start.9) | collective-permute-done | bytes 524320 | tf_op jit(solution)/shard_map/ppermute | solution.py:222
  156.0 7.7 %convolution_convert_fusion = bf16[4096,512]{1,0:T(8,128)(2,1)} fusion(bf16[512,256]{1,0:T(8,128)(2,1)S(1)} %copy-done, bf16[1024,256]{1,0:T(8,128)(2,1)S(1)} %collective-permute-done.10, bf16[1024,256]{1,0:T(8,128)(2,1)S(1)} %collective-permute-done.9, bf16[1024,256]{1,0:T(8,128)(2,1)S(1)} %copy-done.2, bf16[1024,256]{1,0:T(8,128)(2,1)S(1)} %copy-done.3, ...), kind=kOutput, calls=%fused_computation.1 | convolution fusion | flops 1093664768 | bytes 6553601 | tf_op jit(solution)/shard_map/dot_general | solution.py:228
  (42 shorter events, 4.2 us)
Async XLA Ops:
  0.6 4.4 %copy-start = (bf16[512,256]{1,0:T(8,128)(2,1)S(1)}, bf16[512,256]{1,0:T(8,128)(2,1)}, u32[]{:S(2)}) copy-start(bf16[512,256]{1,0:T(8,128)(2,1)} %param.9) | copy-start | bytes 786436
  5.1 5.5 %copy-start.4 = (bf16[512,256]{1,0:T(8,128)(2,1)S(1)}, bf16[512,256]{1,0:T(8,128)(2,1)}, u32[]{:S(2)}) copy-start(bf16[512,256]{1,0:T(8,128)(2,1)} %param.10) | copy-start | bytes 786436
  10.6 6.1 %collective-permute-start.1 = (bf16[1,272,256]{2,1,0:T(8,128)(2,1)S(1)}, bf16[1,272,256]{2,1,0:T(8,128)(2,1)S(1)}, u32[]{:S(2)}, u32[]{:S(2)}) collective-permute-start(bf16[1,272,256]{2,1,0:T(8,128)(2,1)S(1)} %fusion.18), channel_id=1, source_target_pairs={{0,32},{8,40},{16,48},{24,56},{32,0},{40,8},{48,16},{56,24},{64,96... | collective-permute-start | bytes 417800 | tf_op jit(solution)/shard_map/ppermute | solution.py:195
  11.8 5.7 %collective-permute-start.2 = (bf16[1,272,256]{2,1,0:T(8,128)(2,1)S(1)}, bf16[1,272,256]{2,1,0:T(8,128)(2,1)S(1)}, u32[]{:S(2)}, u32[]{:S(2)}) collective-permute-start(bf16[1,272,256]{2,1,0:T(8,128)(2,1)S(1)} %fusion.18), channel_id=1, source_target_pairs={{0,64},{8,72},{16,80},{24,88},{32,96},{40,104},{48,112},{56,120},{... | collective-permute-start | bytes 417800 | tf_op jit(solution)/shard_map/ppermute | solution.py:195
  11.8 8.8 %collective-permute-start.3 = (bf16[1,272,256]{2,1,0:T(8,128)(2,1)S(1)}, bf16[1,272,256]{2,1,0:T(8,128)(2,1)S(1)}, u32[]{:S(2)}, u32[]{:S(2)}) collective-permute-start(bf16[1,272,256]{2,1,0:T(8,128)(2,1)S(1)} %fusion.18), channel_id=1, source_target_pairs={{0,96},{8,104},{16,112},{24,120},{32,64},{40,72},{48,80},{56,88},{... | collective-permute-start | bytes 417800 | tf_op jit(solution)/shard_map/ppermute | solution.py:195
  21.4 14.0 %collective-permute-start.4 = (bf16[4,272,256]{2,1,0:T(8,128)(2,1)S(1)}, bf16[4,272,256]{2,1,0:T(8,128)(2,1)S(1)}, u32[]{:S(2)}, u32[]{:S(2)}) collective-permute-start(bf16[4,272,256]{2,1,0:T(8,128)(2,1)S(1)} %get-tuple-element.19), channel_id=1, source_target_pairs={{0,8},{8,0},{16,24},{24,16},{32,40},{40,32},{48,56},{56,48},{64,72... | collective-permute-start | bytes 1671176 | tf_op jit(solution)/shard_map/ppermute | solution.py:195
  23.0 27.4 %collective-permute-start.5 = (bf16[4,272,256]{2,1,0:T(8,128)(2,1)S(1)}, bf16[4,272,256]{2,1,0:T(8,128)(2,1)S(1)}, u32[]{:S(2)}, u32[]{:S(2)}) collective-permute-start(bf16[4,272,256]{2,1,0:T(8,128)(2,1)S(1)} %get-tuple-element.19), channel_id=1, source_target_pairs={{0,16},{8,24},{16,0},{24,8},{32,48},{40,56},{48,32},{56,40},{64,80... | collective-permute-start | bytes 1671176 | tf_op jit(solution)/shard_map/ppermute | solution.py:195
  26.3 26.2 %collective-permute-start.6 = (bf16[4,272,256]{2,1,0:T(8,128)(2,1)S(1)}, bf16[4,272,256]{2,1,0:T(8,128)(2,1)S(1)}, u32[]{:S(2)}, u32[]{:S(2)}) collective-permute-start(bf16[4,272,256]{2,1,0:T(8,128)(2,1)S(1)} %get-tuple-element.19), channel_id=1, source_target_pairs={{0,24},{8,16},{16,8},{24,0},{32,56},{40,48},{48,40},{56,32},{64,88... | collective-permute-start | bytes 1671176 | tf_op jit(solution)/shard_map/ppermute | solution.py:195
  53.3 30.8 %collective-permute-start.7 = (bf16[16,272,256]{2,1,0:T(8,128)(2,1)}, bf16[16,272,256]{2,1,0:T(8,128)(2,1)}, u32[]{:S(2)}, u32[]{:S(2)}) collective-permute-start(bf16[16,272,256]{2,1,0:T(8,128)(2,1)} %constant_dynamic-update-slice_fusion.4.tab_a_ref), channel_id=1, source_target_pairs={{0,1},{1,0},{2,3},{3,2},{4,5},{5,4},{6,7},{7,6},{8,9},{9,8},{10,11... | collective-permute-start | bytes 6684680 | tf_op jit(solution)/shard_map/ppermute | solution.py:206
  55.4 5.4 %copy-start.8 = (s32[8,12]{1,0:T(8,128)S(1)}, s32[8,12]{1,0:T(8,128)}, u32[]{:S(2)}) copy-start(s32[8,12]{1,0:T(8,128)} %param.14) | copy-start | bytes 1156
  55.4 6.1 %copy-start.7 = (s32[2048]{0:T(1024)S(1)}, s32[2048]{0:T(1024)}, u32[]{:S(2)}) copy-start(s32[2048]{0:T(1024)} %param.13) | copy-start | bytes 24580
  55.4 9.4 %copy-start.9 = (s32[8]{0:T(128)S(1)}, s32[8]{0:T(128)}, u32[]{:S(2)}) copy-start(s32[8]{0:T(128)} %param.15) | copy-start | bytes 100
  59.3 24.8 %collective-permute-start.8 = (f32[1024,256]{1,0:T(8,128)S(1)}, f32[1024,256]{1,0:T(8,128)}, u32[]{:S(2)}, u32[]{:S(2)}) collective-permute-start(f32[1024,256]{1,0:T(8,128)S(1)} %get-tuple-element.17), channel_id=1, source_target_pairs={{0,64},{64,0},{1,65},{65,1},{2,66},{66,2},{3,67},{67,3},{4,68},{68... | collective-permute-start | bytes 3145736 | tf_op jit(solution)/shard_map/ppermute | solution.py:217
  59.9 52.4 %collective-permute-start = (f32[1024,256]{1,0:T(8,128)S(1)}, f32[1024,256]{1,0:T(8,128)}, u32[]{:S(2)}, u32[]{:S(2)}) collective-permute-start(f32[1024,256]{1,0:T(8,128)S(1)} %get-tuple-element.15), channel_id=1, source_target_pairs={{0,64},{64,0},{1,65},{65,1},{2,66},{66,2},{3,67},{67,3},{4,68},{68... | collective-permute-start | bytes 3145736 | tf_op jit(solution)/shard_map/ppermute | solution.py:217
  61.4 22.7 %copy-start.6 = (s32[1024]{0:T(1024)}, s32[1024]{0:T(1024)S(1)}, u32[]{:S(2)}) copy-start(s32[1024]{0:T(1024)S(1)} %get-tuple-element.28.tgt_ref) | copy-start | bytes 12292
  61.4 49.0 %copy-start.5 = (s32[1024]{0:T(1024)}, s32[1024]{0:T(1024)S(1)}, u32[]{:S(2)}) copy-start(s32[1024]{0:T(1024)S(1)} %get-tuple-element.27.tgt_ref) | copy-start | bytes 12292
  110.4 35.6 %collective-permute-start.10 = (bf16[1024,256]{1,0:T(8,128)(2,1)}, bf16[1024,256]{1,0:T(8,128)(2,1)S(1)}, u32[]{:S(2)}, u32[]{:S(2)}) collective-permute-start(bf16[1024,256]{1,0:T(8,128)(2,1)} %get-tuple-element.12), channel_id=1, source_target_pairs={{0,64},{64,0},{1,65},{65,1},{2,66},{66,2},{3,67},{67,3},{4,68},{68... | collective-permute-start | bytes 1572872 | tf_op jit(solution)/shard_map/ppermute | solution.py:222
  112.3 29.6 %copy-start.1 = (f32[1024,1]{1,0:T(8,128)S(1)}, f32[1024,1]{1,0:T(8,128)}, u32[]{:S(2)}) copy-start(f32[1024,1]{1,0:T(8,128)} %get-tuple-element.14) | copy-start | bytes 12292
  112.3 31.7 %copy-start.2 = (bf16[1024,256]{1,0:T(8,128)(2,1)S(1)}, bf16[1024,256]{1,0:T(8,128)(2,1)}, u32[]{:S(2)}) copy-start(bf16[1024,256]{1,0:T(8,128)(2,1)} %get-tuple-element.12) | copy-start | bytes 1572868
  141.8 14.2 %copy-start.3 = (bf16[1024,256]{1,0:T(8,128)(2,1)S(1)}, bf16[1024,256]{1,0:T(8,128)(2,1)}, u32[]{:S(2)}) copy-start(bf16[1024,256]{1,0:T(8,128)(2,1)} %get-tuple-element.11) | copy-start | bytes 1572868
  141.8 14.2 %collective-permute-start.9 = (bf16[1024,256]{1,0:T(8,128)(2,1)}, bf16[1024,256]{1,0:T(8,128)(2,1)S(1)}, u32[]{:S(2)}, u32[]{:S(2)}) collective-permute-start(bf16[1024,256]{1,0:T(8,128)(2,1)} %get-tuple-element.11), channel_id=1, source_target_pairs={{0,64},{64,0},{1,65},{65,1},{2,66},{66,2},{3,67},{67,3},{4,68},{68... | collective-permute-start | bytes 1572872 | tf_op jit(solution)/shard_map/ppermute | solution.py:222

commit v6 on v5

--- a/solution.py
+++ b/solution.py
@@ -188,21 +188,13 @@
     buf = jnp.concatenate([my_block, my_bias], axis=0)[None]
     partial, buf = lax.optimization_barrier((partial, buf))
     n_group = n_sec * n_own
-    steps = [4, 1] if n_group == 16 else []
     dists = []
-    if steps:
-        for step in steps:
-            got = [lax.ppermute(buf, ("section", "owner"), [(i, i ^ (m * step)) for i in range(n_group)])
-                   for m in range(1, 4)]
-            buf = jnp.concatenate([buf] + got, axis=0)
-            dists += [step, 2 * step]
-    else:
-        d = n_group // 2
-        while d >= 1:
-            got = lax.ppermute(buf, ("section", "owner"), [(i, i ^ d) for i in range(n_group)])
-            buf = jnp.concatenate([buf, got], axis=0)
-            dists.append(d)
-            d //= 2
+    d = n_group // 2
+    while d >= 1:
+        got = lax.ppermute(buf, ("section", "owner"), [(i, i ^ d) for i in range(n_group)])
+        buf = jnp.concatenate([buf, got], axis=0)
+        dists.append(d)
+        d //= 2
     tab_b = lax.ppermute(buf, "pos", [(i, i ^ 1) for i in range(n_pos)])
     parity = jnp.stack([core, me]).astype(jnp.int32)
     mine = lax.dynamic_index_in_dim(partial, sec, 0, keepdims=False)

time: 164 us -> 176 us (1.073)
  the two profiles are of different devices: /device:TPU:31 before, /device:TPU:61 now
where the time goes in v6:
time: 176 us
  waiting for transfers between devices  69.6 us (40%)
  Pallas kernels  56.8 us (32%)
  local copies, waits for them, and re-layouts  15.6 us (9%)
  starting transfers between devices  14.4 us (8%)
  matrix products  13.1 us (7%)
  other arithmetic  5.68 us (3%)
    pallas_call x2, Pallas kernels, score(): pl.pallas_call(functools.partial(score_kernel, list_width, n_blocks, dist...  56.8 us
    ppermute x4, waiting for transfers between devices, shards(): lax.ppermute(buf, ('section', 'owner'), [(i, i ^ d) for i in range(n_grou...  42.2 us
    ppermute x2, waiting for transfers between devices, shards(): sent = lax.ppermute(theirs[rows], 'section', partner)  18.7 us
    ppermute x2, waiting for transfers between devices, shards(): others.append(lax.ppermute(grad, 'section', partner))  8.68 us
    dot_general x1, matrix products, shards(): lax.dot_general(both, w_proj, (((1,), (1,)), ((), ())), preferred_element...  7.65 us
    dot_general x1, matrix products, shards(): jnp.dot(flat_rows, w_proj, preferred_element_type=jnp.float32)  5.49 us
    ppermute x4, starting transfers between devices, shards(): lax.ppermute(buf, ('section', 'owner'), [(i, i ^ d) for i in range(n_grou...  4.98 us
    ppermute x2, starting transfers between devices, shards(): others.append(lax.ppermute(grad, 'section', partner))  4.33 us
  transfers between devices with their start and end apart: 9, of which 6 were waited for; matrix products, arithmetic and copies ran while one was open for 9% of the time, Pallas kernels for 32%

profile of v6, /device:TPU:61, one launch (start us, length us, event | category | flops | bytes accessed | tf_op | source)
XLA Modules:
  0.0 176.1 jit_solution(8891157683784636183)
XLA Ops:
  0.7 0.7 compare_select_fusion
  1.4 3.6 %gather_fusion = s32[512]{0:T(512)S(1)} fusion(s32[65536]{0:T(1024)} %param.12, s32[1024]{0:T(1024)S(1)} %pad_clamp_fusion), kind=kCustom, calls=%fused_computation | custom fusion | bytes 6144 | tf_op jit(solution)/shard_map/gather | solution.py:184
  5.1 5.5 %fusion.15 = f32[2,2048,256]{2,1,0:T(8,128)} fusion(bf16[2,2048,512]{2,1,0:T(8,128)(2,1)} %param.8, bf16[512,256]{1,0:T(8,128)(2,1)S(1)} %copy-done), kind=kOutput, calls=%fused_computation.27 | convolution fusion | flops 1073741824 | bytes 8650752 | tf_op jit(solution)/shard_map/dot_general | solution.py:179
  10.6 1.0 collective-permute-start.1
  11.6 3.6 %collective-permute-done.1 = bf16[1,272,256]{2,1,0:T(8,128)(2,1)S(1)} collective-permute-done((bf16[1,272,256]{2,1,0:T(8,128)(2,1)S(1)}, bf16[1,272,256]{2,1,0:T(8,128)(2,1)S(1)}, u32[]{:S(2)}, u32[]{:S(2)}) %collective-permute-start.1) | collective-permute-done | bytes 139296 | tf_op jit(solution)/shard_map/ppermute | solution.py:194
  15.6 7.9 %collective-permute-done.2 = bf16[2,272,256]{2,1,0:T(8,128)(2,1)S(1)} collective-permute-done((bf16[2,272,256]{2,1,0:T(8,128)(2,1)S(1)}, bf16[2,272,256]{2,1,0:T(8,128)(2,1)S(1)}, u32[]{:S(2)}, u32[]{:S(2)}) %collective-permute-start.2) | collective-permute-done | bytes 278560 | tf_op jit(solution)/shard_map/ppermute | solution.py:194
  23.6 2.8 %collective-permute-start.3 = (bf16[4,272,256]{2,1,0:T(8,128)(2,1)S(1)}, bf16[4,272,256]{2,1,0:T(8,128)(2,1)S(1)}, u32[]{:S(2)}, u32[]{:S(2)}) collective-permute-start(bf16[4,272,256]{2,1,0:T(8,128)(2,1)S(1)} %pad_maximum_fusion.2), channel_id=1, source_target_pairs={{0,16},{8,24},{16,0},{24,8},{32,48},{40,56},{48,32},{56,40},{64,80... | collective-permute-start | bytes 1671176 | tf_op jit(solution)/shard_map/ppermute | solution.py:194
  26.4 10.6 %collective-permute-done.3 = bf16[4,272,256]{2,1,0:T(8,128)(2,1)S(1)} collective-permute-done((bf16[4,272,256]{2,1,0:T(8,128)(2,1)S(1)}, bf16[4,272,256]{2,1,0:T(8,128)(2,1)S(1)}, u32[]{:S(2)}, u32[]{:S(2)}) %collective-permute-start.3) | collective-permute-done | bytes 557088 | tf_op jit(solution)/shard_map/ppermute | solution.py:194
  37.1 0.9 collective-permute-start.4
  37.9 0.7 constant_dynamic-update-slice_fusion.4
  38.6 0.7 constant_dynamic-update-slice_fusion.3
  39.3 0.7 constant_dynamic-update-slice_fusion.2
  40.0 0.8 constant_dynamic-update-slice_fusion.1
  40.8 20.1 %collective-permute-done.4 = bf16[8,272,256]{2,1,0:T(8,128)(2,1)S(1)} collective-permute-done((bf16[8,272,256]{2,1,0:T(8,128)(2,1)S(1)}, bf16[8,272,256]{2,1,0:T(8,128)(2,1)S(1)}, u32[]{:S(2)}, u32[]{:S(2)}) %collective-permute-start.4) | collective-permute-done | bytes 1114144 | tf_op jit(solution)/shard_map/ppermute | solution.py:194
  60.9 1.1 constant_dynamic-update-slice_fusion.tab_a_ref
  62.0 3.7 %collective-permute-start.5 = (bf16[16,272,256]{2,1,0:T(8,128)(2,1)}, bf16[16,272,256]{2,1,0:T(8,128)(2,1)}, u32[]{:S(2)}, u32[]{:S(2)}) collective-permute-start(bf16[16,272,256]{2,1,0:T(8,128)(2,1)} %constant_dynamic-update-slice_fusion.tab_a_ref), channel_id=1, source_target_pairs={{0,1},{1,0},{2,3},{3,2},{4,5},{5,4},{6,7},{7,6},{8,9},{9,8},{10,11... | collective-permute-start | bytes 6684680 | tf_op jit(solution)/shard_map/ppermute | solution.py:198
  65.7 3.9 %dynamic-slice_bitcast_fusion.2 = (f32[1024,256]{1,0:T(8,128)S(1)}, f32[1024,256]{1,0:T(8,128)}, f32[1024,256]{1,0:T(8,128)S(1)}, f32[1024,256]{1,0:T(8,128)}) fusion(f32[2,2048,256]{2,1,0:T(8,128)} %fusion.15, s32[]{:T(128)S(6)} %select_n.36, s32[]{:T(128)S(6)} %select_n.35, s32[]{:T(128)S(6)} %add.40), kind=kLoop, calls=%fused_computation.20 | loop fusion | bytes 8388620 | tf_op jit(solution)/shard_map/slice | solution.py:209
  69.6 0.9 collective-permute-start.6
  71.1 0.7 reshape.42.lists_ref
  71.8 1.0 copy.12.tcol_ref
  72.8 0.6 reshape.40.lists_ref
  73.4 1.1 copy.11.tcol_ref
  75.1 0.6 fusion.22
  75.7 18.7 %collective-permute-done.6.qb_ref = f32[1024,256]{1,0:T(8,128)} collective-permute-done((f32[1024,256]{1,0:T(8,128)S(1)}, f32[1024,256]{1,0:T(8,128)}, u32[]{:S(2)}, u32[]{:S(2)}) %collective-permute-start.6) | collective-permute-done | bytes 1048608 | tf_op jit(solution)/shard_map/ppermute | solution.py:209
  94.4 26.3 %shard_map.104 = (bf16[1024,256]{1,0:T(8,128)(2,1)}, f32[1024,1]{1,0:T(8,128)}) custom-call(s32[48]{0:T(128)} %reshape.42.lists_ref, s32[4]{0:T(128)} %get-tuple-element.24.lens_ref, s32[1024]{0:T(1024)} %copy-done.6, s32[2]{0:T(128)} %pad_add_fusion.par_ref, f32[1024,256]{1,0:T(8,128)} %get-tuple-element.18.qa_ref, ...), custom_call_target="tpu_custom_call" | custom-call | flops 2147483648 | bytes 5505024 | tf_op jit(solution)/shard_map/pallas_call | solution.py:154
  120.7 4.2 %collective-permute-start.8 = (bf16[1024,256]{1,0:T(8,128)(2,1)}, bf16[1024,256]{1,0:T(8,128)(2,1)S(1)}, u32[]{:S(2)}, u32[]{:S(2)}) collective-permute-start(bf16[1024,256]{1,0:T(8,128)(2,1)} %get-tuple-element.12), channel_id=1, source_target_pairs={{0,64},{64,0},{1,65},{65,1},{2,66},{66,2},{3,67},{67,3},{4,68},{68... | collective-permute-start | bytes 1572872 | tf_op jit(solution)/shard_map/ppermute | solution.py:214
  125.0 30.5 %shard_map.103 = (bf16[1024,256]{1,0:T(8,128)(2,1)}, f32[1024,1]{1,0:T(8,128)}) custom-call(s32[48]{0:T(128)} %reshape.40.lists_ref, s32[4]{0:T(128)} %get-tuple-element.23.lens_ref, s32[1024]{0:T(1024)} %copy-done.5, s32[2]{0:T(128)} %pad_add_fusion.par_ref, f32[1024,256]{1,0:T(8,128)} %get-tuple-element.16.qa_ref, ...), custom_call_target="tpu_custom_call" | custom-call | flops 2147483648 | bytes 5505024 | tf_op jit(solution)/shard_map/pallas_call | solution.py:154
  155.8 1.2 reduce
  157.1 0.6 pad_maximum_fusion.4
  157.7 2.1 %pad_maximum_fusion.1 = bf16[2048,256]{1,0:T(8,128)(2,1)} fusion(bf16[1024,256]{1,0:T(8,128)(2,1)S(1)} %copy-done.2, bf16[1024,256]{1,0:T(8,128)(2,1)} %get-tuple-element.11), kind=kLoop, calls=%fused_computation.22 | loop fusion | flops 2097152 | bytes 2097152 | tf_op jit(solution)/shard_map/concatenate | solution.py:215
  159.8 8.7 %collective-permute-done.7 = bf16[1024,256]{1,0:T(8,128)(2,1)S(1)} collective-permute-done((bf16[1024,256]{1,0:T(8,128)(2,1)}, bf16[1024,256]{1,0:T(8,128)(2,1)S(1)}, u32[]{:S(2)}, u32[]{:S(2)}) %collective-permute-start.7) | collective-permute-done | bytes 524320 | tf_op jit(solution)/shard_map/ppermute | solution.py:214
  168.4 7.7 %convolution_convert_fusion = bf16[4096,512]{1,0:T(8,128)(2,1)} fusion(bf16[512,256]{1,0:T(8,128)(2,1)S(1)} %copy-done, bf16[1024,256]{1,0:T(8,128)(2,1)S(1)} %collective-permute-done.8, bf16[1024,256]{1,0:T(8,128)(2,1)S(1)} %collective-permute-done.7, bf16[1024,256]{1,0:T(8,128)(2,1)S(1)} %copy-done.2, bf16[1024,256]{1,0:T(8,128)(2,1)S(1)} %copy-done.3, ...), kind=kOutput, calls=%fused_computation.1 | convolution fusion | flops 1093664768 | bytes 6553601 | tf_op jit(solution)/shard_map/dot_general | solution.py:220
  (39 shorter events, 2.1 us)
Async XLA Ops:
  0.6 4.4 %copy-start = (bf16[512,256]{1,0:T(8,128)(2,1)S(1)}, bf16[512,256]{1,0:T(8,128)(2,1)}, u32[]{:S(2)}) copy-start(bf16[512,256]{1,0:T(8,128)(2,1)} %param.9) | copy-start | bytes 786436
  5.1 5.5 %copy-start.4 = (bf16[512,256]{1,0:T(8,128)(2,1)S(1)}, bf16[512,256]{1,0:T(8,128)(2,1)}, u32[]{:S(2)}) copy-start(bf16[512,256]{1,0:T(8,128)(2,1)} %param.10) | copy-start | bytes 786436
  10.6 4.6 %collective-permute-start.1 = (bf16[1,272,256]{2,1,0:T(8,128)(2,1)S(1)}, bf16[1,272,256]{2,1,0:T(8,128)(2,1)S(1)}, u32[]{:S(2)}, u32[]{:S(2)}) collective-permute-start(bf16[1,272,256]{2,1,0:T(8,128)(2,1)S(1)} %fusion.18), channel_id=1, source_target_pairs={{0,64},{8,72},{16,80},{24,88},{32,96},{40,104},{48,112},{56,120},{... | collective-permute-start | bytes 417800 | tf_op jit(solution)/shard_map/ppermute | solution.py:194
  15.3 8.3 %collective-permute-start.2 = (bf16[2,272,256]{2,1,0:T(8,128)(2,1)S(1)}, bf16[2,272,256]{2,1,0:T(8,128)(2,1)S(1)}, u32[]{:S(2)}, u32[]{:S(2)}) collective-permute-start(bf16[2,272,256]{2,1,0:T(8,128)(2,1)S(1)} %pad_maximum_fusion.3), channel_id=1, source_target_pairs={{0,32},{8,40},{16,48},{24,56},{32,0},{40,8},{48,16},{56,24},{64,96... | collective-permute-start | bytes 835592 | tf_op jit(solution)/shard_map/ppermute | solution.py:194
  23.6 13.4 %collective-permute-start.3 = (bf16[4,272,256]{2,1,0:T(8,128)(2,1)S(1)}, bf16[4,272,256]{2,1,0:T(8,128)(2,1)S(1)}, u32[]{:S(2)}, u32[]{:S(2)}) collective-permute-start(bf16[4,272,256]{2,1,0:T(8,128)(2,1)S(1)} %pad_maximum_fusion.2), channel_id=1, source_target_pairs={{0,16},{8,24},{16,0},{24,8},{32,48},{40,56},{48,32},{56,40},{64,80... | collective-permute-start | bytes 1671176 | tf_op jit(solution)/shard_map/ppermute | solution.py:194
  37.1 23.8 %collective-permute-start.4 = (bf16[8,272,256]{2,1,0:T(8,128)(2,1)S(1)}, bf16[8,272,256]{2,1,0:T(8,128)(2,1)S(1)}, u32[]{:S(2)}, u32[]{:S(2)}) collective-permute-start(bf16[8,272,256]{2,1,0:T(8,128)(2,1)S(1)} %pad_maximum_fusion), channel_id=1, source_target_pairs={{0,8},{8,0},{16,24},{24,16},{32,40},{40,32},{48,56},{56,48},{64,72... | collective-permute-start | bytes 3342344 | tf_op jit(solution)/shard_map/ppermute | solution.py:194
  62.0 32.4 %collective-permute-start.5 = (bf16[16,272,256]{2,1,0:T(8,128)(2,1)}, bf16[16,272,256]{2,1,0:T(8,128)(2,1)}, u32[]{:S(2)}, u32[]{:S(2)}) collective-permute-start(bf16[16,272,256]{2,1,0:T(8,128)(2,1)} %constant_dynamic-update-slice_fusion.tab_a_ref), channel_id=1, source_target_pairs={{0,1},{1,0},{2,3},{3,2},{4,5},{5,4},{6,7},{7,6},{8,9},{9,8},{10,11... | collective-permute-start | bytes 6684680 | tf_op jit(solution)/shard_map/ppermute | solution.py:198
  65.7 5.4 %copy-start.8 = (s32[8,12]{1,0:T(8,128)S(1)}, s32[8,12]{1,0:T(8,128)}, u32[]{:S(2)}) copy-start(s32[8,12]{1,0:T(8,128)} %param.14) | copy-start | bytes 1156
  65.7 6.1 %copy-start.7 = (s32[2048]{0:T(1024)S(1)}, s32[2048]{0:T(1024)}, u32[]{:S(2)}) copy-start(s32[2048]{0:T(1024)} %param.13) | copy-start | bytes 24580
  65.7 9.4 %copy-start.9 = (s32[8]{0:T(128)S(1)}, s32[8]{0:T(128)}, u32[]{:S(2)}) copy-start(s32[8]{0:T(128)} %param.15) | copy-start | bytes 100
  69.6 24.8 %collective-permute-start.6 = (f32[1024,256]{1,0:T(8,128)S(1)}, f32[1024,256]{1,0:T(8,128)}, u32[]{:S(2)}, u32[]{:S(2)}) collective-permute-start(f32[1024,256]{1,0:T(8,128)S(1)} %get-tuple-element.17), channel_id=1, source_target_pairs={{0,64},{64,0},{1,65},{65,1},{2,66},{66,2},{3,67},{67,3},{4,68},{68... | collective-permute-start | bytes 3145736 | tf_op jit(solution)/shard_map/ppermute | solution.py:209
  70.5 54.5 %collective-permute-start = (f32[1024,256]{1,0:T(8,128)S(1)}, f32[1024,256]{1,0:T(8,128)}, u32[]{:S(2)}, u32[]{:S(2)}) collective-permute-start(f32[1024,256]{1,0:T(8,128)S(1)} %get-tuple-element.15), channel_id=1, source_target_pairs={{0,64},{64,0},{1,65},{65,1},{2,66},{66,2},{3,67},{67,3},{4,68},{68... | collective-permute-start | bytes 3145736 | tf_op jit(solution)/shard_map/ppermute | solution.py:209
  71.8 22.7 %copy-start.6 = (s32[1024]{0:T(1024)}, s32[1024]{0:T(1024)S(1)}, u32[]{:S(2)}) copy-start(s32[1024]{0:T(1024)S(1)} %get-tuple-element.20.tgt_ref) | copy-start | bytes 12292
  71.8 49.0 %copy-start.5 = (s32[1024]{0:T(1024)}, s32[1024]{0:T(1024)S(1)}, u32[]{:S(2)}) copy-start(s32[1024]{0:T(1024)S(1)} %get-tuple-element.19.tgt_ref) | copy-start | bytes 12292
  120.7 39.0 %collective-permute-start.8 = (bf16[1024,256]{1,0:T(8,128)(2,1)}, bf16[1024,256]{1,0:T(8,128)(2,1)S(1)}, u32[]{:S(2)}, u32[]{:S(2)}) collective-permute-start(bf16[1024,256]{1,0:T(8,128)(2,1)} %get-tuple-element.12), channel_id=1, source_target_pairs={{0,64},{64,0},{1,65},{65,1},{2,66},{66,2},{3,67},{67,3},{4,68},{68... | collective-permute-start | bytes 1572872 | tf_op jit(solution)/shard_map/ppermute | solution.py:214
  125.0 30.6 %copy-start.1 = (f32[1024,1]{1,0:T(8,128)S(1)}, f32[1024,1]{1,0:T(8,128)}, u32[]{:S(2)}) copy-start(f32[1024,1]{1,0:T(8,128)} %get-tuple-element.14) | copy-start | bytes 12292
  125.0 32.7 %copy-start.2 = (bf16[1024,256]{1,0:T(8,128)(2,1)S(1)}, bf16[1024,256]{1,0:T(8,128)(2,1)}, u32[]{:S(2)}) copy-start(bf16[1024,256]{1,0:T(8,128)(2,1)} %get-tuple-element.12) | copy-start | bytes 1572868
  155.5 13.0 %copy-start.3 = (bf16[1024,256]{1,0:T(8,128)(2,1)S(1)}, bf16[1024,256]{1,0:T(8,128)(2,1)}, u32[]{:S(2)}) copy-start(bf16[1024,256]{1,0:T(8,128)(2,1)} %get-tuple-element.11) | copy-start | bytes 1572868
  155.5 12.9 %collective-permute-start.7 = (bf16[1024,256]{1,0:T(8,128)(2,1)}, bf16[1024,256]{1,0:T(8,128)(2,1)S(1)}, u32[]{:S(2)}, u32[]{:S(2)}) collective-permute-start(bf16[1024,256]{1,0:T(8,128)(2,1)} %get-tuple-element.11), channel_id=1, source_target_pairs={{0,64},{64,0},{1,65},{65,1},{2,66},{66,2},{3,67},{67,3},{4,68},{68... | collective-permute-start | bytes 1572872 | tf_op jit(solution)/shard_map/ppermute | solution.py:214

commit v7 on v6

--- a/solution.py
+++ b/solution.py
@@ -15,7 +15,7 @@
 EXT = BLOCK + 128
 
 
-def score_kernel(list_width, n_blocks, dists,
+def score_kernel(list_width, n_blocks, aways,
                  lists_ref, lens_ref, tgt_ref, par_ref,
                  qa_ref, qb_ref, tcol_ref, tab_a_ref, tab_b_ref,
                  qg_ref, loss_ref,
@@ -38,10 +38,7 @@
         mine = par_ref[0]
         me = par_ref[1]
         for s in range(n_shards):
-            away = 0
-            for bit, d in enumerate(dists):
-                if (s >> bit) & 1:
-                    away ^= d
+            away = aways[s]
             for ref, par in ((tab_a_ref, mine), (tab_b_ref, 1 - mine)):
                 j = 2 * (me ^ away) + par
                 blk = ref[s, pl.ds(0, BLOCK), :]
@@ -120,7 +117,7 @@
     loss_ref[...] = log_total - pos_logit
 
 
-def score(q_mine, q_sent, target_slot, block_lists, list_lens, tab_a, tab_b, parity, dists):
+def score(q_mine, q_sent, target_slot, block_lists, list_lens, tab_a, tab_b, parity, aways):
     rows, embed = q_mine.shape
     n_blocks = rows // BLOCK
     n_shards = tab_a.shape[0]
@@ -152,7 +149,7 @@
     )
     flops = 2 * 2 * rows * embed * BLOCK * 8
     qg, loss = pl.pallas_call(
-        functools.partial(score_kernel, list_width, n_blocks, dists),
+        functools.partial(score_kernel, list_width, n_blocks, aways),
         grid_spec=grid_spec,
         out_shape=[
             jax.ShapeDtypeStruct((rows, embed), jnp.bfloat16),
@@ -188,13 +185,26 @@
     buf = jnp.concatenate([my_block, my_bias], axis=0)[None]
     partial, buf = lax.optimization_barrier((partial, buf))
     n_group = n_sec * n_own
-    dists = []
-    d = n_group // 2
-    while d >= 1:
-        got = lax.ppermute(buf, ("section", "owner"), [(i, i ^ d) for i in range(n_group)])
-        buf = jnp.concatenate([buf, got], axis=0)
-        dists.append(d)
-        d //= 2
+    group = ("section", "owner")
+
+    def swap(x, d):
+        return lax.ppermute(x, group, [(i, i ^ d) for i in range(n_group)])
+
+    if n_group == 16:
+        got = [swap(buf, 4 * m) for m in range(1, 4)]
+        buf = jnp.concatenate([buf] + got, axis=0)
+        g1, g3 = swap(buf, 1), swap(buf, 3)
+        h1, h2 = swap(g3[0:2], 1), swap(g1[2:4], 3)
+        buf = jnp.concatenate([buf, g1, g3, h1, h2], axis=0)
+        xs = [4 * k for k in range(4)]
+        aways = xs + [1 ^ a for a in xs] + [3 ^ a for a in xs] + [2 ^ a for a in xs]
+    else:
+        aways = [0]
+        d = n_group // 2
+        while d >= 1:
+            buf = jnp.concatenate([buf, swap(buf, d)], axis=0)
+            aways = aways + [d ^ a for a in aways]
+            d //= 2
     tab_b = lax.ppermute(buf, "pos", [(i, i ^ 1) for i in range(n_pos)])
     parity = jnp.stack([core, me]).astype(jnp.int32)
     mine = lax.dynamic_index_in_dim(partial, sec, 0, keepdims=False)
@@ -208,7 +218,7 @@
         blocks = slice(c * blocks_chunk, (c + 1) * blocks_chunk)
         sent = lax.ppermute(theirs[rows], "section", partner)
         grad, loss = score(mine[rows], sent, target_slot[rows], block_lists[blocks], list_lens[blocks], buf, tab_b,
-                           parity, tuple(dists))
+                           parity, tuple(aways))
         grads.append(grad)
         losses.append(loss)
         others.append(lax.ppermute(grad, "section", partner))

time: 176 us -> 158 us (0.90)
  waiting for transfers between devices: 69.6 us -> 45.4 us
  starting transfers between devices: 14.4 us -> 19 us
  local copies, waits for them, and re-layouts: 15.6 us -> 17.6 us
    ppermute x4 -> x7, waiting for transfers between devices: 42.2 us -> 18 us  [swap(): return lax.ppermute(x, group, [(i, i ^ d) for i in range(n_group)])]
    ppermute x4 -> x7, starting transfers between devices: 4.98 us -> 10.9 us  [swap(): return lax.ppermute(x, group, [(i, i ^ d) for i in range(n_group)])]
    unnamed x24 -> x26, local copies, waits for them, and re-layouts: 2.95 us -> 4.46 us
  transfers between devices with their start and end apart: 9 -> 12, of which waited for: 6 -> 8; matrix products, arithmetic and copies ran while one was open for 9% -> 11% of each run, Pallas kernels for 32% -> 36%
where the time goes in v7:
time: 158 us
  Pallas kernels  56.8 us (36%)
  waiting for transfers between devices  45.4 us (29%)
  starting transfers between devices  19 us (12%)
  local copies, waits for them, and re-layouts  17.6 us (11%)
  matrix products  13.1 us (8%)
  other arithmetic  5.49 us (3%)
    pallas_call x2, Pallas kernels, score(): pl.pallas_call(functools.partial(score_kernel, list_width, n_blocks, away...  56.8 us
    ppermute x2, waiting for transfers between devices, shards(): sent = lax.ppermute(theirs[rows], 'section', partner)  18.7 us
    ppermute x7, waiting for transfers between devices, swap(): return lax.ppermute(x, group, [(i, i ^ d) for i in range(n_group)])  18 us
    ppermute x7, starting transfers between devices, swap(): return lax.ppermute(x, group, [(i, i ^ d) for i in range(n_group)])  10.9 us
    ppermute x2, waiting for transfers between devices, shards(): others.append(lax.ppermute(grad, 'section', partner))  8.68 us
    dot_general x1, matrix products, shards(): lax.dot_general(both, w_proj, (((1,), (1,)), ((), ())), preferred_element...  7.65 us
    dot_general x1, matrix products, shards(): jnp.dot(flat_rows, w_proj, preferred_element_type=jnp.float32)  5.49 us
    unnamed x26, local copies, waits for them, and re-layouts  4.46 us
  transfers between devices with their start and end apart: 12, of which 8 were waited for; matrix products, arithmetic and copies ran while one was open for 11% of the time, Pallas kernels for 36%

profile of v7, /device:TPU:61, one launch (start us, length us, event | category | flops | bytes accessed | tf_op | source)
XLA Modules:
  0.0 158.2 jit_solution(17115544079870303261)
XLA Ops:
  0.7 0.7 compare_select_fusion
  1.4 3.6 %gather_fusion = s32[512]{0:T(512)S(1)} fusion(s32[65536]{0:T(1024)} %param.12, s32[1024]{0:T(1024)S(1)} %pad_clamp_fusion), kind=kCustom, calls=%fused_computation | custom fusion | bytes 6144 | tf_op jit(solution)/shard_map/gather | solution.py:181
  5.1 5.5 %fusion.15 = f32[2,2048,256]{2,1,0:T(8,128)} fusion(bf16[2,2048,512]{2,1,0:T(8,128)(2,1)} %param.8, bf16[512,256]{1,0:T(8,128)(2,1)S(1)} %copy-done), kind=kOutput, calls=%fused_computation.24 | convolution fusion | flops 1073741824 | bytes 8650752 | tf_op jit(solution)/shard_map/dot_general | solution.py:176
  10.9 1.8 %collective-permute-start.2 = (bf16[1,272,256]{2,1,0:T(8,128)(2,1)S(1)}, bf16[1,272,256]{2,1,0:T(8,128)(2,1)S(1)}, u32[]{:S(2)}, u32[]{:S(2)}) collective-permute-start(bf16[1,272,256]{2,1,0:T(8,128)(2,1)S(1)} %fusion.18), channel_id=1, source_target_pairs={{0,64},{8,72},{16,80},{24,88},{32,96},{40,104},{48,112},{56,120},{... | collective-permute-start | bytes 417800 | tf_op jit(solution)/shard_map/ppermute | solution.py:191
  12.8 1.2 collective-permute-start.3
  14.6 2.1 %collective-permute-done.1 = bf16[1,272,256]{2,1,0:T(8,128)(2,1)S(1)} collective-permute-done((bf16[1,272,256]{2,1,0:T(8,128)(2,1)S(1)}, bf16[1,272,256]{2,1,0:T(8,128)(2,1)S(1)}, u32[]{:S(2)}, u32[]{:S(2)}) %collective-permute-start.1) | collective-permute-done | bytes 139296 | tf_op jit(solution)/shard_map/ppermute | solution.py:191
  17.4 1.4 collective-permute-done.2
  19.5 1.2 collective-permute-done.3
  20.7 0.7 constant_dynamic-update-slice_fusion
  21.4 1.6 %collective-permute-start.5 = (bf16[4,272,256]{2,1,0:T(8,128)(2,1)S(1)}, bf16[4,272,256]{2,1,0:T(8,128)(2,1)S(1)}, u32[]{:S(2)}, u32[]{:S(2)}) collective-permute-start(bf16[4,272,256]{2,1,0:T(8,128)(2,1)S(1)} %get-tuple-element.19), channel_id=1, source_target_pairs={{0,24},{8,16},{16,8},{24,0},{32,56},{40,48},{48,40},{56,32},{64,88... | collective-permute-start | bytes 1671176 | tf_op jit(solution)/shard_map/ppermute | solution.py:191
  23.0 1.9 %collective-permute-start.4 = (bf16[4,272,256]{2,1,0:T(8,128)(2,1)S(1)}, bf16[4,272,256]{2,1,0:T(8,128)(2,1)S(1)}, u32[]{:S(2)}, u32[]{:S(2)}) collective-permute-start(bf16[4,272,256]{2,1,0:T(8,128)(2,1)S(1)} %get-tuple-element.19), channel_id=1, source_target_pairs={{0,8},{8,0},{16,24},{24,16},{32,40},{40,32},{48,56},{56,48},{64,72... | collective-permute-start | bytes 1671176 | tf_op jit(solution)/shard_map/ppermute | solution.py:191
  25.0 10.4 %collective-permute-done.5 = bf16[4,272,256]{2,1,0:T(8,128)(2,1)S(1)} collective-permute-done((bf16[4,272,256]{2,1,0:T(8,128)(2,1)S(1)}, bf16[4,272,256]{2,1,0:T(8,128)(2,1)S(1)}, u32[]{:S(2)}, u32[]{:S(2)}) %collective-permute-start.5) | collective-permute-done | bytes 557088 | tf_op jit(solution)/shard_map/ppermute | solution.py:191
  35.4 2.1 %collective-permute-start.6 = (bf16[2,272,256]{2,1,0:T(8,128)(2,1)S(1)}, bf16[2,272,256]{2,1,0:T(8,128)(2,1)S(1)}, u32[]{:S(2)}, u32[]{:S(2)}) collective-permute-start(bf16[2,272,256]{2,1,0:T(8,128)(2,1)S(1)} %slice.66), channel_id=1, source_target_pairs={{0,8},{8,0},{16,24},{24,16},{32,40},{40,32},{48,56},{56,48},{64,72... | collective-permute-start | bytes 835592 | tf_op jit(solution)/shard_map/ppermute | solution.py:191
  37.5 1.9 %collective-permute-start.7 = (bf16[2,272,256]{2,1,0:T(8,128)(2,1)S(1)}, bf16[2,272,256]{2,1,0:T(8,128)(2,1)S(1)}, u32[]{:S(2)}, u32[]{:S(2)}) collective-permute-start(bf16[2,272,256]{2,1,0:T(8,128)(2,1)S(1)} %slice.67), channel_id=1, source_target_pairs={{0,24},{8,16},{16,8},{24,0},{32,56},{40,48},{48,40},{56,32},{64,88... | collective-permute-start | bytes 835592 | tf_op jit(solution)/shard_map/ppermute | solution.py:191
  39.4 0.8 constant_dynamic-update-slice_fusion.7
  40.2 0.8 constant_dynamic-update-slice_fusion.6
  41.0 2.3 %collective-permute-done.6 = bf16[2,272,256]{2,1,0:T(8,128)(2,1)S(1)} collective-permute-done((bf16[2,272,256]{2,1,0:T(8,128)(2,1)S(1)}, bf16[2,272,256]{2,1,0:T(8,128)(2,1)S(1)}, u32[]{:S(2)}, u32[]{:S(2)}) %collective-permute-start.6) | collective-permute-done | bytes 278560 | tf_op jit(solution)/shard_map/ppermute | solution.py:191
  43.3 0.7 constant_dynamic-update-slice_fusion.5
  44.7 0.7 constant_dynamic-update-slice_fusion.4.tab_a_ref
  45.4 2.3 %collective-permute-start.8 = (bf16[16,272,256]{2,1,0:T(8,128)(2,1)}, bf16[16,272,256]{2,1,0:T(8,128)(2,1)}, u32[]{:S(2)}, u32[]{:S(2)}) collective-permute-start(bf16[16,272,256]{2,1,0:T(8,128)(2,1)} %constant_dynamic-update-slice_fusion.4.tab_a_ref), channel_id=1, source_target_pairs={{0,1},{1,0},{2,3},{3,2},{4,5},{5,4},{6,7},{7,6},{8,9},{9,8},{10,11... | collective-permute-start | bytes 6684680 | tf_op jit(solution)/shard_map/ppermute | solution.py:208
  47.7 4.0 %dynamic-slice_bitcast_fusion.2 = (f32[1024,256]{1,0:T(8,128)S(1)}, f32[1024,256]{1,0:T(8,128)}, f32[1024,256]{1,0:T(8,128)S(1)}, f32[1024,256]{1,0:T(8,128)}) fusion(f32[2,2048,256]{2,1,0:T(8,128)} %fusion.15, s32[]{:T(128)S(6)} %select_n.36, s32[]{:T(128)S(6)} %select_n.35, s32[]{:T(128)S(6)} %add.40), kind=kLoop, calls=%fused_computation.19 | loop fusion | bytes 8388620 | tf_op jit(solution)/shard_map/slice | solution.py:219
  51.7 0.9 collective-permute-start.9
  53.8 1.0 copy.12.tcol_ref
  55.5 1.1 copy.11.tcol_ref
  57.8 18.7 %collective-permute-done.9.qb_ref = f32[1024,256]{1,0:T(8,128)} collective-permute-done((f32[1024,256]{1,0:T(8,128)S(1)}, f32[1024,256]{1,0:T(8,128)}, u32[]{:S(2)}, u32[]{:S(2)}) %collective-permute-start.9) | collective-permute-done | bytes 1048608 | tf_op jit(solution)/shard_map/ppermute | solution.py:219
  76.5 26.3 %shard_map.104 = (bf16[1024,256]{1,0:T(8,128)(2,1)}, f32[1024,1]{1,0:T(8,128)}) custom-call(s32[48]{0:T(128)} %reshape.42.lists_ref, s32[4]{0:T(128)} %get-tuple-element.32.lens_ref, s32[1024]{0:T(1024)} %copy-done.6, s32[2]{0:T(128)} %pad_add_fusion.par_ref, f32[1024,256]{1,0:T(8,128)} %get-tuple-element.18.qa_ref, ...), custom_call_target="tpu_custom_call" | custom-call | flops 2147483648 | bytes 5505024 | tf_op jit(solution)/shard_map/pallas_call | solution.py:151
  102.8 4.2 %collective-permute-start.11 = (bf16[1024,256]{1,0:T(8,128)(2,1)}, bf16[1024,256]{1,0:T(8,128)(2,1)S(1)}, u32[]{:S(2)}, u32[]{:S(2)}) collective-permute-start(bf16[1024,256]{1,0:T(8,128)(2,1)} %get-tuple-element.12), channel_id=1, source_target_pairs={{0,64},{64,0},{1,65},{65,1},{2,66},{66,2},{3,67},{67,3},{4,68},{68... | collective-permute-start | bytes 1572872 | tf_op jit(solution)/shard_map/ppermute | solution.py:224
  107.0 30.5 %shard_map.103 = (bf16[1024,256]{1,0:T(8,128)(2,1)}, f32[1024,1]{1,0:T(8,128)}) custom-call(s32[48]{0:T(128)} %reshape.40.lists_ref, s32[4]{0:T(128)} %get-tuple-element.31.lens_ref, s32[1024]{0:T(1024)} %copy-done.5, s32[2]{0:T(128)} %pad_add_fusion.par_ref, f32[1024,256]{1,0:T(8,128)} %get-tuple-element.16.qa_ref, ...), custom_call_target="tpu_custom_call" | custom-call | flops 2147483648 | bytes 5505024 | tf_op jit(solution)/shard_map/pallas_call | solution.py:151
  137.9 1.2 reduce
  139.7 2.1 %pad_maximum_fusion = bf16[2048,256]{1,0:T(8,128)(2,1)} fusion(bf16[1024,256]{1,0:T(8,128)(2,1)S(1)} %copy-done.2, bf16[1024,256]{1,0:T(8,128)(2,1)} %get-tuple-element.11), kind=kLoop, calls=%fused_computation.21 | loop fusion | flops 2097152 | bytes 2097152 | tf_op jit(solution)/shard_map/concatenate | solution.py:225
  141.8 8.7 %collective-permute-done.10 = bf16[1024,256]{1,0:T(8,128)(2,1)S(1)} collective-permute-done((bf16[1024,256]{1,0:T(8,128)(2,1)}, bf16[1024,256]{1,0:T(8,128)(2,1)S(1)}, u32[]{:S(2)}, u32[]{:S(2)}) %collective-permute-start.10) | collective-permute-done | bytes 524320 | tf_op jit(solution)/shard_map/ppermute | solution.py:224
  150.5 7.7 %convolution_convert_fusion = bf16[4096,512]{1,0:T(8,128)(2,1)} fusion(bf16[512,256]{1,0:T(8,128)(2,1)S(1)} %copy-done, bf16[1024,256]{1,0:T(8,128)(2,1)S(1)} %collective-permute-done.11, bf16[1024,256]{1,0:T(8,128)(2,1)S(1)} %collective-permute-done.10, bf16[1024,256]{1,0:T(8,128)(2,1)S(1)} %copy-done.2, bf16[1024,256]{1,0:T(8,128)(2,1)S(1)} %copy-done.3, ...), kind=kOutput, calls=%fused_computation.1 | convolution fusion | flops 1093664768 | bytes 6553601 | tf_op jit(solution)/shard_map/dot_general | solution.py:230
  (47 shorter events, 7.1 us)
Async XLA Ops:
  0.6 4.4 %copy-start = (bf16[512,256]{1,0:T(8,128)(2,1)S(1)}, bf16[512,256]{1,0:T(8,128)(2,1)}, u32[]{:S(2)}) copy-start(bf16[512,256]{1,0:T(8,128)(2,1)} %param.9) | copy-start | bytes 786436
  5.1 5.5 %copy-start.4 = (bf16[512,256]{1,0:T(8,128)(2,1)S(1)}, bf16[512,256]{1,0:T(8,128)(2,1)}, u32[]{:S(2)}) copy-start(bf16[512,256]{1,0:T(8,128)(2,1)} %param.10) | copy-start | bytes 786436
  10.6 6.1 %collective-permute-start.1 = (bf16[1,272,256]{2,1,0:T(8,128)(2,1)S(1)}, bf16[1,272,256]{2,1,0:T(8,128)(2,1)S(1)}, u32[]{:S(2)}, u32[]{:S(2)}) collective-permute-start(bf16[1,272,256]{2,1,0:T(8,128)(2,1)S(1)} %fusion.18), channel_id=1, source_target_pairs={{0,32},{8,40},{16,48},{24,56},{32,0},{40,8},{48,16},{56,24},{64,96... | collective-permute-start | bytes 417800 | tf_op jit(solution)/shard_map/ppermute | solution.py:191
  10.9 7.9 %collective-permute-start.2 = (bf16[1,272,256]{2,1,0:T(8,128)(2,1)S(1)}, bf16[1,272,256]{2,1,0:T(8,128)(2,1)S(1)}, u32[]{:S(2)}, u32[]{:S(2)}) collective-permute-start(bf16[1,272,256]{2,1,0:T(8,128)(2,1)S(1)} %fusion.18), channel_id=1, source_target_pairs={{0,64},{8,72},{16,80},{24,88},{32,96},{40,104},{48,112},{56,120},{... | collective-permute-start | bytes 417800 | tf_op jit(solution)/shard_map/ppermute | solution.py:191
  12.8 7.9 %collective-permute-start.3 = (bf16[1,272,256]{2,1,0:T(8,128)(2,1)S(1)}, bf16[1,272,256]{2,1,0:T(8,128)(2,1)S(1)}, u32[]{:S(2)}, u32[]{:S(2)}) collective-permute-start(bf16[1,272,256]{2,1,0:T(8,128)(2,1)S(1)} %fusion.18), channel_id=1, source_target_pairs={{0,96},{8,104},{16,112},{24,120},{32,64},{40,72},{48,80},{56,88},{... | collective-permute-start | bytes 417800 | tf_op jit(solution)/shard_map/ppermute | solution.py:191
  21.4 14.0 %collective-permute-start.5 = (bf16[4,272,256]{2,1,0:T(8,128)(2,1)S(1)}, bf16[4,272,256]{2,1,0:T(8,128)(2,1)S(1)}, u32[]{:S(2)}, u32[]{:S(2)}) collective-permute-start(bf16[4,272,256]{2,1,0:T(8,128)(2,1)S(1)} %get-tuple-element.19), channel_id=1, source_target_pairs={{0,24},{8,16},{16,8},{24,0},{32,56},{40,48},{48,40},{56,32},{64,88... | collective-permute-start | bytes 1671176 | tf_op jit(solution)/shard_map/ppermute | solution.py:191
  23.0 14.5 %collective-permute-start.4 = (bf16[4,272,256]{2,1,0:T(8,128)(2,1)S(1)}, bf16[4,272,256]{2,1,0:T(8,128)(2,1)S(1)}, u32[]{:S(2)}, u32[]{:S(2)}) collective-permute-start(bf16[4,272,256]{2,1,0:T(8,128)(2,1)S(1)} %get-tuple-element.19), channel_id=1, source_target_pairs={{0,8},{8,0},{16,24},{24,16},{32,40},{40,32},{48,56},{56,48},{64,72... | collective-permute-start | bytes 1671176 | tf_op jit(solution)/shard_map/ppermute | solution.py:191
  35.4 8.0 %collective-permute-start.6 = (bf16[2,272,256]{2,1,0:T(8,128)(2,1)S(1)}, bf16[2,272,256]{2,1,0:T(8,128)(2,1)S(1)}, u32[]{:S(2)}, u32[]{:S(2)}) collective-permute-start(bf16[2,272,256]{2,1,0:T(8,128)(2,1)S(1)} %slice.66), channel_id=1, source_target_pairs={{0,8},{8,0},{16,24},{24,16},{32,40},{40,32},{48,56},{56,48},{64,72... | collective-permute-start | bytes 835592 | tf_op jit(solution)/shard_map/ppermute | solution.py:191
  37.5 7.2 %collective-permute-start.7 = (bf16[2,272,256]{2,1,0:T(8,128)(2,1)S(1)}, bf16[2,272,256]{2,1,0:T(8,128)(2,1)S(1)}, u32[]{:S(2)}, u32[]{:S(2)}) collective-permute-start(bf16[2,272,256]{2,1,0:T(8,128)(2,1)S(1)} %slice.67), channel_id=1, source_target_pairs={{0,24},{8,16},{16,8},{24,0},{32,56},{40,48},{48,40},{56,32},{64,88... | collective-permute-start | bytes 835592 | tf_op jit(solution)/shard_map/ppermute | solution.py:191
  45.4 31.1 %collective-permute-start.8 = (bf16[16,272,256]{2,1,0:T(8,128)(2,1)}, bf16[16,272,256]{2,1,0:T(8,128)(2,1)}, u32[]{:S(2)}, u32[]{:S(2)}) collective-permute-start(bf16[16,272,256]{2,1,0:T(8,128)(2,1)} %constant_dynamic-update-slice_fusion.4.tab_a_ref), channel_id=1, source_target_pairs={{0,1},{1,0},{2,3},{3,2},{4,5},{5,4},{6,7},{7,6},{8,9},{9,8},{10,11... | collective-permute-start | bytes 6684680 | tf_op jit(solution)/shard_map/ppermute | solution.py:208
  47.7 5.4 %copy-start.8 = (s32[8,12]{1,0:T(8,128)S(1)}, s32[8,12]{1,0:T(8,128)}, u32[]{:S(2)}) copy-start(s32[8,12]{1,0:T(8,128)} %param.14) | copy-start | bytes 1156
  47.7 6.1 %copy-start.7 = (s32[2048]{0:T(1024)S(1)}, s32[2048]{0:T(1024)}, u32[]{:S(2)}) copy-start(s32[2048]{0:T(1024)} %param.13) | copy-start | bytes 24580
  47.7 9.4 %copy-start.9 = (s32[8]{0:T(128)S(1)}, s32[8]{0:T(128)}, u32[]{:S(2)}) copy-start(s32[8]{0:T(128)} %param.15) | copy-start | bytes 100
  51.7 24.8 %collective-permute-start.9 = (f32[1024,256]{1,0:T(8,128)S(1)}, f32[1024,256]{1,0:T(8,128)}, u32[]{:S(2)}, u32[]{:S(2)}) collective-permute-start(f32[1024,256]{1,0:T(8,128)S(1)} %get-tuple-element.17), channel_id=1, source_target_pairs={{0,64},{64,0},{1,65},{65,1},{2,66},{66,2},{3,67},{67,3},{4,68},{68... | collective-permute-start | bytes 3145736 | tf_op jit(solution)/shard_map/ppermute | solution.py:219
  52.6 54.4 %collective-permute-start = (f32[1024,256]{1,0:T(8,128)S(1)}, f32[1024,256]{1,0:T(8,128)}, u32[]{:S(2)}, u32[]{:S(2)}) collective-permute-start(f32[1024,256]{1,0:T(8,128)S(1)} %get-tuple-element.15), channel_id=1, source_target_pairs={{0,64},{64,0},{1,65},{65,1},{2,66},{66,2},{3,67},{67,3},{4,68},{68... | collective-permute-start | bytes 3145736 | tf_op jit(solution)/shard_map/ppermute | solution.py:219
  53.8 22.7 %copy-start.6 = (s32[1024]{0:T(1024)}, s32[1024]{0:T(1024)S(1)}, u32[]{:S(2)}) copy-start(s32[1024]{0:T(1024)S(1)} %get-tuple-element.28.tgt_ref) | copy-start | bytes 12292
  53.8 49.0 %copy-start.5 = (s32[1024]{0:T(1024)}, s32[1024]{0:T(1024)S(1)}, u32[]{:S(2)}) copy-start(s32[1024]{0:T(1024)S(1)} %get-tuple-element.27.tgt_ref) | copy-start | bytes 12292
  102.8 39.0 %collective-permute-start.11 = (bf16[1024,256]{1,0:T(8,128)(2,1)}, bf16[1024,256]{1,0:T(8,128)(2,1)S(1)}, u32[]{:S(2)}, u32[]{:S(2)}) collective-permute-start(bf16[1024,256]{1,0:T(8,128)(2,1)} %get-tuple-element.12), channel_id=1, source_target_pairs={{0,64},{64,0},{1,65},{65,1},{2,66},{66,2},{3,67},{67,3},{4,68},{68... | collective-permute-start | bytes 1572872 | tf_op jit(solution)/shard_map/ppermute | solution.py:224
  107.0 30.6 %copy-start.1 = (f32[1024,1]{1,0:T(8,128)S(1)}, f32[1024,1]{1,0:T(8,128)}, u32[]{:S(2)}) copy-start(f32[1024,1]{1,0:T(8,128)} %get-tuple-element.14) | copy-start | bytes 12292
  107.0 32.7 %copy-start.2 = (bf16[1024,256]{1,0:T(8,128)(2,1)S(1)}, bf16[1024,256]{1,0:T(8,128)(2,1)}, u32[]{:S(2)}) copy-start(bf16[1024,256]{1,0:T(8,128)(2,1)} %get-tuple-element.12) | copy-start | bytes 1572868
  137.6 13.0 %copy-start.3 = (bf16[1024,256]{1,0:T(8,128)(2,1)S(1)}, bf16[1024,256]{1,0:T(8,128)(2,1)}, u32[]{:S(2)}) copy-start(bf16[1024,256]{1,0:T(8,128)(2,1)} %get-tuple-element.11) | copy-start | bytes 1572868
  137.6 12.9 %collective-permute-start.10 = (bf16[1024,256]{1,0:T(8,128)(2,1)}, bf16[1024,256]{1,0:T(8,128)(2,1)S(1)}, u32[]{:S(2)}, u32[]{:S(2)}) collective-permute-start(bf16[1024,256]{1,0:T(8,128)(2,1)} %get-tuple-element.11), channel_id=1, source_target_pairs={{0,64},{64,0},{1,65},{65,1},{2,66},{66,2},{3,67},{67,3},{4,68},{68... | collective-permute-start | bytes 1572872 | tf_op jit(solution)/shard_map/ppermute | solution.py:224

commit v8 on v7

--- a/solution.py
+++ b/solution.py
@@ -15,7 +15,16 @@
 EXT = BLOCK + 128
 
 
-def score_kernel(list_width, n_blocks, aways,
+def score_kernel(list_width, n_blocks, aways, n_prev,
+                 lists_ref, lens_ref, tgt_ref, par_ref,
+                 qa_ref, qb_ref, tcol_ref, tab_a_ref, tab_b_ref, *refs):
+    (qg_ref, loss_ref, tabb_ref, tabf_ref, bias_ref, pos_ref, ls_ref, acc_ref, sem) = refs[n_prev:]
+    _score_body(list_width, n_blocks, aways, lists_ref, lens_ref, tgt_ref, par_ref,
+                qa_ref, qb_ref, tcol_ref, tab_a_ref, tab_b_ref, qg_ref, loss_ref,
+                tabb_ref, tabf_ref, bias_ref, pos_ref, ls_ref, acc_ref, sem)
+
+
+def _score_body(list_width, n_blocks, aways,
                  lists_ref, lens_ref, tgt_ref, par_ref,
                  qa_ref, qb_ref, tcol_ref, tab_a_ref, tab_b_ref,
                  qg_ref, loss_ref,
@@ -114,15 +123,19 @@
     lax.fori_loop(0, n_groups, pass_c, 0)
     qg = acc_ref[...] + (jnp.exp(pos_logit - log_total) - 1.0) * positive
     qg_ref[...] = qg.astype(qg_ref.dtype)
-    loss_ref[...] = log_total - pos_logit
-
-
-def score(q_mine, q_sent, target_slot, block_lists, list_lens, tab_a, tab_b, parity, aways):
+    loss_col = jnp.broadcast_to(log_total - pos_logit, (BLOCK, 128))
+    loss_ref[...] = jnp.transpose(loss_col)[0:1, :].reshape(loss_ref.shape)
+
+
+def score(q_mine, q_sent, target_slot, block_lists, list_lens, tab_a, tab_b, parity, aways,
+          offset, total_rows, prev=None):
     rows, embed = q_mine.shape
     n_blocks = rows // BLOCK
+    first = offset // BLOCK
     n_shards = tab_a.shape[0]
     n_cands = 2 * n_shards * BLOCK
     list_width = block_lists.shape[1]
+    prev = () if prev is None else tuple(prev)
     grid_spec = pltpu.PrefetchScalarGridSpec(
         num_scalar_prefetch=4,
         grid=(n_blocks,),
@@ -132,10 +145,10 @@
             pl.BlockSpec((BLOCK, 1), lambda b, *_: (b, 0)),
             pl.BlockSpec(memory_space=pltpu.VMEM),
             pl.BlockSpec(memory_space=pltpu.VMEM),
-        ],
+        ] + [pl.BlockSpec(memory_space=pl.ANY)] * len(prev),
         out_specs=[
-            pl.BlockSpec((BLOCK, embed), lambda b, *_: (b, 0)),
-            pl.BlockSpec((BLOCK, 1), lambda b, *_: (b, 0)),
+            pl.BlockSpec((BLOCK, embed), lambda b, *_: (b + first, 0)),
+            pl.BlockSpec((1, 1, BLOCK), lambda b, *_: (b + first, 0, 0)),
         ],
         scratch_shapes=[
             pltpu.VMEM((2 * n_shards, BLOCK, embed), jnp.bfloat16),
@@ -148,13 +161,15 @@
         ],
     )
     flops = 2 * 2 * rows * embed * BLOCK * 8
+    n_in = 4 + 5
     qg, loss = pl.pallas_call(
-        functools.partial(score_kernel, list_width, n_blocks, aways),
+        functools.partial(score_kernel, list_width, n_blocks, aways, len(prev)),
         grid_spec=grid_spec,
         out_shape=[
-            jax.ShapeDtypeStruct((rows, embed), jnp.bfloat16),
-            jax.ShapeDtypeStruct((rows, 1), jnp.float32),
+            jax.ShapeDtypeStruct((total_rows, embed), jnp.bfloat16),
+            jax.ShapeDtypeStruct((total_rows // BLOCK, 1, BLOCK), jnp.float32),
         ],
+        input_output_aliases={n_in + i: i for i in range(len(prev))},
         compiler_params=pltpu.CompilerParams(
             dimension_semantics=("arbitrary",),
             vmem_limit_bytes=62 * 1024 * 1024,
@@ -163,8 +178,8 @@
             flops=flops, transcendentals=2 * rows * BLOCK * 8,
             bytes_accessed=2 * tab_a.size * 2 + rows * embed * 4),
     )(block_lists.reshape(-1), list_lens, target_slot, parity,
-      q_mine, q_sent, target_slot.reshape(rows, 1), tab_a, tab_b)
-    return qg, loss.reshape(rows)
+      q_mine, q_sent, target_slot.reshape(rows, 1), tab_a, tab_b, *prev)
+    return qg, loss
 
 
 def shards(hidden_rows, w_proj, panels, cand_ids, counts, target_slot, block_lists, list_lens):
@@ -212,28 +227,27 @@
     n_chunks = 2
     rows_chunk = rows_dev // n_chunks
     blocks_chunk = rows_chunk // BLOCK
-    grads, losses, others = [], [], []
+    outs = None
+    others = []
     for c in range(n_chunks):
         rows = slice(c * rows_chunk, (c + 1) * rows_chunk)
         blocks = slice(c * blocks_chunk, (c + 1) * blocks_chunk)
         sent = lax.ppermute(theirs[rows], "section", partner)
-        grad, loss = score(mine[rows], sent, target_slot[rows], block_lists[blocks], list_lens[blocks], buf, tab_b,
-                           parity, tuple(aways))
-        grads.append(grad)
-        losses.append(loss)
-        others.append(lax.ppermute(grad, "section", partner))
-    query_grad = jnp.concatenate(grads, axis=0)
-    other_grad = jnp.concatenate(others, axis=0)
-    position_loss = jnp.concatenate(losses, axis=0)
-    both = jnp.where(sec == 0, jnp.concatenate([query_grad, other_grad], axis=0),
-                     jnp.concatenate([other_grad, query_grad], axis=0))
-    trunk_grad = lax.dot_general(
-        both,
-        w_proj,
-        (((1,), (1,)), ((), ())),
-        preferred_element_type=jnp.float32,
-    ).astype(jnp.bfloat16)
-    return (query_grad, position_loss, trunk_grad.reshape(halves, rows_dev, width_half))
+        outs = score(mine[rows], sent, target_slot[rows], block_lists[blocks], list_lens[blocks], buf, tab_b,
+                     parity, tuple(aways), c * rows_chunk, rows_dev, outs)
+        others.append(lax.ppermute(outs[0][rows], "section", partner))
+    query_grad, loss_rows = outs
+    position_loss = loss_rows.reshape(rows_dev)
+
+    def to_trunk(g):
+        return lax.dot_general(g, w_proj, (((1,), (1,)), ((), ())),
+                               preferred_element_type=jnp.float32).astype(jnp.bfloat16)
+
+    trunk_grad = jnp.zeros((halves, rows_dev, width_half), jnp.bfloat16)
+    trunk_grad = lax.dynamic_update_slice(trunk_grad, to_trunk(query_grad)[None], (sec, 0, 0))
+    for c in range(n_chunks):
+        trunk_grad = lax.dynamic_update_slice(trunk_grad, to_trunk(others[c])[None], (1 - sec, c * rows_chunk, 0))
+    return (query_grad, position_loss, trunk_grad)
 
 
 def solution(mesh):

time: 158 us -> 157 us (level)
  the two profiles are of different devices: /device:TPU:61 before, /device:TPU:62 now
where the time goes in v8:
time: 157 us
  waiting for transfers between devices  52.8 us (34%)
  Pallas kernels  50.8 us (32%)
  starting transfers between devices  22.5 us (14%)
  local copies, waits for them, and re-layouts  20.4 us (13%)
  matrix products  8.22 us (5%)
    pallas_call x2, Pallas kernels, score(): pl.pallas_call(functools.partial(score_kernel, list_width, n_blocks, away...  50.8 us
    ppermute x7, waiting for transfers between devices, swap(): return lax.ppermute(x, group, [(i, i ^ d) for i in range(n_group)])  21.7 us
    ppermute x2, waiting for transfers between devices, shards(): sent = lax.ppermute(theirs[rows], 'section', partner)  20.2 us
    ppermute x7, starting transfers between devices, swap(): return lax.ppermute(x, group, [(i, i ^ d) for i in range(n_group)])  13.1 us
    ppermute x2, waiting for transfers between devices, shards(): others.append(lax.ppermute(outs[0][rows], 'section', partner))  10.9 us
    ppermute x2, starting transfers between devices, shards(): others.append(lax.ppermute(outs[0][rows], 'section', partner))  7.28 us
    dot_general x1, matrix products, shards(): jnp.dot(flat_rows, w_proj, preferred_element_type=jnp.float32)  5.5 us
    slice x1, local copies, waits for them, and re-layouts, shards(): sent = lax.ppermute(theirs[rows], 'section', partner)  4.96 us
  transfers between devices with their start and end apart: 12, of which 7 were waited for; matrix products, arithmetic and copies ran while one was open for 10% of the time, Pallas kernels for 32%

profile of v8, /device:TPU:62, one launch (start us, length us, event | category | flops | bytes accessed | tf_op | source)
XLA Modules:
  0.0 157.0 jit_solution(15982849982169472854)
XLA Ops:
  0.7 0.7 compare_select_fusion
  1.4 3.6 %gather_fusion = s32[512]{0:T(512)S(1)} fusion(s32[65536]{0:T(1024)} %param.12, s32[1024]{0:T(1024)S(1)} %pad_clamp_fusion), kind=kCustom, calls=%fused_computation | custom fusion | bytes 6144 | tf_op jit(solution)/shard_map/gather | solution.py:196
  5.1 5.5 %fusion.7 = f32[2,2048,256]{2,1,0:T(8,128)} fusion(bf16[2,2048,512]{2,1,0:T(8,128)(2,1)} %param.8, bf16[512,256]{1,0:T(8,128)(2,1)S(1)} %copy-done), kind=kOutput, calls=%fused_computation.16 | convolution fusion | flops 1073741824 | bytes 8650752 | tf_op jit(solution)/shard_map/dot_general | solution.py:191
  10.6 1.5 collective-permute-start.1
  12.1 2.7 %collective-permute-start.3 = (bf16[1,272,256]{2,1,0:T(8,128)(2,1)S(1)}, bf16[1,272,256]{2,1,0:T(8,128)(2,1)S(1)}, u32[]{:S(2)}, u32[]{:S(2)}) collective-permute-start(bf16[1,272,256]{2,1,0:T(8,128)(2,1)S(1)} %fusion.10), channel_id=1, source_target_pairs={{0,96},{8,104},{16,112},{24,120},{32,64},{40,72},{48,80},{56,88},{... | collective-permute-start | bytes 417800 | tf_op jit(solution)/shard_map/ppermute | solution.py:206
  14.8 3.9 %collective-permute-done.1 = bf16[1,272,256]{2,1,0:T(8,128)(2,1)S(1)} collective-permute-done((bf16[1,272,256]{2,1,0:T(8,128)(2,1)S(1)}, bf16[1,272,256]{2,1,0:T(8,128)(2,1)S(1)}, u32[]{:S(2)}, u32[]{:S(2)}) %collective-permute-start.1) | collective-permute-done | bytes 139296 | tf_op jit(solution)/shard_map/ppermute | solution.py:206
  18.8 1.8 %collective-permute-done.3 = bf16[1,272,256]{2,1,0:T(8,128)(2,1)S(1)} collective-permute-done((bf16[1,272,256]{2,1,0:T(8,128)(2,1)S(1)}, bf16[1,272,256]{2,1,0:T(8,128)(2,1)S(1)}, u32[]{:S(2)}, u32[]{:S(2)}) %collective-permute-start.3) | collective-permute-done | bytes 139296 | tf_op jit(solution)/shard_map/ppermute | solution.py:206
  20.6 2.0 %collective-permute-start.5 = (bf16[4,272,256]{2,1,0:T(8,128)(2,1)S(1)}, bf16[4,272,256]{2,1,0:T(8,128)(2,1)S(1)}, u32[]{:S(2)}, u32[]{:S(2)}) collective-permute-start(bf16[4,272,256]{2,1,0:T(8,128)(2,1)S(1)} %get-tuple-element.19), channel_id=1, source_target_pairs={{0,24},{8,16},{16,8},{24,0},{32,56},{40,48},{48,40},{56,32},{64,88... | collective-permute-start | bytes 1671176 | tf_op jit(solution)/shard_map/ppermute | solution.py:206
  22.6 2.2 %collective-permute-start.4 = (bf16[4,272,256]{2,1,0:T(8,128)(2,1)S(1)}, bf16[4,272,256]{2,1,0:T(8,128)(2,1)S(1)}, u32[]{:S(2)}, u32[]{:S(2)}) collective-permute-start(bf16[4,272,256]{2,1,0:T(8,128)(2,1)S(1)} %get-tuple-element.19), channel_id=1, source_target_pairs={{0,8},{8,0},{16,24},{24,16},{32,40},{40,32},{48,56},{56,48},{64,72... | collective-permute-start | bytes 1671176 | tf_op jit(solution)/shard_map/ppermute | solution.py:206
  24.9 10.5 %collective-permute-done.5 = bf16[4,272,256]{2,1,0:T(8,128)(2,1)S(1)} collective-permute-done((bf16[4,272,256]{2,1,0:T(8,128)(2,1)S(1)}, bf16[4,272,256]{2,1,0:T(8,128)(2,1)S(1)}, u32[]{:S(2)}, u32[]{:S(2)}) %collective-permute-start.5) | collective-permute-done | bytes 557088 | tf_op jit(solution)/shard_map/ppermute | solution.py:206
  35.4 2.3 %collective-permute-start.6 = (bf16[2,272,256]{2,1,0:T(8,128)(2,1)S(1)}, bf16[2,272,256]{2,1,0:T(8,128)(2,1)S(1)}, u32[]{:S(2)}, u32[]{:S(2)}) collective-permute-start(bf16[2,272,256]{2,1,0:T(8,128)(2,1)S(1)} %slice.74), channel_id=1, source_target_pairs={{0,8},{8,0},{16,24},{24,16},{32,40},{40,32},{48,56},{56,48},{64,72... | collective-permute-start | bytes 835592 | tf_op jit(solution)/shard_map/ppermute | solution.py:206
  37.7 2.4 %collective-permute-start.7 = (bf16[2,272,256]{2,1,0:T(8,128)(2,1)S(1)}, bf16[2,272,256]{2,1,0:T(8,128)(2,1)S(1)}, u32[]{:S(2)}, u32[]{:S(2)}) collective-permute-start(bf16[2,272,256]{2,1,0:T(8,128)(2,1)S(1)} %slice.75), channel_id=1, source_target_pairs={{0,24},{8,16},{16,8},{24,0},{32,56},{40,48},{48,40},{56,32},{64,88... | collective-permute-start | bytes 835592 | tf_op jit(solution)/shard_map/ppermute | solution.py:206
  40.2 3.6 %collective-permute-done.6 = bf16[2,272,256]{2,1,0:T(8,128)(2,1)S(1)} collective-permute-done((bf16[2,272,256]{2,1,0:T(8,128)(2,1)S(1)}, bf16[2,272,256]{2,1,0:T(8,128)(2,1)S(1)}, u32[]{:S(2)}, u32[]{:S(2)}) %collective-permute-start.6) | collective-permute-done | bytes 278560 | tf_op jit(solution)/shard_map/ppermute | solution.py:206
  43.9 1.9 %collective-permute-done.7 = bf16[2,272,256]{2,1,0:T(8,128)(2,1)S(1)} collective-permute-done((bf16[2,272,256]{2,1,0:T(8,128)(2,1)S(1)}, bf16[2,272,256]{2,1,0:T(8,128)(2,1)S(1)}, u32[]{:S(2)}, u32[]{:S(2)}) %collective-permute-start.7) | collective-permute-done | bytes 278560 | tf_op jit(solution)/shard_map/ppermute | solution.py:206
  45.9 5.0 %dynamic-slice_bitcast_fusion = (f32[1024,256]{1,0:T(8,128)}, f32[1024,256]{1,0:T(8,128)}, f32[1024,256]{1,0:T(8,128)}, f32[1024,256]{1,0:T(8,128)}) fusion(f32[2,2048,256]{2,1,0:T(8,128)} %fusion.7, s32[]{:T(128)S(6)} %select_n.31, s32[]{:T(128)S(6)} %add.41, s32[]{:T(128)S(6)} %select_n.30), kind=kLoop, calls=%fused_computation.10 | loop fusion | bytes 8388620 | tf_op jit(solution)/shard_map/slice | solution.py:235
  50.9 0.8 collective-permute-start.9
  51.7 1.2 collective-permute-start
  54.1 1.0 copy.13.tcol_ref
  55.7 1.3 fusion.13
  57.0 20.2 %collective-permute-done.9.qb_ref = f32[1024,256]{1,0:T(8,128)} collective-permute-done((f32[1024,256]{1,0:T(8,128)}, f32[1024,256]{1,0:T(8,128)}, u32[]{:S(2)}, u32[]{:S(2)}) %collective-permute-start.9) | collective-permute-done | bytes 1048608 | tf_op jit(solution)/shard_map/ppermute | solution.py:235
  77.2 24.4 %shard_map.103 = (bf16[2048,256]{1,0:T(8,128)(2,1)}, f32[8,1,256]{2,1,0:T(1,128)}) custom-call(s32[48]{0:T(128)} %reshape.36.lists_ref, s32[4]{0:T(128)} %get-tuple-element.31.lens_ref, s32[1024]{0:T(1024)} %copy-done.7, s32[2]{0:T(128)} %pad_add_fusion.par_ref, f32[1024,256]{1,0:T(8,128)} %get-tuple-element.18.qa_ref, ...), custom_call_target="tpu_custom_call" | custom-call | flops 2147483648 | bytes 5505024 | tf_op jit(solution)/shard_map/pallas_call | solution.py:165
  101.6 1.1 slice.70
  102.7 7.2 %collective-permute-start.10 = (bf16[1024,256]{1,0:T(8,128)(2,1)S(1)}, bf16[1024,256]{1,0:T(8,128)(2,1)}, u32[]{:S(2)}, u32[]{:S(2)}) collective-permute-start(bf16[1024,256]{1,0:T(8,128)(2,1)S(1)} %slice.70), channel_id=1, source_target_pairs={{0,64},{64,0},{1,65},{65,1},{2,66},{66,2},{3,67},{67,3},{4,68},{68... | collective-permute-start | bytes 1572872 | tf_op jit(solution)/shard_map/ppermute | solution.py:238
  110.6 1.0 copy.14.tcol_ref
  111.6 1.0 copy-done.4
  112.6 26.4 %shard_map.104 = (bf16[2048,256]{1,0:T(8,128)(2,1)}, f32[8,1,256]{2,1,0:T(1,128)}) custom-call(s32[48]{0:T(128)} %reshape.34.lists_ref, s32[4]{0:T(128)} %get-tuple-element.32.lens_ref, s32[1024]{0:T(1024)} %copy-done.6, s32[2]{0:T(128)} %pad_add_fusion.par_ref, ...), custom_call_target="tpu_custom_call", output_to_operand_aliasing={{0}: (9, {}), {1}: (10, {})} | custom-call | flops 2147483648 | bytes 5505024 | tf_op jit(solution)/shard_map/pallas_call | solution.py:165
  139.0 1.1 slice.71
  140.5 0.8 copy-done.1
  141.3 0.7 fusion.1
  142.1 1.5 fusion.3
  143.6 10.9 %collective-permute-done.11 = bf16[1024,256]{1,0:T(8,128)(2,1)S(1)} collective-permute-done((bf16[1024,256]{1,0:T(8,128)(2,1)S(1)}, bf16[1024,256]{1,0:T(8,128)(2,1)S(1)}, u32[]{:S(2)}, u32[]{:S(2)}) %collective-permute-start.11) | collective-permute-done | bytes 524320 | tf_op jit(solution)/shard_map/ppermute | solution.py:238
  155.0 2.0 %copy-done.2 = bf16[2,2048,512]{2,1,0:T(8,128)(2,1)} copy-done((bf16[2,2048,512]{2,1,0:T(8,128)(2,1)}, bf16[2,2048,512]{2,1,0:T(8,128)(2,1)S(1)}, u32[]{:S(2)}) %copy-start.2) | copy-done | bytes 4194328
  (50 shorter events, 3.7 us)
Async XLA Ops:
  0.6 4.4 %copy-start = (bf16[512,256]{1,0:T(8,128)(2,1)S(1)}, bf16[512,256]{1,0:T(8,128)(2,1)}, u32[]{:S(2)}) copy-start(bf16[512,256]{1,0:T(8,128)(2,1)} %param.9) | copy-start | bytes 786436
  5.1 5.5 %copy-start.5 = (bf16[512,256]{1,0:T(8,128)(2,1)S(1)}, bf16[512,256]{1,0:T(8,128)(2,1)}, u32[]{:S(2)}) copy-start(bf16[512,256]{1,0:T(8,128)(2,1)} %param.10) | copy-start | bytes 786436
  10.6 8.1 %collective-permute-start.1 = (bf16[1,272,256]{2,1,0:T(8,128)(2,1)S(1)}, bf16[1,272,256]{2,1,0:T(8,128)(2,1)S(1)}, u32[]{:S(2)}, u32[]{:S(2)}) collective-permute-start(bf16[1,272,256]{2,1,0:T(8,128)(2,1)S(1)} %fusion.10), channel_id=1, source_target_pairs={{0,32},{8,40},{16,48},{24,56},{32,0},{40,8},{48,16},{56,24},{64,96... | collective-permute-start | bytes 417800 | tf_op jit(solution)/shard_map/ppermute | solution.py:206
  12.1 6.7 %collective-permute-start.2 = (bf16[1,272,256]{2,1,0:T(8,128)(2,1)S(1)}, bf16[1,272,256]{2,1,0:T(8,128)(2,1)S(1)}, u32[]{:S(2)}, u32[]{:S(2)}) collective-permute-start(bf16[1,272,256]{2,1,0:T(8,128)(2,1)S(1)} %fusion.10), channel_id=1, source_target_pairs={{0,64},{8,72},{16,80},{24,88},{32,96},{40,104},{48,112},{56,120},{... | collective-permute-start | bytes 417800 | tf_op jit(solution)/shard_map/ppermute | solution.py:206
  12.1 8.5 %collective-permute-start.3 = (bf16[1,272,256]{2,1,0:T(8,128)(2,1)S(1)}, bf16[1,272,256]{2,1,0:T(8,128)(2,1)S(1)}, u32[]{:S(2)}, u32[]{:S(2)}) collective-permute-start(bf16[1,272,256]{2,1,0:T(8,128)(2,1)S(1)} %fusion.10), channel_id=1, source_target_pairs={{0,96},{8,104},{16,112},{24,120},{32,64},{40,72},{48,80},{56,88},{... | collective-permute-start | bytes 417800 | tf_op jit(solution)/shard_map/ppermute | solution.py:206
  20.6 14.7 %collective-permute-start.5 = (bf16[4,272,256]{2,1,0:T(8,128)(2,1)S(1)}, bf16[4,272,256]{2,1,0:T(8,128)(2,1)S(1)}, u32[]{:S(2)}, u32[]{:S(2)}) collective-permute-start(bf16[4,272,256]{2,1,0:T(8,128)(2,1)S(1)} %get-tuple-element.19), channel_id=1, source_target_pairs={{0,24},{8,16},{16,8},{24,0},{32,56},{40,48},{48,40},{56,32},{64,88... | collective-permute-start | bytes 1671176 | tf_op jit(solution)/shard_map/ppermute | solution.py:206
  22.6 15.0 %collective-permute-start.4 = (bf16[4,272,256]{2,1,0:T(8,128)(2,1)S(1)}, bf16[4,272,256]{2,1,0:T(8,128)(2,1)S(1)}, u32[]{:S(2)}, u32[]{:S(2)}) collective-permute-start(bf16[4,272,256]{2,1,0:T(8,128)(2,1)S(1)} %get-tuple-element.19), channel_id=1, source_target_pairs={{0,8},{8,0},{16,24},{24,16},{32,40},{40,32},{48,56},{56,48},{64,72... | collective-permute-start | bytes 1671176 | tf_op jit(solution)/shard_map/ppermute | solution.py:206
  35.4 8.5 %collective-permute-start.6 = (bf16[2,272,256]{2,1,0:T(8,128)(2,1)S(1)}, bf16[2,272,256]{2,1,0:T(8,128)(2,1)S(1)}, u32[]{:S(2)}, u32[]{:S(2)}) collective-permute-start(bf16[2,272,256]{2,1,0:T(8,128)(2,1)S(1)} %slice.74), channel_id=1, source_target_pairs={{0,8},{8,0},{16,24},{24,16},{32,40},{40,32},{48,56},{56,48},{64,72... | collective-permute-start | bytes 835592 | tf_op jit(solution)/shard_map/ppermute | solution.py:206
  37.7 8.0 %collective-permute-start.7 = (bf16[2,272,256]{2,1,0:T(8,128)(2,1)S(1)}, bf16[2,272,256]{2,1,0:T(8,128)(2,1)S(1)}, u32[]{:S(2)}, u32[]{:S(2)}) collective-permute-start(bf16[2,272,256]{2,1,0:T(8,128)(2,1)S(1)} %slice.75), channel_id=1, source_target_pairs={{0,24},{8,16},{16,8},{24,0},{32,56},{40,48},{48,40},{56,32},{64,88... | collective-permute-start | bytes 835592 | tf_op jit(solution)/shard_map/ppermute | solution.py:206
  45.8 5.1 %copy-start.3 = (bf16[16,272,256]{2,1,0:T(8,128)(2,1)}, bf16[16,272,256]{2,1,0:T(8,128)(2,1)S(1)}, u32[]{:S(2)}) copy-start(bf16[16,272,256]{2,1,0:T(8,128)(2,1)S(1)} %constant_dynamic-update-slice_fusion.4.tab_a_ref) | copy-start | bytes 6684676
  45.8 31.4 %collective-permute-start.8 = (bf16[16,272,256]{2,1,0:T(8,128)(2,1)S(1)}, bf16[16,272,256]{2,1,0:T(8,128)(2,1)}, u32[]{:S(2)}, u32[]{:S(2)}) collective-permute-start(bf16[16,272,256]{2,1,0:T(8,128)(2,1)S(1)} %constant_dynamic-update-slice_fusion.4.tab_a_ref), channel_id=1, source_target_pairs={{0,1},{1,0},{2,3},{3,2},{4,5},{5,4},{6,7},{7,6},{8,9},{9,8},{10,11... | collective-permute-start | bytes 6684680 | tf_op jit(solution)/shard_map/ppermute | solution.py:223
  45.9 7.0 %copy-start.10 = (s32[8,12]{1,0:T(8,128)S(1)}, s32[8,12]{1,0:T(8,128)}, u32[]{:S(2)}) copy-start(s32[8,12]{1,0:T(8,128)} %param.14) | copy-start | bytes 1156
  45.9 8.2 %copy-start.8 = (s32[2048]{0:T(1024)S(1)}, s32[2048]{0:T(1024)}, u32[]{:S(2)}) copy-start(s32[2048]{0:T(1024)} %param.13) | copy-start | bytes 24580
  50.9 26.3 %collective-permute-start.9 = (f32[1024,256]{1,0:T(8,128)}, f32[1024,256]{1,0:T(8,128)}, u32[]{:S(2)}, u32[]{:S(2)}) collective-permute-start(f32[1024,256]{1,0:T(8,128)} %get-tuple-element.15), channel_id=1, source_target_pairs={{0,64},{64,0},{1,65},{65,1},{2,66},{66,2},{3,67},{67,3},{4,68},{68... | collective-permute-start | bytes 3145736 | tf_op jit(solution)/shard_map/ppermute | solution.py:235
  51.7 59.9 %collective-permute-start = (f32[1024,256]{1,0:T(8,128)}, f32[1024,256]{1,0:T(8,128)S(1)}, u32[]{:S(2)}, u32[]{:S(2)}) collective-permute-start(f32[1024,256]{1,0:T(8,128)} %get-tuple-element.16), channel_id=1, source_target_pairs={{0,64},{64,0},{1,65},{65,1},{2,66},{66,2},{3,67},{67,3},{4,68},{68... | collective-permute-start | bytes 3145736 | tf_op jit(solution)/shard_map/ppermute | solution.py:235
  54.1 23.1 %copy-start.7 = (s32[1024]{0:T(1024)}, s32[1024]{0:T(1024)S(1)}, u32[]{:S(2)}) copy-start(s32[1024]{0:T(1024)S(1)} %get-tuple-element.27.tgt_ref) | copy-start | bytes 12292
  54.1 56.5 %copy-start.6 = (s32[1024]{0:T(1024)}, s32[1024]{0:T(1024)S(1)}, u32[]{:S(2)}) copy-start(s32[1024]{0:T(1024)S(1)} %get-tuple-element.28.tgt_ref) | copy-start | bytes 12292
  77.2 32.7 %copy-start.9 = (s32[4,12]{1,0:T(4,128)S(1)}, s32[4,12]{1,0:T(4,128)}, u32[]{:S(2)}) copy-start(s32[4,12]{1,0:T(4,128)} %get-tuple-element.30) | copy-start | bytes 580
  102.7 39.4 %collective-permute-start.10 = (bf16[1024,256]{1,0:T(8,128)(2,1)S(1)}, bf16[1024,256]{1,0:T(8,128)(2,1)}, u32[]{:S(2)}, u32[]{:S(2)}) collective-permute-start(bf16[1024,256]{1,0:T(8,128)(2,1)S(1)} %slice.70), channel_id=1, source_target_pairs={{0,64},{64,0},{1,65},{65,1},{2,66},{66,2},{3,67},{67,3},{4,68},{68... | collective-permute-start | bytes 1572872 | tf_op jit(solution)/shard_map/ppermute | solution.py:238
  111.6 1.0 copy-start.4
  140.1 1.2 copy-start.1
  140.1 14.4 %collective-permute-start.11 = (bf16[1024,256]{1,0:T(8,128)(2,1)S(1)}, bf16[1024,256]{1,0:T(8,128)(2,1)S(1)}, u32[]{:S(2)}, u32[]{:S(2)}) collective-permute-start(bf16[1024,256]{1,0:T(8,128)(2,1)S(1)} %slice.71), channel_id=1, source_target_pairs={{0,64},{64,0},{1,65},{65,1},{2,66},{66,2},{3,67},{67,3},{4,68},{68... | collective-permute-start | bytes 1572872 | tf_op jit(solution)/shard_map/ppermute | solution.py:238
  155.0 2.0 %copy-start.2 = (bf16[2,2048,512]{2,1,0:T(8,128)(2,1)}, bf16[2,2048,512]{2,1,0:T(8,128)(2,1)S(1)}, u32[]{:S(2)}) copy-start(bf16[2,2048,512]{2,1,0:T(8,128)(2,1)S(1)} %fusion.5) | copy-start | bytes 12582916

commit v9 on v8

--- a/solution.py
+++ b/solution.py
@@ -184,11 +184,9 @@
 
 def shards(hidden_rows, w_proj, panels, cand_ids, counts, target_slot, block_lists, list_lens):
     halves, rows_dev, width_half = hidden_rows.shape
-    flat_rows = hidden_rows.reshape(halves * rows_dev, width_half)
     n_sec = lax.axis_size("section")
     sec = lax.axis_index("section")
     partner = [(i, i ^ 1) for i in range(n_sec)]
-    partial = jnp.dot(flat_rows, w_proj, preferred_element_type=jnp.float32).reshape(halves, rows_dev, -1)
     n_pos = lax.axis_size("pos")
     core = lax.axis_index("pos") % 2
     n_own = lax.axis_size("owner")
@@ -198,7 +196,6 @@
     my_block = lax.dynamic_slice_in_dim(panels, core * BLOCK, BLOCK, axis=0)
     my_bias = jnp.pad(lax.dynamic_slice_in_dim(own_bias, core, 1, axis=0), ((0, BIAS_ROWS - 1), (0, 0)))
     buf = jnp.concatenate([my_block, my_bias], axis=0)[None]
-    partial, buf = lax.optimization_barrier((partial, buf))
     n_group = n_sec * n_own
     group = ("section", "owner")
 
@@ -222,19 +219,24 @@
             d //= 2
     tab_b = lax.ppermute(buf, "pos", [(i, i ^ 1) for i in range(n_pos)])
     parity = jnp.stack([core, me]).astype(jnp.int32)
-    mine = lax.dynamic_index_in_dim(partial, sec, 0, keepdims=False)
-    theirs = lax.dynamic_index_in_dim(partial, 1 - sec, 0, keepdims=False)
+    mine_rows = lax.dynamic_index_in_dim(hidden_rows, sec, 0, keepdims=False)
+    their_rows = lax.dynamic_index_in_dim(hidden_rows, 1 - sec, 0, keepdims=False)
+
+    def project(x):
+        return jnp.dot(x, w_proj, preferred_element_type=jnp.float32)
+
+    n_pblocks = rows_dev // BLOCK
+    first_blocks = (n_pblocks * 5 + 7) // 8
+    bounds = [0, first_blocks * BLOCK, rows_dev] if 0 < first_blocks < n_pblocks else [0, rows_dev // 2, rows_dev]
     n_chunks = 2
-    rows_chunk = rows_dev // n_chunks
-    blocks_chunk = rows_chunk // BLOCK
     outs = None
     others = []
     for c in range(n_chunks):
-        rows = slice(c * rows_chunk, (c + 1) * rows_chunk)
-        blocks = slice(c * blocks_chunk, (c + 1) * blocks_chunk)
-        sent = lax.ppermute(theirs[rows], "section", partner)
-        outs = score(mine[rows], sent, target_slot[rows], block_lists[blocks], list_lens[blocks], buf, tab_b,
-                     parity, tuple(aways), c * rows_chunk, rows_dev, outs)
+        rows = slice(bounds[c], bounds[c + 1])
+        blocks = slice(bounds[c] // BLOCK, bounds[c + 1] // BLOCK)
+        sent = lax.ppermute(project(their_rows[rows]), "section", partner)
+        outs = score(project(mine_rows[rows]), sent, target_slot[rows], block_lists[blocks], list_lens[blocks],
+                     buf, tab_b, parity, tuple(aways), bounds[c], rows_dev, outs)
         others.append(lax.ppermute(outs[0][rows], "section", partner))
     query_grad, loss_rows = outs
     position_loss = loss_rows.reshape(rows_dev)
@@ -246,7 +248,7 @@
     trunk_grad = jnp.zeros((halves, rows_dev, width_half), jnp.bfloat16)
     trunk_grad = lax.dynamic_update_slice(trunk_grad, to_trunk(query_grad)[None], (sec, 0, 0))
     for c in range(n_chunks):
-        trunk_grad = lax.dynamic_update_slice(trunk_grad, to_trunk(others[c])[None], (1 - sec, c * rows_chunk, 0))
+        trunk_grad = lax.dynamic_update_slice(trunk_grad, to_trunk(others[c])[None], (1 - sec, bounds[c], 0))
     return (query_grad, position_loss, trunk_grad)
 
 

time: 157 us -> 153 us (0.975)
  the two profiles are of different devices: /device:TPU:62 before, /device:TPU:7 now
where the time goes in v9:
time: 153 us
  Pallas kernels  54.9 us (36%)
  waiting for transfers between devices  52.2 us (34%)
  starting transfers between devices  17.9 us (12%)
  local copies, waits for them, and re-layouts  13.8 us (9%)
  matrix products  11.4 us (7%)
    pallas_call x2, Pallas kernels, score(): pl.pallas_call(functools.partial(score_kernel, list_width, n_blocks, away...  54.9 us
    ppermute x7, waiting for transfers between devices, swap(): return lax.ppermute(x, group, [(i, i ^ d) for i in range(n_group)])  25.8 us
    ppermute x2, waiting for transfers between devices, shards(): sent = lax.ppermute(project(their_rows[rows]), 'section', partner)  19.6 us
    dot_general x4, matrix products, project(): return jnp.dot(x, w_proj, preferred_element_type=jnp.float32)  9.74 us
    ppermute x7, starting transfers between devices, swap(): return lax.ppermute(x, group, [(i, i ^ d) for i in range(n_group)])  8.98 us
    ppermute x2, waiting for transfers between devices, shards(): others.append(lax.ppermute(outs[0][rows], 'section', partner))  6.81 us
    ppermute x2, starting transfers between devices, shards(): others.append(lax.ppermute(outs[0][rows], 'section', partner))  4.72 us
    gather x1, local copies, waits for them, and re-layouts, shards(): counts[cand_ids].astype(jnp.float32)  3.63 us
  transfers between devices with their start and end apart: 12, of which 9 were waited for; matrix products, arithmetic and copies ran while one was open for 12% of the time, Pallas kernels for 36%

profile of v9, /device:TPU:7, one launch (start us, length us, event | category | flops | bytes accessed | tf_op | source)
XLA Modules:
  0.0 152.5 jit_solution(9603821341094860549)
XLA Ops:
  0.7 0.7 compare_select_fusion
  1.4 3.6 %gather_fusion = s32[512]{0:T(512)S(1)} fusion(s32[65536]{0:T(1024)} %param.12, s32[1024]{0:T(1024)S(1)} %pad_clamp_fusion), kind=kCustom, calls=%fused_computation | custom fusion | bytes 6144 | tf_op jit(solution)/shard_map/gather | solution.py:194
  5.2 1.2 collective-permute-start.1
  6.4 2.1 %collective-permute-start.3 = (bf16[1,272,256]{2,1,0:T(8,128)(2,1)S(1)}, bf16[1,272,256]{2,1,0:T(8,128)(2,1)S(1)}, u32[]{:S(2)}, u32[]{:S(2)}) collective-permute-start(bf16[1,272,256]{2,1,0:T(8,128)(2,1)S(1)} %fusion.12), channel_id=1, source_target_pairs={{0,96},{8,104},{16,112},{24,120},{32,64},{40,72},{48,80},{56,88},{... | collective-permute-start | bytes 417800 | tf_op jit(solution)/shard_map/ppermute | solution.py:203
  8.5 2.8 %collective-permute-done.1 = bf16[1,272,256]{2,1,0:T(8,128)(2,1)S(1)} collective-permute-done((bf16[1,272,256]{2,1,0:T(8,128)(2,1)S(1)}, bf16[1,272,256]{2,1,0:T(8,128)(2,1)S(1)}, u32[]{:S(2)}, u32[]{:S(2)}) %collective-permute-start.1) | collective-permute-done | bytes 139296 | tf_op jit(solution)/shard_map/ppermute | solution.py:203
  11.3 0.8 collective-permute-done.2
  12.1 3.2 %collective-permute-done.3 = bf16[1,272,256]{2,1,0:T(8,128)(2,1)S(1)} collective-permute-done((bf16[1,272,256]{2,1,0:T(8,128)(2,1)S(1)}, bf16[1,272,256]{2,1,0:T(8,128)(2,1)S(1)}, u32[]{:S(2)}, u32[]{:S(2)}) %collective-permute-start.3) | collective-permute-done | bytes 139296 | tf_op jit(solution)/shard_map/ppermute | solution.py:203
  15.3 3.8 %collective-permute-start.5 = (bf16[4,272,256]{2,1,0:T(8,128)(2,1)S(1)}, bf16[4,272,256]{2,1,0:T(8,128)(2,1)S(1)}, u32[]{:S(2)}, u32[]{:S(2)}) collective-permute-start(bf16[4,272,256]{2,1,0:T(8,128)(2,1)S(1)} %pad_maximum_fusion), channel_id=1, source_target_pairs={{0,24},{8,16},{16,8},{24,0},{32,56},{40,48},{48,40},{56,32},{64,88... | collective-permute-start | bytes 1671176 | tf_op jit(solution)/shard_map/ppermute | solution.py:203
  19.2 12.4 %collective-permute-done.5 = bf16[4,272,256]{2,1,0:T(8,128)(2,1)S(1)} collective-permute-done((bf16[4,272,256]{2,1,0:T(8,128)(2,1)S(1)}, bf16[4,272,256]{2,1,0:T(8,128)(2,1)S(1)}, u32[]{:S(2)}, u32[]{:S(2)}) %collective-permute-start.5) | collective-permute-done | bytes 557088 | tf_op jit(solution)/shard_map/ppermute | solution.py:203
  31.7 0.8 collective-permute-done.4
  32.5 1.7 %collective-permute-start.7 = (bf16[2,272,256]{2,1,0:T(8,128)(2,1)S(1)}, bf16[2,272,256]{2,1,0:T(8,128)(2,1)S(1)}, u32[]{:S(2)}, u32[]{:S(2)}) collective-permute-start(bf16[2,272,256]{2,1,0:T(8,128)(2,1)S(1)} %slice.75), channel_id=1, source_target_pairs={{0,24},{8,16},{16,8},{24,0},{32,56},{40,48},{48,40},{56,32},{64,88... | collective-permute-start | bytes 835592 | tf_op jit(solution)/shard_map/ppermute | solution.py:203
  34.3 4.4 %collective-permute-done.6 = bf16[2,272,256]{2,1,0:T(8,128)(2,1)S(1)} collective-permute-done((bf16[2,272,256]{2,1,0:T(8,128)(2,1)S(1)}, bf16[2,272,256]{2,1,0:T(8,128)(2,1)S(1)}, u32[]{:S(2)}, u32[]{:S(2)}) %collective-permute-start.6) | collective-permute-done | bytes 278560 | tf_op jit(solution)/shard_map/ppermute | solution.py:203
  38.7 1.5 %collective-permute-done.7 = bf16[2,272,256]{2,1,0:T(8,128)(2,1)S(1)} collective-permute-done((bf16[2,272,256]{2,1,0:T(8,128)(2,1)S(1)}, bf16[2,272,256]{2,1,0:T(8,128)(2,1)S(1)}, u32[]{:S(2)}, u32[]{:S(2)}) %collective-permute-start.7) | collective-permute-done | bytes 278560 | tf_op jit(solution)/shard_map/ppermute | solution.py:203
  40.3 2.7 %collective-permute-start.8 = (bf16[16,272,256]{2,1,0:T(8,128)(2,1)S(1)}, bf16[16,272,256]{2,1,0:T(8,128)(2,1)}, u32[]{:S(2)}, u32[]{:S(2)}) collective-permute-start(bf16[16,272,256]{2,1,0:T(8,128)(2,1)S(1)} %constant_dynamic-update-slice_fusion.tab_a_ref), channel_id=1, source_target_pairs={{0,1},{1,0},{2,3},{3,2},{4,5},{5,4},{6,7},{7,6},{8,9},{9,8},{10,11... | collective-permute-start | bytes 6684680 | tf_op jit(solution)/shard_map/ppermute | solution.py:220
  43.0 2.9 %fusion.4 = f32[1280,256]{1,0:T(8,128)} fusion(bf16[512,256]{1,0:T(8,128)(2,1)S(1)} %copy-done, bf16[2,2048,512]{2,1,0:T(8,128)(2,1)} %param.8, s32[]{:T(128)S(6)} %select_n.28), kind=kOutput, calls=%fused_computation.9 | convolution fusion | flops 335544320 | bytes 2883588 | tf_op jit(solution)/shard_map/dot_general | solution.py:226
  46.5 1.5 fusion.8
  48.0 1.0 collective-permute-start
  50.1 1.1 reshape.45.tcol_ref
  51.2 0.6 reshape.30.lists_ref
  52.4 0.9 reshape.44.tcol_ref
  53.3 2.9 %fusion.5.qa_ref = f32[1280,256]{1,0:T(8,128)} fusion(bf16[512,256]{1,0:T(8,128)(2,1)S(1)} %copy-done, bf16[2,2048,512]{2,1,0:T(8,128)(2,1)} %param.8, s32[]{:T(128)S(6)} %select_n.27), kind=kOutput, calls=%fused_computation.11 | convolution fusion | flops 335544320 | bytes 2883588 | tf_op jit(solution)/shard_map/dot_general | solution.py:226
  56.2 19.6 %collective-permute-done.9.qb_ref = f32[1280,256]{1,0:T(8,128)} collective-permute-done((f32[1280,256]{1,0:T(8,128)}, f32[1280,256]{1,0:T(8,128)}, u32[]{:S(2)}, u32[]{:S(2)}) %collective-permute-start.9) | collective-permute-done | bytes 1310752 | tf_op jit(solution)/shard_map/ppermute | solution.py:237
  75.8 31.5 %shard_map.103 = (bf16[2048,256]{1,0:T(8,128)(2,1)}, f32[8,1,256]{2,1,0:T(1,128)}) custom-call(s32[60]{0:T(128)} %reshape.32.lists_ref, s32[5]{0:T(128)} %bitcast.48, s32[1280]{0:T(1024)} %bitcast.44, s32[2]{0:T(128)} %pad_add_fusion.par_ref, f32[1280,256]{1,0:T(8,128)} %fusion.5.qa_ref, f32[1280,256]{1,0:T(8,128)} %collective-permute-done.9.qb_ref, ...), custom_call_target="tpu_custom_call" | custom-call | flops 2684354560 | bytes 5767168 | tf_op jit(solution)/shard_map/pallas_call | solution.py:165
  107.3 2.0 %slice.70 = bf16[1280,256]{1,0:T(8,128)(2,1)} slice(bf16[2048,256]{1,0:T(8,128)(2,1)} %get-tuple-element.7.refs_0_), slice={[0:1280], [0:256]} | slice | bytes 1310720 | tf_op jit(solution)/shard_map/slice | solution.py:240
  109.3 4.6 %collective-permute-start.10 = (bf16[1280,256]{1,0:T(8,128)(2,1)}, bf16[1280,256]{1,0:T(8,128)(2,1)S(1)}, u32[]{:S(2)}, u32[]{:S(2)}) collective-permute-start(bf16[1280,256]{1,0:T(8,128)(2,1)} %slice.70), channel_id=1, source_target_pairs={{0,64},{64,0},{1,65},{65,1},{2,66},{66,2},{3,67},{67,3},{4,68},{68... | collective-permute-start | bytes 1966088 | tf_op jit(solution)/shard_map/ppermute | solution.py:240
  113.9 2.4 %fusion.9.qa_ref = f32[768,256]{1,0:T(8,128)} fusion(bf16[512,256]{1,0:T(8,128)(2,1)S(1)} %copy-done, bf16[2,2048,512]{2,1,0:T(8,128)(2,1)} %param.8, s32[]{:T(128)S(6)} %select_n.27, s32[]{:T(128)S(6)} %add.41), kind=kOutput, calls=%fused_computation.17 | convolution fusion | flops 201326592 | bytes 1835016 | tf_op jit(solution)/shard_map/dot_general | solution.py:226
  116.3 23.4 %shard_map.104 = (bf16[2048,256]{1,0:T(8,128)(2,1)}, f32[8,1,256]{2,1,0:T(1,128)}) custom-call(s32[36]{0:T(128)} %reshape.30.lists_ref, s32[3]{0:T(128)} %slice.55.lens_ref, s32[768]{0:T(1024)} %copy-done.5, s32[2]{0:T(128)} %pad_add_fusion.par_ref, f32[768,256]{1,0:T(8,128)} %fusion.9.qa_ref, ...), custom_call_target="tpu_custom_call", output_to_operand_aliasing={{0}: (9, {}), {1}: (10, {})} | custom-call | flops 1610612736 | bytes 5242880 | tf_op jit(solution)/shard_map/pallas_call | solution.py:165
  139.7 1.0 slice.71
  141.2 0.8 copy-done.1
  142.0 0.7 fusion.1
  143.3 6.8 %collective-permute-done.11 = bf16[768,256]{1,0:T(8,128)(2,1)S(1)} collective-permute-done((bf16[768,256]{1,0:T(8,128)(2,1)S(1)}, bf16[768,256]{1,0:T(8,128)(2,1)S(1)}, u32[]{:S(2)}, u32[]{:S(2)}) %collective-permute-start.11) | collective-permute-done | bytes 393248 | tf_op jit(solution)/shard_map/ppermute | solution.py:240
  150.5 2.0 %copy-done.2 = bf16[2,2048,512]{2,1,0:T(8,128)(2,1)} copy-done((bf16[2,2048,512]{2,1,0:T(8,128)(2,1)}, bf16[2,2048,512]{2,1,0:T(8,128)(2,1)S(1)}, u32[]{:S(2)}) %copy-start.2) | copy-done | bytes 4194328
  (49 shorter events, 4.1 us)
Async XLA Ops:
  0.6 42.3 %copy-start = (bf16[512,256]{1,0:T(8,128)(2,1)S(1)}, bf16[512,256]{1,0:T(8,128)(2,1)}, u32[]{:S(2)}) copy-start(bf16[512,256]{1,0:T(8,128)(2,1)} %param.9) | copy-start | bytes 786436
  0.6 4.5 %copy-start.4 = (bf16[512,256]{1,0:T(8,128)(2,1)S(1)}, bf16[512,256]{1,0:T(8,128)(2,1)}, u32[]{:S(2)}) copy-start(bf16[512,256]{1,0:T(8,128)(2,1)} %param.10) | copy-start | bytes 786436
  5.2 6.1 %collective-permute-start.1 = (bf16[1,272,256]{2,1,0:T(8,128)(2,1)S(1)}, bf16[1,272,256]{2,1,0:T(8,128)(2,1)S(1)}, u32[]{:S(2)}, u32[]{:S(2)}) collective-permute-start(bf16[1,272,256]{2,1,0:T(8,128)(2,1)S(1)} %fusion.12), channel_id=1, source_target_pairs={{0,32},{8,40},{16,48},{24,56},{32,0},{40,8},{48,16},{56,24},{64,96... | collective-permute-start | bytes 417800 | tf_op jit(solution)/shard_map/ppermute | solution.py:203
  6.4 5.7 %collective-permute-start.2 = (bf16[1,272,256]{2,1,0:T(8,128)(2,1)S(1)}, bf16[1,272,256]{2,1,0:T(8,128)(2,1)S(1)}, u32[]{:S(2)}, u32[]{:S(2)}) collective-permute-start(bf16[1,272,256]{2,1,0:T(8,128)(2,1)S(1)} %fusion.12), channel_id=1, source_target_pairs={{0,64},{8,72},{16,80},{24,88},{32,96},{40,104},{48,112},{56,120},{... | collective-permute-start | bytes 417800 | tf_op jit(solution)/shard_map/ppermute | solution.py:203
  6.4 8.8 %collective-permute-start.3 = (bf16[1,272,256]{2,1,0:T(8,128)(2,1)S(1)}, bf16[1,272,256]{2,1,0:T(8,128)(2,1)S(1)}, u32[]{:S(2)}, u32[]{:S(2)}) collective-permute-start(bf16[1,272,256]{2,1,0:T(8,128)(2,1)S(1)} %fusion.12), channel_id=1, source_target_pairs={{0,96},{8,104},{16,112},{24,120},{32,64},{40,72},{48,80},{56,88},{... | collective-permute-start | bytes 417800 | tf_op jit(solution)/shard_map/ppermute | solution.py:203
  15.3 16.2 %collective-permute-start.5 = (bf16[4,272,256]{2,1,0:T(8,128)(2,1)S(1)}, bf16[4,272,256]{2,1,0:T(8,128)(2,1)S(1)}, u32[]{:S(2)}, u32[]{:S(2)}) collective-permute-start(bf16[4,272,256]{2,1,0:T(8,128)(2,1)S(1)} %pad_maximum_fusion), channel_id=1, source_target_pairs={{0,24},{8,16},{16,8},{24,0},{32,56},{40,48},{48,40},{56,32},{64,88... | collective-permute-start | bytes 1671176 | tf_op jit(solution)/shard_map/ppermute | solution.py:203
  19.1 13.3 %collective-permute-start.4 = (bf16[4,272,256]{2,1,0:T(8,128)(2,1)S(1)}, bf16[4,272,256]{2,1,0:T(8,128)(2,1)S(1)}, u32[]{:S(2)}, u32[]{:S(2)}) collective-permute-start(bf16[4,272,256]{2,1,0:T(8,128)(2,1)S(1)} %pad_maximum_fusion), channel_id=1, source_target_pairs={{0,8},{8,0},{16,24},{24,16},{32,40},{40,32},{48,56},{56,48},{64,72... | collective-permute-start | bytes 1671176 | tf_op jit(solution)/shard_map/ppermute | solution.py:203
  31.6 7.1 %collective-permute-start.6 = (bf16[2,272,256]{2,1,0:T(8,128)(2,1)S(1)}, bf16[2,272,256]{2,1,0:T(8,128)(2,1)S(1)}, u32[]{:S(2)}, u32[]{:S(2)}) collective-permute-start(bf16[2,272,256]{2,1,0:T(8,128)(2,1)S(1)} %slice.74), channel_id=1, source_target_pairs={{0,8},{8,0},{16,24},{24,16},{32,40},{40,32},{48,56},{56,48},{64,72... | collective-permute-start | bytes 835592 | tf_op jit(solution)/shard_map/ppermute | solution.py:203
  32.5 7.8 %collective-permute-start.7 = (bf16[2,272,256]{2,1,0:T(8,128)(2,1)S(1)}, bf16[2,272,256]{2,1,0:T(8,128)(2,1)S(1)}, u32[]{:S(2)}, u32[]{:S(2)}) collective-permute-start(bf16[2,272,256]{2,1,0:T(8,128)(2,1)S(1)} %slice.75), channel_id=1, source_target_pairs={{0,24},{8,16},{16,8},{24,0},{32,56},{40,48},{48,40},{56,32},{64,88... | collective-permute-start | bytes 835592 | tf_op jit(solution)/shard_map/ppermute | solution.py:203
  40.3 7.7 %copy-start.3 = (bf16[16,272,256]{2,1,0:T(8,128)(2,1)}, bf16[16,272,256]{2,1,0:T(8,128)(2,1)S(1)}, u32[]{:S(2)}) copy-start(bf16[16,272,256]{2,1,0:T(8,128)(2,1)S(1)} %constant_dynamic-update-slice_fusion.tab_a_ref) | copy-start | bytes 6684676
  40.3 35.6 %collective-permute-start.8 = (bf16[16,272,256]{2,1,0:T(8,128)(2,1)S(1)}, bf16[16,272,256]{2,1,0:T(8,128)(2,1)}, u32[]{:S(2)}, u32[]{:S(2)}) collective-permute-start(bf16[16,272,256]{2,1,0:T(8,128)(2,1)S(1)} %constant_dynamic-update-slice_fusion.tab_a_ref), channel_id=1, source_target_pairs={{0,1},{1,0},{2,3},{3,2},{4,5},{5,4},{6,7},{7,6},{8,9},{9,8},{10,11... | collective-permute-start | bytes 6684680 | tf_op jit(solution)/shard_map/ppermute | solution.py:220
  42.9 6.6 %copy-start.7 = (s32[8,12]{1,0:T(8,128)S(1)}, s32[8,12]{1,0:T(8,128)}, u32[]{:S(2)}) copy-start(s32[8,12]{1,0:T(8,128)} %param.14) | copy-start | bytes 1156
  42.9 7.2 %copy-start.6 = (s32[2048]{0:T(1024)S(1)}, s32[2048]{0:T(1024)}, u32[]{:S(2)}) copy-start(s32[2048]{0:T(1024)} %param.13) | copy-start | bytes 24580
  43.0 8.9 %copy-start.8 = (s32[8]{0:T(128)S(1)}, s32[8]{0:T(128)}, u32[]{:S(2)}) copy-start(s32[8]{0:T(128)} %param.15) | copy-start | bytes 100
  45.9 29.9 %collective-permute-start.9 = (f32[1280,256]{1,0:T(8,128)}, f32[1280,256]{1,0:T(8,128)}, u32[]{:S(2)}, u32[]{:S(2)}) collective-permute-start(f32[1280,256]{1,0:T(8,128)} %fusion.4), channel_id=1, source_target_pairs={{0,64},{64,0},{1,65},{65,1},{2,66},{66,2},{3,67},{67,3},{4,68},{68... | collective-permute-start | bytes 3932168 | tf_op jit(solution)/shard_map/ppermute | solution.py:237
  48.0 68.3 %collective-permute-start = (f32[768,256]{1,0:T(8,128)S(1)}, f32[768,256]{1,0:T(8,128)}, u32[]{:S(2)}, u32[]{:S(2)}) collective-permute-start(f32[768,256]{1,0:T(8,128)S(1)} %fusion.8), channel_id=1, source_target_pairs={{0,64},{64,0},{1,65},{65,1},{2,66},{66,2},{3,67},{67,3},{4,68},{68... | collective-permute-start | bytes 2359304 | tf_op jit(solution)/shard_map/ppermute | solution.py:237
  50.1 57.2 %copy-start.5 = (s32[768]{0:T(1024)}, s32[768]{0:T(1024)S(1)}, u32[]{:S(2)}) copy-start(s32[768]{0:T(1024)S(1)} %slice.56.tgt_ref) | copy-start | bytes 9220
  109.3 33.5 %collective-permute-start.10 = (bf16[1280,256]{1,0:T(8,128)(2,1)}, bf16[1280,256]{1,0:T(8,128)(2,1)S(1)}, u32[]{:S(2)}, u32[]{:S(2)}) collective-permute-start(bf16[1280,256]{1,0:T(8,128)(2,1)} %slice.70), channel_id=1, source_target_pairs={{0,64},{64,0},{1,65},{65,1},{2,66},{66,2},{3,67},{67,3},{4,68},{68... | collective-permute-start | bytes 1966088 | tf_op jit(solution)/shard_map/ppermute | solution.py:240
  140.8 1.2 copy-start.1
  140.8 9.3 %collective-permute-start.11 = (bf16[768,256]{1,0:T(8,128)(2,1)S(1)}, bf16[768,256]{1,0:T(8,128)(2,1)S(1)}, u32[]{:S(2)}, u32[]{:S(2)}) collective-permute-start(bf16[768,256]{1,0:T(8,128)(2,1)S(1)} %slice.71), channel_id=1, source_target_pairs={{0,64},{64,0},{1,65},{65,1},{2,66},{66,2},{3,67},{67,3},{4,68},{68... | collective-permute-start | bytes 1179656 | tf_op jit(solution)/shard_map/ppermute | solution.py:240
  150.5 2.0 %copy-start.2 = (bf16[2,2048,512]{2,1,0:T(8,128)(2,1)}, bf16[2,2048,512]{2,1,0:T(8,128)(2,1)S(1)}, u32[]{:S(2)}) copy-start(bf16[2,2048,512]{2,1,0:T(8,128)(2,1)S(1)} %fusion.7) | copy-start | bytes 12582916

commit v10 on v9

--- a/solution.py
+++ b/solution.py
@@ -234,8 +234,10 @@
     for c in range(n_chunks):
         rows = slice(bounds[c], bounds[c + 1])
         blocks = slice(bounds[c] // BLOCK, bounds[c + 1] // BLOCK)
-        sent = lax.ppermute(project(their_rows[rows]), "section", partner)
-        outs = score(project(mine_rows[rows]), sent, target_slot[rows], block_lists[blocks], list_lens[blocks],
+        theirs = project(their_rows[rows])
+        mine = project(mine_rows[rows])
+        sent = lax.ppermute(theirs, "section", partner)
+        outs = score(mine, sent, target_slot[rows], block_lists[blocks], list_lens[blocks],
                      buf, tab_b, parity, tuple(aways), bounds[c], rows_dev, outs)
         others.append(lax.ppermute(outs[0][rows], "section", partner))
     query_grad, loss_rows = outs

time: 153 us -> 153 us (level)
  no operation moved by 1% of the time
where the time goes in v10:
time: 153 us
  Pallas kernels  54.9 us (36%)
  waiting for transfers between devices  52.2 us (34%)
  starting transfers between devices  17.9 us (12%)
  local copies, waits for them, and re-layouts  13.8 us (9%)
  matrix products  11.4 us (7%)
    pallas_call x2, Pallas kernels, score(): pl.pallas_call(functools.partial(score_kernel, list_width, n_blocks, away...  54.9 us
    ppermute x7, waiting for transfers between devices, swap(): return lax.ppermute(x, group, [(i, i ^ d) for i in range(n_group)])  25.8 us
    ppermute x2, waiting for transfers between devices, shards(): sent = lax.ppermute(theirs, 'section', partner)  19.6 us
    dot_general x4, matrix products, project(): return jnp.dot(x, w_proj, preferred_element_type=jnp.float32)  9.74 us
    ppermute x7, starting transfers between devices, swap(): return lax.ppermute(x, group, [(i, i ^ d) for i in range(n_group)])  8.98 us
    ppermute x2, waiting for transfers between devices, shards(): others.append(lax.ppermute(outs[0][rows], 'section', partner))  6.81 us
    ppermute x2, starting transfers between devices, shards(): others.append(lax.ppermute(outs[0][rows], 'section', partner))  4.72 us
    gather x1, local copies, waits for them, and re-layouts, shards(): counts[cand_ids].astype(jnp.float32)  3.63 us
  transfers between devices with their start and end apart: 12, of which 9 were waited for; matrix products, arithmetic and copies ran while one was open for 12% of the time, Pallas kernels for 36%

profile of v10, /device:TPU:7, one launch (start us, length us, event | category | flops | bytes accessed | tf_op | source)
XLA Modules:
  0.0 152.5 jit_solution(9603821341094860549)
XLA Ops:
  0.7 0.7 compare_select_fusion
  1.4 3.6 %gather_fusion = s32[512]{0:T(512)S(1)} fusion(s32[65536]{0:T(1024)} %param.12, s32[1024]{0:T(1024)S(1)} %pad_clamp_fusion), kind=kCustom, calls=%fused_computation | custom fusion | bytes 6144 | tf_op jit(solution)/shard_map/gather | solution.py:194
  5.2 1.2 collective-permute-start.1
  6.4 2.1 %collective-permute-start.3 = (bf16[1,272,256]{2,1,0:T(8,128)(2,1)S(1)}, bf16[1,272,256]{2,1,0:T(8,128)(2,1)S(1)}, u32[]{:S(2)}, u32[]{:S(2)}) collective-permute-start(bf16[1,272,256]{2,1,0:T(8,128)(2,1)S(1)} %fusion.12), channel_id=1, source_target_pairs={{0,96},{8,104},{16,112},{24,120},{32,64},{40,72},{48,80},{56,88},{... | collective-permute-start | bytes 417800 | tf_op jit(solution)/shard_map/ppermute | solution.py:203
  8.5 2.8 %collective-permute-done.1 = bf16[1,272,256]{2,1,0:T(8,128)(2,1)S(1)} collective-permute-done((bf16[1,272,256]{2,1,0:T(8,128)(2,1)S(1)}, bf16[1,272,256]{2,1,0:T(8,128)(2,1)S(1)}, u32[]{:S(2)}, u32[]{:S(2)}) %collective-permute-start.1) | collective-permute-done | bytes 139296 | tf_op jit(solution)/shard_map/ppermute | solution.py:203
  11.3 0.8 collective-permute-done.2
  12.1 3.2 %collective-permute-done.3 = bf16[1,272,256]{2,1,0:T(8,128)(2,1)S(1)} collective-permute-done((bf16[1,272,256]{2,1,0:T(8,128)(2,1)S(1)}, bf16[1,272,256]{2,1,0:T(8,128)(2,1)S(1)}, u32[]{:S(2)}, u32[]{:S(2)}) %collective-permute-start.3) | collective-permute-done | bytes 139296 | tf_op jit(solution)/shard_map/ppermute | solution.py:203
  15.3 3.8 %collective-permute-start.5 = (bf16[4,272,256]{2,1,0:T(8,128)(2,1)S(1)}, bf16[4,272,256]{2,1,0:T(8,128)(2,1)S(1)}, u32[]{:S(2)}, u32[]{:S(2)}) collective-permute-start(bf16[4,272,256]{2,1,0:T(8,128)(2,1)S(1)} %pad_maximum_fusion), channel_id=1, source_target_pairs={{0,24},{8,16},{16,8},{24,0},{32,56},{40,48},{48,40},{56,32},{64,88... | collective-permute-start | bytes 1671176 | tf_op jit(solution)/shard_map/ppermute | solution.py:203
  19.2 12.4 %collective-permute-done.5 = bf16[4,272,256]{2,1,0:T(8,128)(2,1)S(1)} collective-permute-done((bf16[4,272,256]{2,1,0:T(8,128)(2,1)S(1)}, bf16[4,272,256]{2,1,0:T(8,128)(2,1)S(1)}, u32[]{:S(2)}, u32[]{:S(2)}) %collective-permute-start.5) | collective-permute-done | bytes 557088 | tf_op jit(solution)/shard_map/ppermute | solution.py:203
  31.7 0.8 collective-permute-done.4
  32.5 1.7 %collective-permute-start.7 = (bf16[2,272,256]{2,1,0:T(8,128)(2,1)S(1)}, bf16[2,272,256]{2,1,0:T(8,128)(2,1)S(1)}, u32[]{:S(2)}, u32[]{:S(2)}) collective-permute-start(bf16[2,272,256]{2,1,0:T(8,128)(2,1)S(1)} %slice.75), channel_id=1, source_target_pairs={{0,24},{8,16},{16,8},{24,0},{32,56},{40,48},{48,40},{56,32},{64,88... | collective-permute-start | bytes 835592 | tf_op jit(solution)/shard_map/ppermute | solution.py:203
  34.3 4.4 %collective-permute-done.6 = bf16[2,272,256]{2,1,0:T(8,128)(2,1)S(1)} collective-permute-done((bf16[2,272,256]{2,1,0:T(8,128)(2,1)S(1)}, bf16[2,272,256]{2,1,0:T(8,128)(2,1)S(1)}, u32[]{:S(2)}, u32[]{:S(2)}) %collective-permute-start.6) | collective-permute-done | bytes 278560 | tf_op jit(solution)/shard_map/ppermute | solution.py:203
  38.7 1.5 %collective-permute-done.7 = bf16[2,272,256]{2,1,0:T(8,128)(2,1)S(1)} collective-permute-done((bf16[2,272,256]{2,1,0:T(8,128)(2,1)S(1)}, bf16[2,272,256]{2,1,0:T(8,128)(2,1)S(1)}, u32[]{:S(2)}, u32[]{:S(2)}) %collective-permute-start.7) | collective-permute-done | bytes 278560 | tf_op jit(solution)/shard_map/ppermute | solution.py:203
  40.3 2.7 %collective-permute-start.8 = (bf16[16,272,256]{2,1,0:T(8,128)(2,1)S(1)}, bf16[16,272,256]{2,1,0:T(8,128)(2,1)}, u32[]{:S(2)}, u32[]{:S(2)}) collective-permute-start(bf16[16,272,256]{2,1,0:T(8,128)(2,1)S(1)} %constant_dynamic-update-slice_fusion.tab_a_ref), channel_id=1, source_target_pairs={{0,1},{1,0},{2,3},{3,2},{4,5},{5,4},{6,7},{7,6},{8,9},{9,8},{10,11... | collective-permute-start | bytes 6684680 | tf_op jit(solution)/shard_map/ppermute | solution.py:220
  43.0 2.9 %fusion.4 = f32[1280,256]{1,0:T(8,128)} fusion(bf16[512,256]{1,0:T(8,128)(2,1)S(1)} %copy-done, bf16[2,2048,512]{2,1,0:T(8,128)(2,1)} %param.8, s32[]{:T(128)S(6)} %select_n.28), kind=kOutput, calls=%fused_computation.9 | convolution fusion | flops 335544320 | bytes 2883588 | tf_op jit(solution)/shard_map/dot_general | solution.py:226
  46.5 1.5 fusion.8
  48.0 1.0 collective-permute-start
  50.1 1.1 reshape.45.tcol_ref
  51.2 0.6 reshape.30.lists_ref
  52.4 0.9 reshape.44.tcol_ref
  53.3 2.9 %fusion.5.qa_ref = f32[1280,256]{1,0:T(8,128)} fusion(bf16[512,256]{1,0:T(8,128)(2,1)S(1)} %copy-done, bf16[2,2048,512]{2,1,0:T(8,128)(2,1)} %param.8, s32[]{:T(128)S(6)} %select_n.27), kind=kOutput, calls=%fused_computation.11 | convolution fusion | flops 335544320 | bytes 2883588 | tf_op jit(solution)/shard_map/dot_general | solution.py:226
  56.2 19.6 %collective-permute-done.9.qb_ref = f32[1280,256]{1,0:T(8,128)} collective-permute-done((f32[1280,256]{1,0:T(8,128)}, f32[1280,256]{1,0:T(8,128)}, u32[]{:S(2)}, u32[]{:S(2)}) %collective-permute-start.9) | collective-permute-done | bytes 1310752 | tf_op jit(solution)/shard_map/ppermute | solution.py:239
  75.8 31.5 %shard_map.103 = (bf16[2048,256]{1,0:T(8,128)(2,1)}, f32[8,1,256]{2,1,0:T(1,128)}) custom-call(s32[60]{0:T(128)} %reshape.32.lists_ref, s32[5]{0:T(128)} %bitcast.48, s32[1280]{0:T(1024)} %bitcast.44, s32[2]{0:T(128)} %pad_add_fusion.par_ref, f32[1280,256]{1,0:T(8,128)} %fusion.5.qa_ref, f32[1280,256]{1,0:T(8,128)} %collective-permute-done.9.qb_ref, ...), custom_call_target="tpu_custom_call" | custom-call | flops 2684354560 | bytes 5767168 | tf_op jit(solution)/shard_map/pallas_call | solution.py:165
  107.3 2.0 %slice.70 = bf16[1280,256]{1,0:T(8,128)(2,1)} slice(bf16[2048,256]{1,0:T(8,128)(2,1)} %get-tuple-element.7.refs_0_), slice={[0:1280], [0:256]} | slice | bytes 1310720 | tf_op jit(solution)/shard_map/slice | solution.py:242
  109.3 4.6 %collective-permute-start.10 = (bf16[1280,256]{1,0:T(8,128)(2,1)}, bf16[1280,256]{1,0:T(8,128)(2,1)S(1)}, u32[]{:S(2)}, u32[]{:S(2)}) collective-permute-start(bf16[1280,256]{1,0:T(8,128)(2,1)} %slice.70), channel_id=1, source_target_pairs={{0,64},{64,0},{1,65},{65,1},{2,66},{66,2},{3,67},{67,3},{4,68},{68... | collective-permute-start | bytes 1966088 | tf_op jit(solution)/shard_map/ppermute | solution.py:242
  113.9 2.4 %fusion.9.qa_ref = f32[768,256]{1,0:T(8,128)} fusion(bf16[512,256]{1,0:T(8,128)(2,1)S(1)} %copy-done, bf16[2,2048,512]{2,1,0:T(8,128)(2,1)} %param.8, s32[]{:T(128)S(6)} %select_n.27, s32[]{:T(128)S(6)} %add.41), kind=kOutput, calls=%fused_computation.17 | convolution fusion | flops 201326592 | bytes 1835016 | tf_op jit(solution)/shard_map/dot_general | solution.py:226
  116.3 23.4 %shard_map.104 = (bf16[2048,256]{1,0:T(8,128)(2,1)}, f32[8,1,256]{2,1,0:T(1,128)}) custom-call(s32[36]{0:T(128)} %reshape.30.lists_ref, s32[3]{0:T(128)} %slice.55.lens_ref, s32[768]{0:T(1024)} %copy-done.5, s32[2]{0:T(128)} %pad_add_fusion.par_ref, f32[768,256]{1,0:T(8,128)} %fusion.9.qa_ref, ...), custom_call_target="tpu_custom_call", output_to_operand_aliasing={{0}: (9, {}), {1}: (10, {})} | custom-call | flops 1610612736 | bytes 5242880 | tf_op jit(solution)/shard_map/pallas_call | solution.py:165
  139.7 1.0 slice.71
  141.2 0.8 copy-done.1
  142.0 0.7 fusion.1
  143.3 6.8 %collective-permute-done.11 = bf16[768,256]{1,0:T(8,128)(2,1)S(1)} collective-permute-done((bf16[768,256]{1,0:T(8,128)(2,1)S(1)}, bf16[768,256]{1,0:T(8,128)(2,1)S(1)}, u32[]{:S(2)}, u32[]{:S(2)}) %collective-permute-start.11) | collective-permute-done | bytes 393248 | tf_op jit(solution)/shard_map/ppermute | solution.py:242
  150.5 2.0 %copy-done.2 = bf16[2,2048,512]{2,1,0:T(8,128)(2,1)} copy-done((bf16[2,2048,512]{2,1,0:T(8,128)(2,1)}, bf16[2,2048,512]{2,1,0:T(8,128)(2,1)S(1)}, u32[]{:S(2)}) %copy-start.2) | copy-done | bytes 4194328
  (49 shorter events, 4.1 us)
Async XLA Ops:
  0.6 42.3 %copy-start = (bf16[512,256]{1,0:T(8,128)(2,1)S(1)}, bf16[512,256]{1,0:T(8,128)(2,1)}, u32[]{:S(2)}) copy-start(bf16[512,256]{1,0:T(8,128)(2,1)} %param.9) | copy-start | bytes 786436
  0.6 4.5 %copy-start.4 = (bf16[512,256]{1,0:T(8,128)(2,1)S(1)}, bf16[512,256]{1,0:T(8,128)(2,1)}, u32[]{:S(2)}) copy-start(bf16[512,256]{1,0:T(8,128)(2,1)} %param.10) | copy-start | bytes 786436
  5.2 6.1 %collective-permute-start.1 = (bf16[1,272,256]{2,1,0:T(8,128)(2,1)S(1)}, bf16[1,272,256]{2,1,0:T(8,128)(2,1)S(1)}, u32[]{:S(2)}, u32[]{:S(2)}) collective-permute-start(bf16[1,272,256]{2,1,0:T(8,128)(2,1)S(1)} %fusion.12), channel_id=1, source_target_pairs={{0,32},{8,40},{16,48},{24,56},{32,0},{40,8},{48,16},{56,24},{64,96... | collective-permute-start | bytes 417800 | tf_op jit(solution)/shard_map/ppermute | solution.py:203
  6.4 5.7 %collective-permute-start.2 = (bf16[1,272,256]{2,1,0:T(8,128)(2,1)S(1)}, bf16[1,272,256]{2,1,0:T(8,128)(2,1)S(1)}, u32[]{:S(2)}, u32[]{:S(2)}) collective-permute-start(bf16[1,272,256]{2,1,0:T(8,128)(2,1)S(1)} %fusion.12), channel_id=1, source_target_pairs={{0,64},{8,72},{16,80},{24,88},{32,96},{40,104},{48,112},{56,120},{... | collective-permute-start | bytes 417800 | tf_op jit(solution)/shard_map/ppermute | solution.py:203
  6.4 8.8 %collective-permute-start.3 = (bf16[1,272,256]{2,1,0:T(8,128)(2,1)S(1)}, bf16[1,272,256]{2,1,0:T(8,128)(2,1)S(1)}, u32[]{:S(2)}, u32[]{:S(2)}) collective-permute-start(bf16[1,272,256]{2,1,0:T(8,128)(2,1)S(1)} %fusion.12), channel_id=1, source_target_pairs={{0,96},{8,104},{16,112},{24,120},{32,64},{40,72},{48,80},{56,88},{... | collective-permute-start | bytes 417800 | tf_op jit(solution)/shard_map/ppermute | solution.py:203
  15.3 16.2 %collective-permute-start.5 = (bf16[4,272,256]{2,1,0:T(8,128)(2,1)S(1)}, bf16[4,272,256]{2,1,0:T(8,128)(2,1)S(1)}, u32[]{:S(2)}, u32[]{:S(2)}) collective-permute-start(bf16[4,272,256]{2,1,0:T(8,128)(2,1)S(1)} %pad_maximum_fusion), channel_id=1, source_target_pairs={{0,24},{8,16},{16,8},{24,0},{32,56},{40,48},{48,40},{56,32},{64,88... | collective-permute-start | bytes 1671176 | tf_op jit(solution)/shard_map/ppermute | solution.py:203
  19.1 13.3 %collective-permute-start.4 = (bf16[4,272,256]{2,1,0:T(8,128)(2,1)S(1)}, bf16[4,272,256]{2,1,0:T(8,128)(2,1)S(1)}, u32[]{:S(2)}, u32[]{:S(2)}) collective-permute-start(bf16[4,272,256]{2,1,0:T(8,128)(2,1)S(1)} %pad_maximum_fusion), channel_id=1, source_target_pairs={{0,8},{8,0},{16,24},{24,16},{32,40},{40,32},{48,56},{56,48},{64,72... | collective-permute-start | bytes 1671176 | tf_op jit(solution)/shard_map/ppermute | solution.py:203
  31.6 7.1 %collective-permute-start.6 = (bf16[2,272,256]{2,1,0:T(8,128)(2,1)S(1)}, bf16[2,272,256]{2,1,0:T(8,128)(2,1)S(1)}, u32[]{:S(2)}, u32[]{:S(2)}) collective-permute-start(bf16[2,272,256]{2,1,0:T(8,128)(2,1)S(1)} %slice.74), channel_id=1, source_target_pairs={{0,8},{8,0},{16,24},{24,16},{32,40},{40,32},{48,56},{56,48},{64,72... | collective-permute-start | bytes 835592 | tf_op jit(solution)/shard_map/ppermute | solution.py:203
  32.5 7.8 %collective-permute-start.7 = (bf16[2,272,256]{2,1,0:T(8,128)(2,1)S(1)}, bf16[2,272,256]{2,1,0:T(8,128)(2,1)S(1)}, u32[]{:S(2)}, u32[]{:S(2)}) collective-permute-start(bf16[2,272,256]{2,1,0:T(8,128)(2,1)S(1)} %slice.75), channel_id=1, source_target_pairs={{0,24},{8,16},{16,8},{24,0},{32,56},{40,48},{48,40},{56,32},{64,88... | collective-permute-start | bytes 835592 | tf_op jit(solution)/shard_map/ppermute | solution.py:203
  40.3 7.7 %copy-start.3 = (bf16[16,272,256]{2,1,0:T(8,128)(2,1)}, bf16[16,272,256]{2,1,0:T(8,128)(2,1)S(1)}, u32[]{:S(2)}) copy-start(bf16[16,272,256]{2,1,0:T(8,128)(2,1)S(1)} %constant_dynamic-update-slice_fusion.tab_a_ref) | copy-start | bytes 6684676
  40.3 35.6 %collective-permute-start.8 = (bf16[16,272,256]{2,1,0:T(8,128)(2,1)S(1)}, bf16[16,272,256]{2,1,0:T(8,128)(2,1)}, u32[]{:S(2)}, u32[]{:S(2)}) collective-permute-start(bf16[16,272,256]{2,1,0:T(8,128)(2,1)S(1)} %constant_dynamic-update-slice_fusion.tab_a_ref), channel_id=1, source_target_pairs={{0,1},{1,0},{2,3},{3,2},{4,5},{5,4},{6,7},{7,6},{8,9},{9,8},{10,11... | collective-permute-start | bytes 6684680 | tf_op jit(solution)/shard_map/ppermute | solution.py:220
  42.9 6.6 %copy-start.7 = (s32[8,12]{1,0:T(8,128)S(1)}, s32[8,12]{1,0:T(8,128)}, u32[]{:S(2)}) copy-start(s32[8,12]{1,0:T(8,128)} %param.14) | copy-start | bytes 1156
  42.9 7.2 %copy-start.6 = (s32[2048]{0:T(1024)S(1)}, s32[2048]{0:T(1024)}, u32[]{:S(2)}) copy-start(s32[2048]{0:T(1024)} %param.13) | copy-start | bytes 24580
  43.0 8.9 %copy-start.8 = (s32[8]{0:T(128)S(1)}, s32[8]{0:T(128)}, u32[]{:S(2)}) copy-start(s32[8]{0:T(128)} %param.15) | copy-start | bytes 100
  45.9 29.9 %collective-permute-start.9 = (f32[1280,256]{1,0:T(8,128)}, f32[1280,256]{1,0:T(8,128)}, u32[]{:S(2)}, u32[]{:S(2)}) collective-permute-start(f32[1280,256]{1,0:T(8,128)} %fusion.4), channel_id=1, source_target_pairs={{0,64},{64,0},{1,65},{65,1},{2,66},{66,2},{3,67},{67,3},{4,68},{68... | collective-permute-start | bytes 3932168 | tf_op jit(solution)/shard_map/ppermute | solution.py:239
  48.0 68.3 %collective-permute-start = (f32[768,256]{1,0:T(8,128)S(1)}, f32[768,256]{1,0:T(8,128)}, u32[]{:S(2)}, u32[]{:S(2)}) collective-permute-start(f32[768,256]{1,0:T(8,128)S(1)} %fusion.8), channel_id=1, source_target_pairs={{0,64},{64,0},{1,65},{65,1},{2,66},{66,2},{3,67},{67,3},{4,68},{68... | collective-permute-start | bytes 2359304 | tf_op jit(solution)/shard_map/ppermute | solution.py:239
  50.1 57.2 %copy-start.5 = (s32[768]{0:T(1024)}, s32[768]{0:T(1024)S(1)}, u32[]{:S(2)}) copy-start(s32[768]{0:T(1024)S(1)} %slice.56.tgt_ref) | copy-start | bytes 9220
  109.3 33.5 %collective-permute-start.10 = (bf16[1280,256]{1,0:T(8,128)(2,1)}, bf16[1280,256]{1,0:T(8,128)(2,1)S(1)}, u32[]{:S(2)}, u32[]{:S(2)}) collective-permute-start(bf16[1280,256]{1,0:T(8,128)(2,1)} %slice.70), channel_id=1, source_target_pairs={{0,64},{64,0},{1,65},{65,1},{2,66},{66,2},{3,67},{67,3},{4,68},{68... | collective-permute-start | bytes 1966088 | tf_op jit(solution)/shard_map/ppermute | solution.py:242
  140.8 1.2 copy-start.1
  140.8 9.3 %collective-permute-start.11 = (bf16[768,256]{1,0:T(8,128)(2,1)S(1)}, bf16[768,256]{1,0:T(8,128)(2,1)S(1)}, u32[]{:S(2)}, u32[]{:S(2)}) collective-permute-start(bf16[768,256]{1,0:T(8,128)(2,1)S(1)} %slice.71), channel_id=1, source_target_pairs={{0,64},{64,0},{1,65},{65,1},{2,66},{66,2},{3,67},{67,3},{4,68},{68... | collective-permute-start | bytes 1179656 | tf_op jit(solution)/shard_map/ppermute | solution.py:242
  150.5 2.0 %copy-start.2 = (bf16[2,2048,512]{2,1,0:T(8,128)(2,1)}, bf16[2,2048,512]{2,1,0:T(8,128)(2,1)S(1)}, u32[]{:S(2)}) copy-start(bf16[2,2048,512]{2,1,0:T(8,128)(2,1)S(1)} %fusion.7) | copy-start | bytes 12582916

commit v11 on v10

--- a/solution.py
+++ b/solution.py
@@ -15,27 +15,28 @@
 EXT = BLOCK + 128
 
 
-def score_kernel(list_width, n_blocks, aways, n_prev,
+def score_kernel(list_width, n_blocks, aways, n_prev, first,
                  lists_ref, lens_ref, tgt_ref, par_ref,
                  qa_ref, qb_ref, tcol_ref, tab_a_ref, tab_b_ref, *refs):
-    (qg_ref, loss_ref, tabb_ref, tabf_ref, bias_ref, pos_ref, ls_ref, acc_ref, sem) = refs[n_prev:]
-    _score_body(list_width, n_blocks, aways, lists_ref, lens_ref, tgt_ref, par_ref,
-                qa_ref, qb_ref, tcol_ref, tab_a_ref, tab_b_ref, qg_ref, loss_ref,
+    (qg_ref, loss_ref, qgc_ref, tabb_ref, tabf_ref, bias_ref, pos_ref, ls_ref, acc_ref, sem) = refs[n_prev:]
+    _score_body(list_width, n_blocks, aways, first, lists_ref, lens_ref, tgt_ref, par_ref,
+                qa_ref, qb_ref, tcol_ref, tab_a_ref, tab_b_ref, qg_ref, loss_ref, qgc_ref,
                 tabb_ref, tabf_ref, bias_ref, pos_ref, ls_ref, acc_ref, sem)
 
 
-def _score_body(list_width, n_blocks, aways,
+def _score_body(list_width, n_blocks, aways, first,
                  lists_ref, lens_ref, tgt_ref, par_ref,
                  qa_ref, qb_ref, tcol_ref, tab_a_ref, tab_b_ref,
-                 qg_ref, loss_ref,
+                 qg_ref, loss_ref, qgc_ref,
                  tabb_ref, tabf_ref, bias_ref, pos_ref, ls_ref, acc_ref, sem):
     b = pl.program_id(0)
+    bg = b + first
     n_shards = tab_a_ref.shape[0]
     n_cand_blocks = 2 * n_shards
 
     def issue(block, slot):
         def one(r, carry):
-            t = tgt_ref[block * BLOCK + r]
+            t = tgt_ref[(first + block) * BLOCK + r]
             pltpu.make_async_copy(tabf_ref.at[pl.ds(t, 1), :], pos_ref.at[slot, pl.ds(r, 1), :],
                                   sem.at[slot]).start()
             return carry
@@ -75,7 +76,7 @@
     qf = q.astype(jnp.float32)
     tcol = tcol_ref[...]
     lane = lax.broadcasted_iota(jnp.int32, (BLOCK, BLOCK), 1)
-    length = lens_ref[b]
+    length = lens_ref[bg]
     n_groups = (length + GROUP - 1) // GROUP
 
     pltpu.make_async_copy(pos_ref.at[slot], pos_ref.at[slot], sem.at[slot]).wait()
@@ -86,7 +87,7 @@
     def pass_a(g, m):
         for i in range(GROUP):
             k = g * GROUP + i
-            j = lists_ref[b * list_width + k]
+            j = lists_ref[bg * list_width + k]
             cand = tabb_ref[j]
             logits = lax.dot_general(q, cand, (((1,), (1,)), ((), ())),
                                      preferred_element_type=jnp.float32) - bias_ref[pl.ds(j, 1), :]
@@ -113,7 +114,7 @@
         part = None
         for i in range(GROUP):
             k = g * GROUP + i
-            j = lists_ref[b * list_width + k]
+            j = lists_ref[bg * list_width + k]
             w = jnp.exp(ls_ref[k] - log_total).astype(jnp.bfloat16)
             d = jnp.dot(w, tabb_ref[j], preferred_element_type=jnp.float32)
             part = d if part is None else part + d
@@ -123,6 +124,7 @@
     lax.fori_loop(0, n_groups, pass_c, 0)
     qg = acc_ref[...] + (jnp.exp(pos_logit - log_total) - 1.0) * positive
     qg_ref[...] = qg.astype(qg_ref.dtype)
+    qgc_ref[...] = qg.astype(qgc_ref.dtype)
     loss_col = jnp.broadcast_to(log_total - pos_logit, (BLOCK, 128))
     loss_ref[...] = jnp.transpose(loss_col)[0:1, :].reshape(loss_ref.shape)
 
@@ -142,13 +144,14 @@
         in_specs=[
             pl.BlockSpec((BLOCK, embed), lambda b, *_: (b, 0)),
             pl.BlockSpec((BLOCK, embed), lambda b, *_: (b, 0)),
-            pl.BlockSpec((BLOCK, 1), lambda b, *_: (b, 0)),
+            pl.BlockSpec((BLOCK, 1), lambda b, *_: (b + first, 0)),
             pl.BlockSpec(memory_space=pltpu.VMEM),
             pl.BlockSpec(memory_space=pltpu.VMEM),
         ] + [pl.BlockSpec(memory_space=pl.ANY)] * len(prev),
         out_specs=[
             pl.BlockSpec((BLOCK, embed), lambda b, *_: (b + first, 0)),
             pl.BlockSpec((1, 1, BLOCK), lambda b, *_: (b + first, 0, 0)),
+            pl.BlockSpec((BLOCK, embed), lambda b, *_: (b, 0)),
         ],
         scratch_shapes=[
             pltpu.VMEM((2 * n_shards, BLOCK, embed), jnp.bfloat16),
@@ -162,12 +165,13 @@
     )
     flops = 2 * 2 * rows * embed * BLOCK * 8
     n_in = 4 + 5
-    qg, loss = pl.pallas_call(
-        functools.partial(score_kernel, list_width, n_blocks, aways, len(prev)),
+    qg, loss, qg_chunk = pl.pallas_call(
+        functools.partial(score_kernel, list_width, n_blocks, aways, len(prev), first),
         grid_spec=grid_spec,
         out_shape=[
             jax.ShapeDtypeStruct((total_rows, embed), jnp.bfloat16),
             jax.ShapeDtypeStruct((total_rows // BLOCK, 1, BLOCK), jnp.float32),
+            jax.ShapeDtypeStruct((rows, embed), jnp.bfloat16),
         ],
         input_output_aliases={n_in + i: i for i in range(len(prev))},
         compiler_params=pltpu.CompilerParams(
@@ -178,8 +182,8 @@
             flops=flops, transcendentals=2 * rows * BLOCK * 8,
             bytes_accessed=2 * tab_a.size * 2 + rows * embed * 4),
     )(block_lists.reshape(-1), list_lens, target_slot, parity,
-      q_mine, q_sent, target_slot.reshape(rows, 1), tab_a, tab_b, *prev)
-    return qg, loss
+      q_mine, q_sent, target_slot.reshape(total_rows, 1), tab_a, tab_b, *prev)
+    return (qg, loss), qg_chunk
 
 
 def shards(hidden_rows, w_proj, panels, cand_ids, counts, target_slot, block_lists, list_lens):
@@ -233,13 +237,12 @@
     others = []
     for c in range(n_chunks):
         rows = slice(bounds[c], bounds[c + 1])
-        blocks = slice(bounds[c] // BLOCK, bounds[c + 1] // BLOCK)
         theirs = project(their_rows[rows])
         mine = project(mine_rows[rows])
         sent = lax.ppermute(theirs, "section", partner)
-        outs = score(mine, sent, target_slot[rows], block_lists[blocks], list_lens[blocks],
-                     buf, tab_b, parity, tuple(aways), bounds[c], rows_dev, outs)
-        others.append(lax.ppermute(outs[0][rows], "section", partner))
+        outs, grad = score(mine, sent, target_slot, block_lists, list_lens,
+                           buf, tab_b, parity, tuple(aways), bounds[c], rows_dev, outs)
+        others.append(lax.ppermute(grad, "section", partner))
     query_grad, loss_rows = outs
     position_loss = loss_rows.reshape(rows_dev)
 

time: 153 us -> 152 us (level)
  local copies, waits for them, and re-layouts: 13.8 us -> 9.96 us
    slice x5 -> x0, local copies, waits for them, and re-layouts: 3.59 us -> none  [the longest x2 3 us: shards(): others.append(lax.ppermute(outs[0][rows], 'section', partner))]
    unnamed x24 -> x22, local copies, waits for them, and re-layouts: 3.02 us -> 3.92 us
  transfers between devices with their start and end apart: 12 -> 12, of which waited for: 9 -> 9; matrix products, arithmetic and copies ran while one was open for 12% -> 10% of each run, Pallas kernels for 36% -> 37%
where the time goes in v11:
time: 152 us; the launch traced here: 151 us
  Pallas kernels  55.4 us (36%)
  waiting for transfers between devices  53.3 us (35%)
  starting transfers between devices  18.1 us (12%)
  matrix products  12.3 us (8%)
  local copies, waits for them, and re-layouts  9.96 us (7%)
    pallas_call x2, Pallas kernels, score(): pl.pallas_call(functools.partial(score_kernel, list_width, n_blocks, away...  55.4 us
    ppermute x7, waiting for transfers between devices, swap(): return lax.ppermute(x, group, [(i, i ^ d) for i in range(n_group)])  25.8 us
    ppermute x2, waiting for transfers between devices, shards(): sent = lax.ppermute(theirs, 'section', partner)  20.5 us
    dot_general x4, matrix products, project(): return jnp.dot(x, w_proj, preferred_element_type=jnp.float32)  10.6 us
    ppermute x7, starting transfers between devices, swap(): return lax.ppermute(x, group, [(i, i ^ d) for i in range(n_group)])  8.98 us
    ppermute x2, waiting for transfers between devices, shards(): others.append(lax.ppermute(grad, 'section', partner))  7.03 us
    ppermute x2, starting transfers between devices, shards(): others.append(lax.ppermute(grad, 'section', partner))  4.99 us
    unnamed x22, local copies, waits for them, and re-layouts  3.92 us
  transfers between devices with their start and end apart: 12, of which 9 were waited for; matrix products, arithmetic and copies ran while one was open for 10% of the time, Pallas kernels for 37%

profile of v11, /device:TPU:7, one launch (start us, length us, event | category | flops | bytes accessed | tf_op | source)
XLA Modules:
  0.0 151.3 jit_solution(12574023241601514912)
XLA Ops:
  0.7 0.8 compare_select_fusion
  1.4 3.6 %gather_fusion = s32[512]{0:T(512)S(1)} fusion(s32[65536]{0:T(1024)} %param.12, s32[1024]{0:T(1024)S(1)} %pad_clamp_fusion), kind=kCustom, calls=%fused_computation | custom fusion | bytes 6144 | tf_op jit(solution)/shard_map/gather | solution.py:198
  5.2 1.2 collective-permute-start.1
  6.4 2.1 %collective-permute-start.3 = (bf16[1,272,256]{2,1,0:T(8,128)(2,1)S(1)}, bf16[1,272,256]{2,1,0:T(8,128)(2,1)S(1)}, u32[]{:S(2)}, u32[]{:S(2)}) collective-permute-start(bf16[1,272,256]{2,1,0:T(8,128)(2,1)S(1)} %fusion.12), channel_id=1, source_target_pairs={{0,96},{8,104},{16,112},{24,120},{32,64},{40,72},{48,80},{56,88},{... | collective-permute-start | bytes 417800 | tf_op jit(solution)/shard_map/ppermute | solution.py:207
  8.5 2.8 %collective-permute-done.1 = bf16[1,272,256]{2,1,0:T(8,128)(2,1)S(1)} collective-permute-done((bf16[1,272,256]{2,1,0:T(8,128)(2,1)S(1)}, bf16[1,272,256]{2,1,0:T(8,128)(2,1)S(1)}, u32[]{:S(2)}, u32[]{:S(2)}) %collective-permute-start.1) | collective-permute-done | bytes 139296 | tf_op jit(solution)/shard_map/ppermute | solution.py:207
  11.3 0.8 collective-permute-done.2
  12.1 3.2 %collective-permute-done.3 = bf16[1,272,256]{2,1,0:T(8,128)(2,1)S(1)} collective-permute-done((bf16[1,272,256]{2,1,0:T(8,128)(2,1)S(1)}, bf16[1,272,256]{2,1,0:T(8,128)(2,1)S(1)}, u32[]{:S(2)}, u32[]{:S(2)}) %collective-permute-start.3) | collective-permute-done | bytes 139296 | tf_op jit(solution)/shard_map/ppermute | solution.py:207
  15.3 3.8 %collective-permute-start.5 = (bf16[4,272,256]{2,1,0:T(8,128)(2,1)S(1)}, bf16[4,272,256]{2,1,0:T(8,128)(2,1)S(1)}, u32[]{:S(2)}, u32[]{:S(2)}) collective-permute-start(bf16[4,272,256]{2,1,0:T(8,128)(2,1)S(1)} %pad_maximum_fusion), channel_id=1, source_target_pairs={{0,24},{8,16},{16,8},{24,0},{32,56},{40,48},{48,40},{56,32},{64,88... | collective-permute-start | bytes 1671176 | tf_op jit(solution)/shard_map/ppermute | solution.py:207
  19.2 12.4 %collective-permute-done.5 = bf16[4,272,256]{2,1,0:T(8,128)(2,1)S(1)} collective-permute-done((bf16[4,272,256]{2,1,0:T(8,128)(2,1)S(1)}, bf16[4,272,256]{2,1,0:T(8,128)(2,1)S(1)}, u32[]{:S(2)}, u32[]{:S(2)}) %collective-permute-start.5) | collective-permute-done | bytes 557088 | tf_op jit(solution)/shard_map/ppermute | solution.py:207
  31.7 0.8 collective-permute-done.4
  32.5 1.7 %collective-permute-start.7 = (bf16[2,272,256]{2,1,0:T(8,128)(2,1)S(1)}, bf16[2,272,256]{2,1,0:T(8,128)(2,1)S(1)}, u32[]{:S(2)}, u32[]{:S(2)}) collective-permute-start(bf16[2,272,256]{2,1,0:T(8,128)(2,1)S(1)} %slice.43), channel_id=1, source_target_pairs={{0,24},{8,16},{16,8},{24,0},{32,56},{40,48},{48,40},{56,32},{64,88... | collective-permute-start | bytes 835592 | tf_op jit(solution)/shard_map/ppermute | solution.py:207
  34.3 4.4 %collective-permute-done.6 = bf16[2,272,256]{2,1,0:T(8,128)(2,1)S(1)} collective-permute-done((bf16[2,272,256]{2,1,0:T(8,128)(2,1)S(1)}, bf16[2,272,256]{2,1,0:T(8,128)(2,1)S(1)}, u32[]{:S(2)}, u32[]{:S(2)}) %collective-permute-start.6) | collective-permute-done | bytes 278560 | tf_op jit(solution)/shard_map/ppermute | solution.py:207
  38.7 1.5 %collective-permute-done.7 = bf16[2,272,256]{2,1,0:T(8,128)(2,1)S(1)} collective-permute-done((bf16[2,272,256]{2,1,0:T(8,128)(2,1)S(1)}, bf16[2,272,256]{2,1,0:T(8,128)(2,1)S(1)}, u32[]{:S(2)}, u32[]{:S(2)}) %collective-permute-start.7) | collective-permute-done | bytes 278560 | tf_op jit(solution)/shard_map/ppermute | solution.py:207
  40.3 2.7 %collective-permute-start.8 = (bf16[16,272,256]{2,1,0:T(8,128)(2,1)S(1)}, bf16[16,272,256]{2,1,0:T(8,128)(2,1)}, u32[]{:S(2)}, u32[]{:S(2)}) collective-permute-start(bf16[16,272,256]{2,1,0:T(8,128)(2,1)S(1)} %constant_dynamic-update-slice_fusion.tab_a_ref), channel_id=1, source_target_pairs={{0,1},{1,0},{2,3},{3,2},{4,5},{5,4},{6,7},{7,6},{8,9},{9,8},{10,11... | collective-permute-start | bytes 6684680 | tf_op jit(solution)/shard_map/ppermute | solution.py:224
  43.0 2.9 %fusion.4 = f32[1280,256]{1,0:T(8,128)} fusion(bf16[512,256]{1,0:T(8,128)(2,1)S(1)} %copy-done, bf16[2,2048,512]{2,1,0:T(8,128)(2,1)} %param.8, s32[]{:T(128)S(6)} %select_n.28), kind=kOutput, calls=%fused_computation.9 | convolution fusion | flops 335544320 | bytes 2883588 | tf_op jit(solution)/shard_map/dot_general | solution.py:230
  45.9 0.6 collective-permute-start.9
  46.4 2.4 %fusion.8 = f32[768,256]{1,0:T(8,128)} fusion(bf16[512,256]{1,0:T(8,128)(2,1)S(1)} %copy-done, bf16[2,2048,512]{2,1,0:T(8,128)(2,1)} %param.8, s32[]{:T(128)S(6)} %select_n.28, s32[]{:T(128)S(6)} %add.41), kind=kOutput, calls=%fused_computation.15 | convolution fusion | flops 201326592 | bytes 1835016 | tf_op jit(solution)/shard_map/dot_general | solution.py:230
  48.8 0.9 collective-permute-start
  49.7 0.6 pad_add_fusion.par_ref
  50.4 1.4 copy.14.tcol_ref
  51.7 0.7 reshape.26.lists_ref
  52.4 2.9 %fusion.5.qa_ref = f32[1280,256]{1,0:T(8,128)} fusion(bf16[512,256]{1,0:T(8,128)(2,1)S(1)} %copy-done, bf16[2,2048,512]{2,1,0:T(8,128)(2,1)} %param.8, s32[]{:T(128)S(6)} %select_n.27), kind=kOutput, calls=%fused_computation.11 | convolution fusion | flops 335544320 | bytes 2883588 | tf_op jit(solution)/shard_map/dot_general | solution.py:230
  55.3 20.5 %collective-permute-done.9.qb_ref = f32[1280,256]{1,0:T(8,128)} collective-permute-done((f32[1280,256]{1,0:T(8,128)}, f32[1280,256]{1,0:T(8,128)}, u32[]{:S(2)}, u32[]{:S(2)}) %collective-permute-start.9) | collective-permute-done | bytes 1310752 | tf_op jit(solution)/shard_map/ppermute | solution.py:242
  75.8 31.6 %shard_map.103 = (bf16[2048,256]{1,0:T(8,128)(2,1)}, f32[8,1,256]{2,1,0:T(1,128)}, bf16[1280,256]{1,0:T(8,128)(2,1)}) custom-call(s32[96]{0:T(128)} %reshape.26.lists_ref, s32[8]{0:T(128)} %lens_ref.3, s32[2048]{0:T(1024)} %tgt_ref.3, s32[2]{0:T(128)} %pad_add_fusion.par_ref, f32[1280,256]{1,0:T(8,128)} %fusion.5.qa_ref, ...), custom_call_target="tpu_custom_call" | custom-call | flops 2684354560 | bytes 5767168 | tf_op jit(solution)/shard_map/pallas_call | solution.py:168
  107.4 4.9 %collective-permute-start.10 = (bf16[1280,256]{1,0:T(8,128)(2,1)}, bf16[1280,256]{1,0:T(8,128)(2,1)S(1)}, u32[]{:S(2)}, u32[]{:S(2)}) collective-permute-start(bf16[1280,256]{1,0:T(8,128)(2,1)} %get-tuple-element.13), channel_id=1, source_target_pairs={{0,64},{64,0},{1,65},{65,1},{2,66},{66,2},{3,67},{67,3},{4,68},{68... | collective-permute-start | bytes 1966088 | tf_op jit(solution)/shard_map/ppermute | solution.py:245
  112.3 2.4 %fusion.9.qa_ref = f32[768,256]{1,0:T(8,128)} fusion(bf16[512,256]{1,0:T(8,128)(2,1)S(1)} %copy-done, bf16[2,2048,512]{2,1,0:T(8,128)(2,1)} %param.8, s32[]{:T(128)S(6)} %select_n.27, s32[]{:T(128)S(6)} %add.41), kind=kOutput, calls=%fused_computation.17 | convolution fusion | flops 201326592 | bytes 1835016 | tf_op jit(solution)/shard_map/dot_general | solution.py:230
  114.7 0.9 copy-done.4
  115.6 23.7 %shard_map.104 = (bf16[2048,256]{1,0:T(8,128)(2,1)}, f32[8,1,256]{2,1,0:T(1,128)}, bf16[768,256]{1,0:T(8,128)(2,1)}) custom-call(s32[96]{0:T(128)} %reshape.26.lists_ref, s32[8]{0:T(128)} %lens_ref.3, s32[2048]{0:T(1024)} %tgt_ref.3, s32[2]{0:T(128)} %pad_add_fusion.par_ref, ...), custom_call_target="tpu_custom_call", output_to_operand_aliasing={{0}: (9, {}), {1}: (10, {})} | custom-call | flops 1610612736 | bytes 5242880 | tf_op jit(solution)/shard_map/pallas_call | solution.py:168
  139.8 0.8 copy-done.1
  140.6 0.7 fusion.1
  141.9 7.0 %collective-permute-done.11 = bf16[768,256]{1,0:T(8,128)(2,1)S(1)} collective-permute-done((bf16[768,256]{1,0:T(8,128)(2,1)}, bf16[768,256]{1,0:T(8,128)(2,1)S(1)}, u32[]{:S(2)}, u32[]{:S(2)}) %collective-permute-start.11) | collective-permute-done | bytes 393248 | tf_op jit(solution)/shard_map/ppermute | solution.py:245
  149.3 2.0 %copy-done.2 = bf16[2,2048,512]{2,1,0:T(8,128)(2,1)} copy-done((bf16[2,2048,512]{2,1,0:T(8,128)(2,1)}, bf16[2,2048,512]{2,1,0:T(8,128)(2,1)S(1)}, u32[]{:S(2)}) %copy-start.2) | copy-done | bytes 4194328
  (40 shorter events, 1.8 us)
Async XLA Ops:
  0.6 42.3 %copy-start = (bf16[512,256]{1,0:T(8,128)(2,1)S(1)}, bf16[512,256]{1,0:T(8,128)(2,1)}, u32[]{:S(2)}) copy-start(bf16[512,256]{1,0:T(8,128)(2,1)} %param.9) | copy-start | bytes 786436
  0.6 4.5 %copy-start.5 = (bf16[512,256]{1,0:T(8,128)(2,1)S(1)}, bf16[512,256]{1,0:T(8,128)(2,1)}, u32[]{:S(2)}) copy-start(bf16[512,256]{1,0:T(8,128)(2,1)} %param.10) | copy-start | bytes 786436
  5.2 6.1 %collective-permute-start.1 = (bf16[1,272,256]{2,1,0:T(8,128)(2,1)S(1)}, bf16[1,272,256]{2,1,0:T(8,128)(2,1)S(1)}, u32[]{:S(2)}, u32[]{:S(2)}) collective-permute-start(bf16[1,272,256]{2,1,0:T(8,128)(2,1)S(1)} %fusion.12), channel_id=1, source_target_pairs={{0,32},{8,40},{16,48},{24,56},{32,0},{40,8},{48,16},{56,24},{64,96... | collective-permute-start | bytes 417800 | tf_op jit(solution)/shard_map/ppermute | solution.py:207
  6.4 5.7 %collective-permute-start.2 = (bf16[1,272,256]{2,1,0:T(8,128)(2,1)S(1)}, bf16[1,272,256]{2,1,0:T(8,128)(2,1)S(1)}, u32[]{:S(2)}, u32[]{:S(2)}) collective-permute-start(bf16[1,272,256]{2,1,0:T(8,128)(2,1)S(1)} %fusion.12), channel_id=1, source_target_pairs={{0,64},{8,72},{16,80},{24,88},{32,96},{40,104},{48,112},{56,120},{... | collective-permute-start | bytes 417800 | tf_op jit(solution)/shard_map/ppermute | solution.py:207
  6.4 8.8 %collective-permute-start.3 = (bf16[1,272,256]{2,1,0:T(8,128)(2,1)S(1)}, bf16[1,272,256]{2,1,0:T(8,128)(2,1)S(1)}, u32[]{:S(2)}, u32[]{:S(2)}) collective-permute-start(bf16[1,272,256]{2,1,0:T(8,128)(2,1)S(1)} %fusion.12), channel_id=1, source_target_pairs={{0,96},{8,104},{16,112},{24,120},{32,64},{40,72},{48,80},{56,88},{... | collective-permute-start | bytes 417800 | tf_op jit(solution)/shard_map/ppermute | solution.py:207
  15.3 16.2 %collective-permute-start.5 = (bf16[4,272,256]{2,1,0:T(8,128)(2,1)S(1)}, bf16[4,272,256]{2,1,0:T(8,128)(2,1)S(1)}, u32[]{:S(2)}, u32[]{:S(2)}) collective-permute-start(bf16[4,272,256]{2,1,0:T(8,128)(2,1)S(1)} %pad_maximum_fusion), channel_id=1, source_target_pairs={{0,24},{8,16},{16,8},{24,0},{32,56},{40,48},{48,40},{56,32},{64,88... | collective-permute-start | bytes 1671176 | tf_op jit(solution)/shard_map/ppermute | solution.py:207
  19.1 13.3 %collective-permute-start.4 = (bf16[4,272,256]{2,1,0:T(8,128)(2,1)S(1)}, bf16[4,272,256]{2,1,0:T(8,128)(2,1)S(1)}, u32[]{:S(2)}, u32[]{:S(2)}) collective-permute-start(bf16[4,272,256]{2,1,0:T(8,128)(2,1)S(1)} %pad_maximum_fusion), channel_id=1, source_target_pairs={{0,8},{8,0},{16,24},{24,16},{32,40},{40,32},{48,56},{56,48},{64,72... | collective-permute-start | bytes 1671176 | tf_op jit(solution)/shard_map/ppermute | solution.py:207
  31.6 7.1 %collective-permute-start.6 = (bf16[2,272,256]{2,1,0:T(8,128)(2,1)S(1)}, bf16[2,272,256]{2,1,0:T(8,128)(2,1)S(1)}, u32[]{:S(2)}, u32[]{:S(2)}) collective-permute-start(bf16[2,272,256]{2,1,0:T(8,128)(2,1)S(1)} %slice.42), channel_id=1, source_target_pairs={{0,8},{8,0},{16,24},{24,16},{32,40},{40,32},{48,56},{56,48},{64,72... | collective-permute-start | bytes 835592 | tf_op jit(solution)/shard_map/ppermute | solution.py:207
  32.5 7.8 %collective-permute-start.7 = (bf16[2,272,256]{2,1,0:T(8,128)(2,1)S(1)}, bf16[2,272,256]{2,1,0:T(8,128)(2,1)S(1)}, u32[]{:S(2)}, u32[]{:S(2)}) collective-permute-start(bf16[2,272,256]{2,1,0:T(8,128)(2,1)S(1)} %slice.43), channel_id=1, source_target_pairs={{0,24},{8,16},{16,8},{24,0},{32,56},{40,48},{48,40},{56,32},{64,88... | collective-permute-start | bytes 835592 | tf_op jit(solution)/shard_map/ppermute | solution.py:207
  40.3 8.6 %copy-start.3 = (bf16[16,272,256]{2,1,0:T(8,128)(2,1)}, bf16[16,272,256]{2,1,0:T(8,128)(2,1)S(1)}, u32[]{:S(2)}) copy-start(bf16[16,272,256]{2,1,0:T(8,128)(2,1)S(1)} %constant_dynamic-update-slice_fusion.tab_a_ref) | copy-start | bytes 6684676
  40.3 35.5 %collective-permute-start.8 = (bf16[16,272,256]{2,1,0:T(8,128)(2,1)S(1)}, bf16[16,272,256]{2,1,0:T(8,128)(2,1)}, u32[]{:S(2)}, u32[]{:S(2)}) collective-permute-start(bf16[16,272,256]{2,1,0:T(8,128)(2,1)S(1)} %constant_dynamic-update-slice_fusion.tab_a_ref), channel_id=1, source_target_pairs={{0,1},{1,0},{2,3},{3,2},{4,5},{5,4},{6,7},{7,6},{8,9},{9,8},{10,11... | collective-permute-start | bytes 6684680 | tf_op jit(solution)/shard_map/ppermute | solution.py:224
  42.9 7.4 %copy-start.6 = (s32[2048]{0:T(1024)S(1)}, s32[2048]{0:T(1024)}, u32[]{:S(2)}) copy-start(s32[2048]{0:T(1024)} %tgt_ref.3) | copy-start | bytes 24580
  43.0 8.8 %copy-start.7 = (s32[8,12]{1,0:T(8,128)S(1)}, s32[8,12]{1,0:T(8,128)}, u32[]{:S(2)}) copy-start(s32[8,12]{1,0:T(8,128)} %param.14) | copy-start | bytes 1156
  45.9 29.9 %collective-permute-start.9 = (f32[1280,256]{1,0:T(8,128)}, f32[1280,256]{1,0:T(8,128)}, u32[]{:S(2)}, u32[]{:S(2)}) collective-permute-start(f32[1280,256]{1,0:T(8,128)} %fusion.4), channel_id=1, source_target_pairs={{0,64},{64,0},{1,65},{65,1},{2,66},{66,2},{3,67},{67,3},{4,68},{68... | collective-permute-start | bytes 3932168 | tf_op jit(solution)/shard_map/ppermute | solution.py:242
  48.8 65.9 %collective-permute-start = (f32[768,256]{1,0:T(8,128)}, f32[768,256]{1,0:T(8,128)S(1)}, u32[]{:S(2)}, u32[]{:S(2)}) collective-permute-start(f32[768,256]{1,0:T(8,128)} %fusion.8), channel_id=1, source_target_pairs={{0,64},{64,0},{1,65},{65,1},{2,66},{66,2},{3,67},{67,3},{4,68},{68... | collective-permute-start | bytes 2359304 | tf_op jit(solution)/shard_map/ppermute | solution.py:242
  107.4 33.9 %collective-permute-start.10 = (bf16[1280,256]{1,0:T(8,128)(2,1)}, bf16[1280,256]{1,0:T(8,128)(2,1)S(1)}, u32[]{:S(2)}, u32[]{:S(2)}) collective-permute-start(bf16[1280,256]{1,0:T(8,128)(2,1)} %get-tuple-element.13), channel_id=1, source_target_pairs={{0,64},{64,0},{1,65},{65,1},{2,66},{66,2},{3,67},{67,3},{4,68},{68... | collective-permute-start | bytes 1966088 | tf_op jit(solution)/shard_map/ppermute | solution.py:245
  114.7 0.9 copy-start.4
  139.4 1.2 copy-start.1
  139.4 9.5 %collective-permute-start.11 = (bf16[768,256]{1,0:T(8,128)(2,1)}, bf16[768,256]{1,0:T(8,128)(2,1)S(1)}, u32[]{:S(2)}, u32[]{:S(2)}) collective-permute-start(bf16[768,256]{1,0:T(8,128)(2,1)} %get-tuple-element.14), channel_id=1, source_target_pairs={{0,64},{64,0},{1,65},{65,1},{2,66},{66,2},{3,67},{67,3},{4,68},{68... | collective-permute-start | bytes 1179656 | tf_op jit(solution)/shard_map/ppermute | solution.py:245
  149.3 2.0 %copy-start.2 = (bf16[2,2048,512]{2,1,0:T(8,128)(2,1)}, bf16[2,2048,512]{2,1,0:T(8,128)(2,1)S(1)}, u32[]{:S(2)}) copy-start(bf16[2,2048,512]{2,1,0:T(8,128)(2,1)S(1)} %fusion.7) | copy-start | bytes 12582916

commit v12 on v11

--- a/solution.py
+++ b/solution.py
@@ -129,7 +129,7 @@
     loss_ref[...] = jnp.transpose(loss_col)[0:1, :].reshape(loss_ref.shape)
 
 
-def score(q_mine, q_sent, target_slot, block_lists, list_lens, tab_a, tab_b, parity, aways,
+def score(q_mine, q_sent, target_slot, target_col, block_lists, list_lens, tab_a, tab_b, parity, aways,
           offset, total_rows, prev=None):
     rows, embed = q_mine.shape
     n_blocks = rows // BLOCK
@@ -182,7 +182,7 @@
             flops=flops, transcendentals=2 * rows * BLOCK * 8,
             bytes_accessed=2 * tab_a.size * 2 + rows * embed * 4),
     )(block_lists.reshape(-1), list_lens, target_slot, parity,
-      q_mine, q_sent, target_slot.reshape(total_rows, 1), tab_a, tab_b, *prev)
+      q_mine, q_sent, target_col, tab_a, tab_b, *prev)
     return (qg, loss), qg_chunk
 
 
@@ -233,6 +233,7 @@
     first_blocks = (n_pblocks * 5 + 7) // 8
     bounds = [0, first_blocks * BLOCK, rows_dev] if 0 < first_blocks < n_pblocks else [0, rows_dev // 2, rows_dev]
     n_chunks = 2
+    target_col = target_slot.reshape(rows_dev, 1)
     outs = None
     others = []
     for c in range(n_chunks):
@@ -240,7 +241,7 @@
         theirs = project(their_rows[rows])
         mine = project(mine_rows[rows])
         sent = lax.ppermute(theirs, "section", partner)
-        outs, grad = score(mine, sent, target_slot, block_lists, list_lens,
+        outs, grad = score(mine, sent, target_slot, target_col, block_lists, list_lens,
                            buf, tab_b, parity, tuple(aways), bounds[c], rows_dev, outs)
         others.append(lax.ppermute(grad, "section", partner))
     query_grad, loss_rows = outs

time: 152 us -> 152 us (level)
  no operation moved by 1% of the time
where the time goes in v12:
time: 152 us; the launch traced here: 151 us
  Pallas kernels  55.4 us (36%)
  waiting for transfers between devices  53.3 us (35%)
  starting transfers between devices  18.1 us (12%)
  matrix products  12.3 us (8%)
  local copies, waits for them, and re-layouts  9.96 us (7%)
    pallas_call x2, Pallas kernels, score(): pl.pallas_call(functools.partial(score_kernel, list_width, n_blocks, away...  55.4 us
    ppermute x7, waiting for transfers between devices, swap(): return lax.ppermute(x, group, [(i, i ^ d) for i in range(n_group)])  25.8 us
    ppermute x2, waiting for transfers between devices, shards(): sent = lax.ppermute(theirs, 'section', partner)  20.5 us
    dot_general x4, matrix products, project(): return jnp.dot(x, w_proj, preferred_element_type=jnp.float32)  10.6 us
    ppermute x7, starting transfers between devices, swap(): return lax.ppermute(x, group, [(i, i ^ d) for i in range(n_group)])  8.98 us
    ppermute x2, waiting for transfers between devices, shards(): others.append(lax.ppermute(grad, 'section', partner))  7.03 us
    ppermute x2, starting transfers between devices, shards(): others.append(lax.ppermute(grad, 'section', partner))  4.99 us
    unnamed x22, local copies, waits for them, and re-layouts  3.92 us
  transfers between devices with their start and end apart: 12, of which 9 were waited for; matrix products, arithmetic and copies ran while one was open for 10% of the time, Pallas kernels for 37%

profile of v12, /device:TPU:7, one launch (start us, length us, event | category | flops | bytes accessed | tf_op | source)
XLA Modules:
  0.0 151.3 jit_solution(12574023241601514912)
XLA Ops:
  0.7 0.8 compare_select_fusion
  1.4 3.6 %gather_fusion = s32[512]{0:T(512)S(1)} fusion(s32[65536]{0:T(1024)} %param.12, s32[1024]{0:T(1024)S(1)} %pad_clamp_fusion), kind=kCustom, calls=%fused_computation | custom fusion | bytes 6144 | tf_op jit(solution)/shard_map/gather | solution.py:198
  5.2 1.2 collective-permute-start.1
  6.4 2.1 %collective-permute-start.3 = (bf16[1,272,256]{2,1,0:T(8,128)(2,1)S(1)}, bf16[1,272,256]{2,1,0:T(8,128)(2,1)S(1)}, u32[]{:S(2)}, u32[]{:S(2)}) collective-permute-start(bf16[1,272,256]{2,1,0:T(8,128)(2,1)S(1)} %fusion.12), channel_id=1, source_target_pairs={{0,96},{8,104},{16,112},{24,120},{32,64},{40,72},{48,80},{56,88},{... | collective-permute-start | bytes 417800 | tf_op jit(solution)/shard_map/ppermute | solution.py:207
  8.5 2.8 %collective-permute-done.1 = bf16[1,272,256]{2,1,0:T(8,128)(2,1)S(1)} collective-permute-done((bf16[1,272,256]{2,1,0:T(8,128)(2,1)S(1)}, bf16[1,272,256]{2,1,0:T(8,128)(2,1)S(1)}, u32[]{:S(2)}, u32[]{:S(2)}) %collective-permute-start.1) | collective-permute-done | bytes 139296 | tf_op jit(solution)/shard_map/ppermute | solution.py:207
  11.3 0.8 collective-permute-done.2
  12.1 3.2 %collective-permute-done.3 = bf16[1,272,256]{2,1,0:T(8,128)(2,1)S(1)} collective-permute-done((bf16[1,272,256]{2,1,0:T(8,128)(2,1)S(1)}, bf16[1,272,256]{2,1,0:T(8,128)(2,1)S(1)}, u32[]{:S(2)}, u32[]{:S(2)}) %collective-permute-start.3) | collective-permute-done | bytes 139296 | tf_op jit(solution)/shard_map/ppermute | solution.py:207
  15.3 3.8 %collective-permute-start.5 = (bf16[4,272,256]{2,1,0:T(8,128)(2,1)S(1)}, bf16[4,272,256]{2,1,0:T(8,128)(2,1)S(1)}, u32[]{:S(2)}, u32[]{:S(2)}) collective-permute-start(bf16[4,272,256]{2,1,0:T(8,128)(2,1)S(1)} %pad_maximum_fusion), channel_id=1, source_target_pairs={{0,24},{8,16},{16,8},{24,0},{32,56},{40,48},{48,40},{56,32},{64,88... | collective-permute-start | bytes 1671176 | tf_op jit(solution)/shard_map/ppermute | solution.py:207
  19.2 12.4 %collective-permute-done.5 = bf16[4,272,256]{2,1,0:T(8,128)(2,1)S(1)} collective-permute-done((bf16[4,272,256]{2,1,0:T(8,128)(2,1)S(1)}, bf16[4,272,256]{2,1,0:T(8,128)(2,1)S(1)}, u32[]{:S(2)}, u32[]{:S(2)}) %collective-permute-start.5) | collective-permute-done | bytes 557088 | tf_op jit(solution)/shard_map/ppermute | solution.py:207
  31.7 0.8 collective-permute-done.4
  32.5 1.7 %collective-permute-start.7 = (bf16[2,272,256]{2,1,0:T(8,128)(2,1)S(1)}, bf16[2,272,256]{2,1,0:T(8,128)(2,1)S(1)}, u32[]{:S(2)}, u32[]{:S(2)}) collective-permute-start(bf16[2,272,256]{2,1,0:T(8,128)(2,1)S(1)} %slice.43), channel_id=1, source_target_pairs={{0,24},{8,16},{16,8},{24,0},{32,56},{40,48},{48,40},{56,32},{64,88... | collective-permute-start | bytes 835592 | tf_op jit(solution)/shard_map/ppermute | solution.py:207
  34.3 4.4 %collective-permute-done.6 = bf16[2,272,256]{2,1,0:T(8,128)(2,1)S(1)} collective-permute-done((bf16[2,272,256]{2,1,0:T(8,128)(2,1)S(1)}, bf16[2,272,256]{2,1,0:T(8,128)(2,1)S(1)}, u32[]{:S(2)}, u32[]{:S(2)}) %collective-permute-start.6) | collective-permute-done | bytes 278560 | tf_op jit(solution)/shard_map/ppermute | solution.py:207
  38.7 1.5 %collective-permute-done.7 = bf16[2,272,256]{2,1,0:T(8,128)(2,1)S(1)} collective-permute-done((bf16[2,272,256]{2,1,0:T(8,128)(2,1)S(1)}, bf16[2,272,256]{2,1,0:T(8,128)(2,1)S(1)}, u32[]{:S(2)}, u32[]{:S(2)}) %collective-permute-start.7) | collective-permute-done | bytes 278560 | tf_op jit(solution)/shard_map/ppermute | solution.py:207
  40.3 2.7 %collective-permute-start.8 = (bf16[16,272,256]{2,1,0:T(8,128)(2,1)S(1)}, bf16[16,272,256]{2,1,0:T(8,128)(2,1)}, u32[]{:S(2)}, u32[]{:S(2)}) collective-permute-start(bf16[16,272,256]{2,1,0:T(8,128)(2,1)S(1)} %constant_dynamic-update-slice_fusion.tab_a_ref), channel_id=1, source_target_pairs={{0,1},{1,0},{2,3},{3,2},{4,5},{5,4},{6,7},{7,6},{8,9},{9,8},{10,11... | collective-permute-start | bytes 6684680 | tf_op jit(solution)/shard_map/ppermute | solution.py:224
  43.0 2.9 %fusion.4 = f32[1280,256]{1,0:T(8,128)} fusion(bf16[512,256]{1,0:T(8,128)(2,1)S(1)} %copy-done, bf16[2,2048,512]{2,1,0:T(8,128)(2,1)} %param.8, s32[]{:T(128)S(6)} %select_n.28), kind=kOutput, calls=%fused_computation.9 | convolution fusion | flops 335544320 | bytes 2883588 | tf_op jit(solution)/shard_map/dot_general | solution.py:230
  45.9 0.6 collective-permute-start.9
  46.4 2.4 %fusion.8 = f32[768,256]{1,0:T(8,128)} fusion(bf16[512,256]{1,0:T(8,128)(2,1)S(1)} %copy-done, bf16[2,2048,512]{2,1,0:T(8,128)(2,1)} %param.8, s32[]{:T(128)S(6)} %select_n.28, s32[]{:T(128)S(6)} %add.41), kind=kOutput, calls=%fused_computation.15 | convolution fusion | flops 201326592 | bytes 1835016 | tf_op jit(solution)/shard_map/dot_general | solution.py:230
  48.8 0.9 collective-permute-start
  49.7 0.6 pad_add_fusion.par_ref
  50.4 1.4 copy.14.tcol_ref
  51.7 0.7 reshape.25.lists_ref
  52.4 2.9 %fusion.5.qa_ref = f32[1280,256]{1,0:T(8,128)} fusion(bf16[512,256]{1,0:T(8,128)(2,1)S(1)} %copy-done, bf16[2,2048,512]{2,1,0:T(8,128)(2,1)} %param.8, s32[]{:T(128)S(6)} %select_n.27), kind=kOutput, calls=%fused_computation.11 | convolution fusion | flops 335544320 | bytes 2883588 | tf_op jit(solution)/shard_map/dot_general | solution.py:230
  55.3 20.5 %collective-permute-done.9.qb_ref = f32[1280,256]{1,0:T(8,128)} collective-permute-done((f32[1280,256]{1,0:T(8,128)}, f32[1280,256]{1,0:T(8,128)}, u32[]{:S(2)}, u32[]{:S(2)}) %collective-permute-start.9) | collective-permute-done | bytes 1310752 | tf_op jit(solution)/shard_map/ppermute | solution.py:243
  75.8 31.6 %shard_map.103 = (bf16[2048,256]{1,0:T(8,128)(2,1)}, f32[8,1,256]{2,1,0:T(1,128)}, bf16[1280,256]{1,0:T(8,128)(2,1)}) custom-call(s32[96]{0:T(128)} %reshape.25.lists_ref, s32[8]{0:T(128)} %lens_ref.3, s32[2048]{0:T(1024)} %tgt_ref.3, s32[2]{0:T(128)} %pad_add_fusion.par_ref, f32[1280,256]{1,0:T(8,128)} %fusion.5.qa_ref, ...), custom_call_target="tpu_custom_call" | custom-call | flops 2684354560 | bytes 5767168 | tf_op jit(solution)/shard_map/pallas_call | solution.py:168
  107.4 4.9 %collective-permute-start.10 = (bf16[1280,256]{1,0:T(8,128)(2,1)}, bf16[1280,256]{1,0:T(8,128)(2,1)S(1)}, u32[]{:S(2)}, u32[]{:S(2)}) collective-permute-start(bf16[1280,256]{1,0:T(8,128)(2,1)} %get-tuple-element.13), channel_id=1, source_target_pairs={{0,64},{64,0},{1,65},{65,1},{2,66},{66,2},{3,67},{67,3},{4,68},{68... | collective-permute-start | bytes 1966088 | tf_op jit(solution)/shard_map/ppermute | solution.py:246
  112.3 2.4 %fusion.9.qa_ref = f32[768,256]{1,0:T(8,128)} fusion(bf16[512,256]{1,0:T(8,128)(2,1)S(1)} %copy-done, bf16[2,2048,512]{2,1,0:T(8,128)(2,1)} %param.8, s32[]{:T(128)S(6)} %select_n.27, s32[]{:T(128)S(6)} %add.41), kind=kOutput, calls=%fused_computation.17 | convolution fusion | flops 201326592 | bytes 1835016 | tf_op jit(solution)/shard_map/dot_general | solution.py:230
  114.7 0.9 copy-done.4
  115.6 23.7 %shard_map.104 = (bf16[2048,256]{1,0:T(8,128)(2,1)}, f32[8,1,256]{2,1,0:T(1,128)}, bf16[768,256]{1,0:T(8,128)(2,1)}) custom-call(s32[96]{0:T(128)} %reshape.25.lists_ref, s32[8]{0:T(128)} %lens_ref.3, s32[2048]{0:T(1024)} %tgt_ref.3, s32[2]{0:T(128)} %pad_add_fusion.par_ref, ...), custom_call_target="tpu_custom_call", output_to_operand_aliasing={{0}: (9, {}), {1}: (10, {})} | custom-call | flops 1610612736 | bytes 5242880 | tf_op jit(solution)/shard_map/pallas_call | solution.py:168
  139.8 0.8 copy-done.1
  140.6 0.7 fusion.1
  141.9 7.0 %collective-permute-done.11 = bf16[768,256]{1,0:T(8,128)(2,1)S(1)} collective-permute-done((bf16[768,256]{1,0:T(8,128)(2,1)}, bf16[768,256]{1,0:T(8,128)(2,1)S(1)}, u32[]{:S(2)}, u32[]{:S(2)}) %collective-permute-start.11) | collective-permute-done | bytes 393248 | tf_op jit(solution)/shard_map/ppermute | solution.py:246
  149.3 2.0 %copy-done.2 = bf16[2,2048,512]{2,1,0:T(8,128)(2,1)} copy-done((bf16[2,2048,512]{2,1,0:T(8,128)(2,1)}, bf16[2,2048,512]{2,1,0:T(8,128)(2,1)S(1)}, u32[]{:S(2)}) %copy-start.2) | copy-done | bytes 4194328
  (40 shorter events, 1.8 us)
Async XLA Ops:
  0.6 42.3 %copy-start = (bf16[512,256]{1,0:T(8,128)(2,1)S(1)}, bf16[512,256]{1,0:T(8,128)(2,1)}, u32[]{:S(2)}) copy-start(bf16[512,256]{1,0:T(8,128)(2,1)} %param.9) | copy-start | bytes 786436
  0.6 4.5 %copy-start.5 = (bf16[512,256]{1,0:T(8,128)(2,1)S(1)}, bf16[512,256]{1,0:T(8,128)(2,1)}, u32[]{:S(2)}) copy-start(bf16[512,256]{1,0:T(8,128)(2,1)} %param.10) | copy-start | bytes 786436
  5.2 6.1 %collective-permute-start.1 = (bf16[1,272,256]{2,1,0:T(8,128)(2,1)S(1)}, bf16[1,272,256]{2,1,0:T(8,128)(2,1)S(1)}, u32[]{:S(2)}, u32[]{:S(2)}) collective-permute-start(bf16[1,272,256]{2,1,0:T(8,128)(2,1)S(1)} %fusion.12), channel_id=1, source_target_pairs={{0,32},{8,40},{16,48},{24,56},{32,0},{40,8},{48,16},{56,24},{64,96... | collective-permute-start | bytes 417800 | tf_op jit(solution)/shard_map/ppermute | solution.py:207
  6.4 5.7 %collective-permute-start.2 = (bf16[1,272,256]{2,1,0:T(8,128)(2,1)S(1)}, bf16[1,272,256]{2,1,0:T(8,128)(2,1)S(1)}, u32[]{:S(2)}, u32[]{:S(2)}) collective-permute-start(bf16[1,272,256]{2,1,0:T(8,128)(2,1)S(1)} %fusion.12), channel_id=1, source_target_pairs={{0,64},{8,72},{16,80},{24,88},{32,96},{40,104},{48,112},{56,120},{... | collective-permute-start | bytes 417800 | tf_op jit(solution)/shard_map/ppermute | solution.py:207
  6.4 8.8 %collective-permute-start.3 = (bf16[1,272,256]{2,1,0:T(8,128)(2,1)S(1)}, bf16[1,272,256]{2,1,0:T(8,128)(2,1)S(1)}, u32[]{:S(2)}, u32[]{:S(2)}) collective-permute-start(bf16[1,272,256]{2,1,0:T(8,128)(2,1)S(1)} %fusion.12), channel_id=1, source_target_pairs={{0,96},{8,104},{16,112},{24,120},{32,64},{40,72},{48,80},{56,88},{... | collective-permute-start | bytes 417800 | tf_op jit(solution)/shard_map/ppermute | solution.py:207
  15.3 16.2 %collective-permute-start.5 = (bf16[4,272,256]{2,1,0:T(8,128)(2,1)S(1)}, bf16[4,272,256]{2,1,0:T(8,128)(2,1)S(1)}, u32[]{:S(2)}, u32[]{:S(2)}) collective-permute-start(bf16[4,272,256]{2,1,0:T(8,128)(2,1)S(1)} %pad_maximum_fusion), channel_id=1, source_target_pairs={{0,24},{8,16},{16,8},{24,0},{32,56},{40,48},{48,40},{56,32},{64,88... | collective-permute-start | bytes 1671176 | tf_op jit(solution)/shard_map/ppermute | solution.py:207
  19.1 13.3 %collective-permute-start.4 = (bf16[4,272,256]{2,1,0:T(8,128)(2,1)S(1)}, bf16[4,272,256]{2,1,0:T(8,128)(2,1)S(1)}, u32[]{:S(2)}, u32[]{:S(2)}) collective-permute-start(bf16[4,272,256]{2,1,0:T(8,128)(2,1)S(1)} %pad_maximum_fusion), channel_id=1, source_target_pairs={{0,8},{8,0},{16,24},{24,16},{32,40},{40,32},{48,56},{56,48},{64,72... | collective-permute-start | bytes 1671176 | tf_op jit(solution)/shard_map/ppermute | solution.py:207
  31.6 7.1 %collective-permute-start.6 = (bf16[2,272,256]{2,1,0:T(8,128)(2,1)S(1)}, bf16[2,272,256]{2,1,0:T(8,128)(2,1)S(1)}, u32[]{:S(2)}, u32[]{:S(2)}) collective-permute-start(bf16[2,272,256]{2,1,0:T(8,128)(2,1)S(1)} %slice.42), channel_id=1, source_target_pairs={{0,8},{8,0},{16,24},{24,16},{32,40},{40,32},{48,56},{56,48},{64,72... | collective-permute-start | bytes 835592 | tf_op jit(solution)/shard_map/ppermute | solution.py:207
  32.5 7.8 %collective-permute-start.7 = (bf16[2,272,256]{2,1,0:T(8,128)(2,1)S(1)}, bf16[2,272,256]{2,1,0:T(8,128)(2,1)S(1)}, u32[]{:S(2)}, u32[]{:S(2)}) collective-permute-start(bf16[2,272,256]{2,1,0:T(8,128)(2,1)S(1)} %slice.43), channel_id=1, source_target_pairs={{0,24},{8,16},{16,8},{24,0},{32,56},{40,48},{48,40},{56,32},{64,88... | collective-permute-start | bytes 835592 | tf_op jit(solution)/shard_map/ppermute | solution.py:207
  40.3 8.6 %copy-start.3 = (bf16[16,272,256]{2,1,0:T(8,128)(2,1)}, bf16[16,272,256]{2,1,0:T(8,128)(2,1)S(1)}, u32[]{:S(2)}) copy-start(bf16[16,272,256]{2,1,0:T(8,128)(2,1)S(1)} %constant_dynamic-update-slice_fusion.tab_a_ref) | copy-start | bytes 6684676
  40.3 35.5 %collective-permute-start.8 = (bf16[16,272,256]{2,1,0:T(8,128)(2,1)S(1)}, bf16[16,272,256]{2,1,0:T(8,128)(2,1)}, u32[]{:S(2)}, u32[]{:S(2)}) collective-permute-start(bf16[16,272,256]{2,1,0:T(8,128)(2,1)S(1)} %constant_dynamic-update-slice_fusion.tab_a_ref), channel_id=1, source_target_pairs={{0,1},{1,0},{2,3},{3,2},{4,5},{5,4},{6,7},{7,6},{8,9},{9,8},{10,11... | collective-permute-start | bytes 6684680 | tf_op jit(solution)/shard_map/ppermute | solution.py:224
  42.9 7.4 %copy-start.6 = (s32[2048]{0:T(1024)S(1)}, s32[2048]{0:T(1024)}, u32[]{:S(2)}) copy-start(s32[2048]{0:T(1024)} %tgt_ref.3) | copy-start | bytes 24580
  43.0 8.8 %copy-start.7 = (s32[8,12]{1,0:T(8,128)S(1)}, s32[8,12]{1,0:T(8,128)}, u32[]{:S(2)}) copy-start(s32[8,12]{1,0:T(8,128)} %param.14) | copy-start | bytes 1156
  45.9 29.9 %collective-permute-start.9 = (f32[1280,256]{1,0:T(8,128)}, f32[1280,256]{1,0:T(8,128)}, u32[]{:S(2)}, u32[]{:S(2)}) collective-permute-start(f32[1280,256]{1,0:T(8,128)} %fusion.4), channel_id=1, source_target_pairs={{0,64},{64,0},{1,65},{65,1},{2,66},{66,2},{3,67},{67,3},{4,68},{68... | collective-permute-start | bytes 3932168 | tf_op jit(solution)/shard_map/ppermute | solution.py:243
  48.8 65.9 %collective-permute-start = (f32[768,256]{1,0:T(8,128)}, f32[768,256]{1,0:T(8,128)S(1)}, u32[]{:S(2)}, u32[]{:S(2)}) collective-permute-start(f32[768,256]{1,0:T(8,128)} %fusion.8), channel_id=1, source_target_pairs={{0,64},{64,0},{1,65},{65,1},{2,66},{66,2},{3,67},{67,3},{4,68},{68... | collective-permute-start | bytes 2359304 | tf_op jit(solution)/shard_map/ppermute | solution.py:243
  107.4 33.9 %collective-permute-start.10 = (bf16[1280,256]{1,0:T(8,128)(2,1)}, bf16[1280,256]{1,0:T(8,128)(2,1)S(1)}, u32[]{:S(2)}, u32[]{:S(2)}) collective-permute-start(bf16[1280,256]{1,0:T(8,128)(2,1)} %get-tuple-element.13), channel_id=1, source_target_pairs={{0,64},{64,0},{1,65},{65,1},{2,66},{66,2},{3,67},{67,3},{4,68},{68... | collective-permute-start | bytes 1966088 | tf_op jit(solution)/shard_map/ppermute | solution.py:246
  114.7 0.9 copy-start.4
  139.4 1.2 copy-start.1
  139.4 9.5 %collective-permute-start.11 = (bf16[768,256]{1,0:T(8,128)(2,1)}, bf16[768,256]{1,0:T(8,128)(2,1)S(1)}, u32[]{:S(2)}, u32[]{:S(2)}) collective-permute-start(bf16[768,256]{1,0:T(8,128)(2,1)} %get-tuple-element.14), channel_id=1, source_target_pairs={{0,64},{64,0},{1,65},{65,1},{2,66},{66,2},{3,67},{67,3},{4,68},{68... | collective-permute-start | bytes 1179656 | tf_op jit(solution)/shard_map/ppermute | solution.py:246
  149.3 2.0 %copy-start.2 = (bf16[2,2048,512]{2,1,0:T(8,128)(2,1)}, bf16[2,2048,512]{2,1,0:T(8,128)(2,1)S(1)}, u32[]{:S(2)}) copy-start(bf16[2,2048,512]{2,1,0:T(8,128)(2,1)S(1)} %fusion.7) | copy-start | bytes 12582916
